TPU v7x, 256 devices: a whole 4x4x8 slice. The times are simulated.
256 devices in a mesh: gx: 16 (over x, z_hi, core), gy: 4 (over z_lo), gz: 4 (over y).
Axes of the slice: x: 4, y: 4, z: 8 (z_hi: 2, z_lo: 4; z = z_hi * 4 + z_lo), core: 2. Of those that a mesh axis runs over, the one named last changes fastest.
Arguments:
- image_slab: float32 [64, 1024, 1024], P(('gz', 'gx'), None, 'gy'), may hold values from -6 to 6
- deformed_slab: float32 [64, 1024, 1024], P(('gz', 'gx'), None, 'gy'), may hold values from -6 to 6
- shifts: int32 [2, 3, 4, 16, 4], P(None, None, 'gz', 'gx', 'gy'), may hold values from -8 to 8, as said below
Outputs:
- displacement: float32 [3, 12, 144, 132], P(None, 'gz', 'gx', 'gy')
- residual_map: float32 [64, 1024, 1024], P('gz', 'gx', 'gy')
Inputs may be any that keep to these rules, and one draw needn't show every extreme that they name: `shifts`: every component lies within -8 to 8, and both ends are taken by some entry.
All inputs are finite; a program needn't handle non-finite values.
Results may differ from a plain program's by a relative error of at most 0.0003.
Values sent between devices are 32-bit elements; how exact they have to be, the bound alone decides.
No kernel may reach another device: no remote copies, remote signals or barrier semaphores. Data moves between devices by JAX's collectives and lax.ppermute only.
A program may use at most 128 MiB of HBM per device.

v0:
```python
import jax
import jax.numpy as jnp
from jax import lax
from jax.sharding import PartitionSpec as P

ELEMENT = 8
DMAX = 8
ITERS = 2
SWEEPS = 3


DAMPING = 0.7
REGULARIZE = 4.0


def padded(block, sides, width):
    for axis, dim in sides:
        count = lax.axis_size(axis)
        forward = [(i, i + 1) for i in range(count - 1)]
        backward = [(target, source) for source, target in forward]
        low = lax.ppermute(
            lax.slice_in_dim(block, block.shape[dim] - width, None, axis=dim), axis, forward
        )
        high = lax.ppermute(lax.slice_in_dim(block, 0, width, axis=dim), axis, backward)
        block = jnp.concatenate([low, block, high], axis=dim)
    return block


def node_weights(squared):
    fraction = (jnp.arange(ELEMENT, dtype=jnp.float32) + 0.5) / ELEMENT
    lower_weight = 1.0 - fraction
    if squared:
        return (lower_weight * lower_weight, fraction * fraction)
    return (lower_weight, fraction)


def weight_shape(weight, ndim, axis):
    shape = [1] * (ndim + 1)
    shape[axis + 1] = ELEMENT
    return weight.reshape(shape)


def spread_axis(nodal, axis, weights):
    count = nodal.shape[axis] - 1
    lower = jnp.expand_dims(lax.slice_in_dim(nodal, 0, count, axis=axis), axis + 1)
    upper = jnp.expand_dims(lax.slice_in_dim(nodal, 1, count + 1, axis=axis), axis + 1)
    ndim = nodal.ndim
    joined = lower * weight_shape(weights[0], ndim, axis) + upper * weight_shape(
        weights[1], ndim, axis
    )
    shape = list(nodal.shape)
    shape[axis] = count * ELEMENT
    return joined.reshape(shape)


def collect_axis(field, axis, weights):
    count = field.shape[axis] // ELEMENT
    shape = list(field.shape)
    split_shape = shape[:axis] + [count, ELEMENT] + shape[axis + 1 :]
    blocks = field.reshape(split_shape)
    ndim = field.ndim
    lower = jnp.sum(blocks * weight_shape(weights[0], ndim, axis), axis=axis + 1)
    upper = jnp.sum(blocks * weight_shape(weights[1], ndim, axis), axis=axis + 1)
    pad_low = [(0, 0)] * ndim
    pad_high = [(0, 0)] * ndim
    pad_low[axis] = (0, 1)
    pad_high[axis] = (1, 0)
    return jnp.pad(lower, pad_low) + jnp.pad(upper, pad_high)


def cut_range(array, axis, start, length):
    return lax.slice_in_dim(array, start, start + length, axis=axis)


def smooth(array, axis):
    length = array.shape[axis] - 2
    return (
        cut_range(array, axis, 0, length)
        + 2.0 * cut_range(array, axis, 1, length)
        + cut_range(array, axis, 2, length)
    ) * 0.25


def differ(array, axis):
    length = array.shape[axis] - 2
    return (cut_range(array, axis, 2, length) - cut_range(array, axis, 0, length)) * 0.5


def gradients(extended):
    along_z = smooth(smooth(differ(extended, 0), 1), 2)
    along_x = smooth(smooth(differ(extended, 1), 0), 2)
    along_y = smooth(smooth(differ(extended, 2), 0), 1)
    return jnp.stack([along_z, along_x, along_y])


def interpolate(nodal, weights):
    step = spread_axis(nodal, 3, weights)
    step = spread_axis(step, 2, weights)
    return spread_axis(step, 1, weights)


def restrict(field, weights):
    step = collect_axis(field, 1, weights)
    step = collect_axis(step, 2, weights)
    return collect_axis(step, 3, weights)


def fold_rims(extended, axis):
    moved = jnp.moveaxis(extended, axis, 0)
    inner = moved[1:-1]
    inner = inner.at[0].add(moved[0])
    inner = inner.at[-1].add(moved[-1])
    return jnp.moveaxis(inner, 0, axis)


def share(partial_value):
    extended = padded(partial_value, (("gx", 2), ("gy", 3), ("gz", 1)), 1)
    for axis in (1, 2, 3):
        extended = fold_rims(extended, axis)
    return extended


def invert(diag):
    a, b, c, d, e, f = (diag[0], diag[1], diag[2], diag[3], diag[4], diag[5])
    i00 = b * c - f * f
    i11 = a * c - e * e
    i22 = a * b - d * d
    i01 = e * f - d * c
    i02 = d * f - b * e
    i12 = d * e - a * f
    det = a * i00 + d * i01 + e * i02
    return jnp.stack([i00, i11, i22, i01, i02, i12]) / det


def apply_inverse(inverse, vector):
    out_z = inverse[0] * vector[0] + inverse[3] * vector[1] + inverse[4] * vector[2]
    out_x = inverse[3] * vector[0] + inverse[1] * vector[1] + inverse[5] * vector[2]
    out_y = inverse[4] * vector[0] + inverse[5] * vector[1] + inverse[2] * vector[2]
    return jnp.stack([out_z, out_x, out_y])


def shards(image_slab, deformed_slab, shifts):
    image, deformed_block = (
        lax.all_to_all(image_slab, "gx", split_axis=1, concat_axis=0, tiled=True),
        lax.all_to_all(deformed_slab, "gx", split_axis=1, concat_axis=0, tiled=True),
    )
    z_count, x_count, y_count = image.shape
    image_ext = padded(image, (("gx", 1), ("gy", 2), ("gz", 0)), 1)
    deformed_ext = padded(deformed_block, (("gx", 1), ("gy", 2), ("gz", 0)), DMAX)
    grads = gradients(image_ext)
    weights = node_weights(False)
    squared = node_weights(True)
    pairs = ((0, 0), (1, 1), (2, 2), (0, 1), (0, 2), (1, 2))
    products = jnp.stack([grads[i] * grads[j] for i, j in pairs])
    diag = share(restrict(products, squared))
    diag = (
        diag
        + REGULARIZE * jnp.array([1.0, 1.0, 1.0, 0.0, 0.0, 0.0], jnp.float32)[:, None, None, None]
    )
    inverse = invert(diag)
    nodal = jnp.zeros(
        (3, z_count // ELEMENT + 1, x_count // ELEMENT + 1, y_count // ELEMENT + 1), jnp.float32
    )

    def residual(nodal_now, warped_now, offset):
        moved = interpolate(nodal_now, weights)
        offset_float = offset.astype(jnp.float32)[:, None, None, None]
        return image - warped_now - jnp.sum(grads * (moved - offset_float), axis=0)

    warped = image
    offset = shifts[0, :, 0, 0, 0]
    for iteration in range(ITERS):
        offset = shifts[iteration, :, 0, 0, 0]
        starts = [DMAX + offset[0], DMAX + offset[1], DMAX + offset[2]]
        warped = lax.dynamic_slice(deformed_ext, starts, (z_count, x_count, y_count))
        resid = residual(nodal, warped, offset)
        rhs = share(restrict(grads * resid[None], weights))
        delta = DAMPING * apply_inverse(inverse, rhs)
        for sweep in range(SWEEPS - 1):
            inner = jnp.sum(grads * interpolate(delta, weights), axis=0)
            applied = share(restrict(grads * inner[None], weights)) + REGULARIZE * delta
            delta = delta + DAMPING * apply_inverse(inverse, rhs - applied)
        nodal = nodal + delta
    final = residual(nodal, warped, offset)
    return (nodal, final)


def solution(mesh):
    return jax.shard_map(
        shards,
        mesh=mesh,
        in_specs=(
            P(("gz", "gx"), None, "gy"),
            P(("gz", "gx"), None, "gy"),
            P(None, None, "gz", "gx", "gy"),
        ),
        out_specs=(P(None, "gz", "gx", "gy"), P("gz", "gx", "gy")),
        check_vma=False,
    )
```

profile of v0, /device:TPU:4, one launch (start us, length us, event | category | flops | bytes accessed | tf_op | source)
XLA Modules:
  0.0 510.8 jit_solution(6681661447291161037)
XLA Ops:
  4.0 11.4 %all-to-all-start = ((f32[1,1024,256]{2,0,1:T(1,128)}), f32[1,1024,256]{2,0,1:T(1,128)S(1)}, u32[]{:S(2)}, u32[]{:S(2)}) async-start(f32[1,1024,256]{2,0,1:T(1,128)} %copy.154), calls=%async_computation | async-start | bytes 2097152 | tf_op jit(solution)/shard_map/all_to_all | solution.py:144
  17.5 18.1 %all-to-all-done = f32[1,1024,256]{2,0,1:T(1,128)S(1)} async-done(((f32[1,1024,256]{2,0,1:T(1,128)}), f32[1,1024,256]{2,0,1:T(1,128)S(1)}, u32[]{:S(2)}, u32[]{:S(2)}) %all-to-all-start) | async-done | bytes 1048608 | tf_op jit(solution)/shard_map/all_to_all | solution.py:144
  35.6 6.8 %all-to-all-start.1 = ((f32[1,1024,256]{2,0,1:T(1,128)}), f32[1,1024,256]{2,0,1:T(1,128)}, u32[]{:S(2)}, u32[]{:S(2)}) async-start(f32[1,1024,256]{2,0,1:T(1,128)} %copy.162), calls=%async_computation.1 | async-start | bytes 2097152 | tf_op jit(solution)/shard_map/all_to_all | solution.py:145
  46.3 8.3 %collective-permute-start.1 = (f32[16,1,256]{2,1,0:T(1,128)S(1)}, f32[16,1,256]{2,1,0:T(1,128)S(1)}, u32[]{:S(2)}, u32[]{:S(2)}) collective-permute-start(f32[16,1,256]{2,1,0:T(1,128)S(1)} %get-tuple-element.580), channel_id=1, source_target_pairs={{16,0},{32,16},{48,32},{64,48},{80,64},{96,80},{112,96},{128,112},... | collective-permute-start | bytes 49160 | tf_op jit(solution)/shard_map/ppermute | solution.py:24
  55.2 4.9 collective-permute-done
  62.5 15.9 %collective-permute-start.2 = (f32[16,66,1]{1,0,2:T(8,128)S(1)}, f32[16,66,1]{1,0,2:T(8,128)S(1)}, u32[]{:S(2)}, u32[]{:S(2)}) collective-permute-start(f32[16,66,1]{1,0,2:T(8,128)S(1)} %copy.155), channel_id=1, source_target_pairs={{0,4},{4,8},{8,12},{1,5},{5,9},{9,13},{2,6},{6,10},{10,14},{3,7},{... | collective-permute-start | bytes 12680 | tf_op jit(solution)/shard_map/ppermute | solution.py:21
  87.7 5.4 %collective-permute-start.5 = (f32[1,66,258]{2,1,0:T(8,128)S(1)}, f32[1,66,258]{2,1,0:T(8,128)}, u32[]{:S(2)}, u32[]{:S(2)}) collective-permute-start(f32[1,66,258]{2,1,0:T(8,128)S(1)} %get-tuple-element.565), channel_id=1, source_target_pairs={{0,1},{1,2},{2,3},{4,5},{5,6},{6,7},{8,9},{9,10},{10,11},{12,13},{... | collective-permute-start | bytes 204344 | tf_op jit(solution)/shard_map/ppermute | solution.py:21
  116.7 8.4 %collective-permute-start.7 = (f32[6,3,1,33]{3,0,2,1:T(8,128)S(1)}, f32[6,3,1,33]{3,0,2,1:T(8,128)S(1)}, u32[]{:S(2)}, u32[]{:S(2)}) collective-permute-start(f32[6,3,1,33]{3,0,2,1:T(8,128)S(1)} %get-tuple-element.598), channel_id=1, source_target_pairs={{16,0},{32,16},{48,32},{64,48},{80,64},{96,80},{112,96},{128,112},... | collective-permute-start | bytes 7136 | tf_op jit(solution)/shard_map/ppermute | solution.py:24
  126.6 4.6 collective-permute-start.8
  134.5 8.4 %collective-permute-start.13 = (f32[16,8,256]{2,1,0:T(8,128)S(1)}, f32[16,8,256]{2,1,0:T(8,128)S(1)}, u32[]{:S(2)}, u32[]{:S(2)}) collective-permute-start(f32[16,8,256]{2,1,0:T(8,128)S(1)} %get-tuple-element.578), channel_id=1, source_target_pairs={{16,0},{32,16},{48,32},{64,48},{80,64},{96,80},{112,96},{128,112},... | collective-permute-start | bytes 393224 | tf_op jit(solution)/shard_map/ppermute | solution.py:24
  154.9 4.9 collective-permute-start.14
  164.1 4.1 collective-permute-done.15
  174.0 4.4 collective-permute-start.16
  192.7 5.1 collective-permute-done.17
  209.8 8.4 %collective-permute-start.19 = (f32[3,3,1,33]{3,0,2,1:T(4,128)S(1)}, f32[3,3,1,33]{3,0,2,1:T(4,128)S(1)}, u32[]{:S(2)}, u32[]{:S(2)}) collective-permute-start(f32[3,3,1,33]{3,0,2,1:T(4,128)S(1)} %get-tuple-element.657), channel_id=1, source_target_pairs={{16,0},{32,16},{48,32},{64,48},{80,64},{96,80},{112,96},{128,112},... | collective-permute-start | bytes 3572 | tf_op jit(solution)/shard_map/ppermute | solution.py:24
  225.5 4.2 collective-permute-done.21
  233.8 4.2 collective-permute-done.23
  258.9 5.1 collective-permute-start.24
  264.0 5.3 %collective-permute-start.25 = (f32[3,3,1,33]{3,0,2,1:T(4,128)S(1)}, f32[3,3,1,33]{3,0,2,1:T(4,128)S(1)}, u32[]{:S(2)}, u32[]{:S(2)}) collective-permute-start(f32[3,3,1,33]{3,0,2,1:T(4,128)S(1)} %get-tuple-element.650), channel_id=1, source_target_pairs={{16,0},{32,16},{48,32},{64,48},{80,64},{96,80},{112,96},{128,112},... | collective-permute-start | bytes 3572 | tf_op jit(solution)/shard_map/ppermute | solution.py:24
  274.9 4.3 collective-permute-done.27
  284.2 4.2 collective-permute-done.29
  311.7 6.9 %collective-permute-start.31 = (f32[3,3,1,33]{3,0,2,1:T(4,128)S(1)}, f32[3,3,1,33]{3,0,2,1:T(4,128)S(1)}, u32[]{:S(2)}, u32[]{:S(2)}) collective-permute-start(f32[3,3,1,33]{3,0,2,1:T(4,128)S(1)} %get-tuple-element.646), channel_id=1, source_target_pairs={{16,0},{32,16},{48,32},{64,48},{80,64},{96,80},{112,96},{128,112},... | collective-permute-start | bytes 3572 | tf_op jit(solution)/shard_map/ppermute | solution.py:24
  323.9 4.3 collective-permute-done.33
  363.9 6.8 %collective-permute-start.37 = (f32[3,3,1,33]{3,0,2,1:T(4,128)S(1)}, f32[3,3,1,33]{3,0,2,1:T(4,128)S(1)}, u32[]{:S(2)}, u32[]{:S(2)}) collective-permute-start(f32[3,3,1,33]{3,0,2,1:T(4,128)S(1)} %get-tuple-element.642), channel_id=1, source_target_pairs={{16,0},{32,16},{48,32},{64,48},{80,64},{96,80},{112,96},{128,112},... | collective-permute-start | bytes 3572 | tf_op jit(solution)/shard_map/ppermute | solution.py:24
  376.0 4.3 collective-permute-done.39
  385.3 4.2 collective-permute-done.41
  412.6 7.8 %collective-permute-start.43 = (f32[3,3,1,33]{3,0,2,1:T(4,128)S(1)}, f32[3,3,1,33]{3,0,2,1:T(4,128)S(1)}, u32[]{:S(2)}, u32[]{:S(2)}) collective-permute-start(f32[3,3,1,33]{3,0,2,1:T(4,128)S(1)} %get-tuple-element.638), channel_id=1, source_target_pairs={{16,0},{32,16},{48,32},{64,48},{80,64},{96,80},{112,96},{128,112},... | collective-permute-start | bytes 3572 | tf_op jit(solution)/shard_map/ppermute | solution.py:24
  425.7 4.3 collective-permute-done.45
  433.5 4.4 collective-permute-done.47
  464.2 8.4 %collective-permute-start.49 = (f32[3,3,1,33]{3,0,2,1:T(4,128)S(1)}, f32[3,3,1,33]{3,0,2,1:T(4,128)S(1)}, u32[]{:S(2)}, u32[]{:S(2)}) collective-permute-start(f32[3,3,1,33]{3,0,2,1:T(4,128)S(1)} %get-tuple-element.634), channel_id=1, source_target_pairs={{16,0},{32,16},{48,32},{64,48},{80,64},{96,80},{112,96},{128,112},... | collective-permute-start | bytes 3572 | tf_op jit(solution)/shard_map/ppermute | solution.py:24
  477.7 4.5 collective-permute-done.51
  486.4 4.2 collective-permute-done.53
  (516 shorter events, 293.6 us)
Async XLA Ops:
  4.0 31.6 %all-to-all-start = ((f32[1,1024,256]{2,0,1:T(1,128)}), f32[1,1024,256]{2,0,1:T(1,128)S(1)}, u32[]{:S(2)}, u32[]{:S(2)}) async-start(f32[1,1024,256]{2,0,1:T(1,128)} %copy.154), calls=%async_computation | async-start | bytes 2097152 | tf_op jit(solution)/shard_map/all_to_all | solution.py:144
  35.6 57.6 %all-to-all-start.1 = ((f32[1,1024,256]{2,0,1:T(1,128)}), f32[1,1024,256]{2,0,1:T(1,128)}, u32[]{:S(2)}, u32[]{:S(2)}) async-start(f32[1,1024,256]{2,0,1:T(1,128)} %copy.162), calls=%async_computation.1 | async-start | bytes 2097152 | tf_op jit(solution)/shard_map/all_to_all | solution.py:145
  44.2 15.8 %collective-permute-start = (f32[16,1,256]{2,1,0:T(1,128)S(1)}, f32[16,1,256]{2,1,0:T(1,128)S(1)}, u32[]{:S(2)}, u32[]{:S(2)}) collective-permute-start(f32[16,1,256]{2,1,0:T(1,128)S(1)} %get-tuple-element.579), channel_id=1, source_target_pairs={{0,16},{16,32},{32,48},{48,64},{64,80},{80,96},{96,112},{112,128},... | collective-permute-start | bytes 49160 | tf_op jit(solution)/shard_map/ppermute | solution.py:21
  46.3 13.8 %collective-permute-start.1 = (f32[16,1,256]{2,1,0:T(1,128)S(1)}, f32[16,1,256]{2,1,0:T(1,128)S(1)}, u32[]{:S(2)}, u32[]{:S(2)}) collective-permute-start(f32[16,1,256]{2,1,0:T(1,128)S(1)} %get-tuple-element.580), channel_id=1, source_target_pairs={{16,0},{32,16},{48,32},{64,48},{80,64},{96,80},{112,96},{128,112},... | collective-permute-start | bytes 49160 | tf_op jit(solution)/shard_map/ppermute | solution.py:24
  62.5 23.1 %collective-permute-start.2 = (f32[16,66,1]{1,0,2:T(8,128)S(1)}, f32[16,66,1]{1,0,2:T(8,128)S(1)}, u32[]{:S(2)}, u32[]{:S(2)}) collective-permute-start(f32[16,66,1]{1,0,2:T(8,128)S(1)} %copy.155), channel_id=1, source_target_pairs={{0,4},{4,8},{8,12},{1,5},{5,9},{9,13},{2,6},{6,10},{10,14},{3,7},{... | collective-permute-start | bytes 12680 | tf_op jit(solution)/shard_map/ppermute | solution.py:21
  78.7 7.3 %collective-permute-start.3 = (f32[16,66,1]{1,0,2:T(8,128)S(1)}, f32[16,66,1]{1,0,2:T(8,128)S(1)}, u32[]{:S(2)}, u32[]{:S(2)}) collective-permute-start(f32[16,66,1]{1,0,2:T(8,128)S(1)} %copy.156), channel_id=1, source_target_pairs={{4,0},{8,4},{12,8},{5,1},{9,5},{13,9},{6,2},{10,6},{14,10},{7,3},{... | collective-permute-start | bytes 12680 | tf_op jit(solution)/shard_map/ppermute | solution.py:24
  86.4 9.0 %collective-permute-start.4 = (f32[1,66,258]{2,1,0:T(8,128)S(1)}, f32[1,66,258]{2,1,0:T(8,128)S(1)}, u32[]{:S(2)}, u32[]{:S(2)}) collective-permute-start(f32[1,66,258]{2,1,0:T(8,128)S(1)} %get-tuple-element.566), channel_id=1, source_target_pairs={{1,0},{2,1},{3,2},{5,4},{6,5},{7,6},{9,8},{10,9},{11,10},{13,12},{... | collective-permute-start | bytes 204344 | tf_op jit(solution)/shard_map/ppermute | solution.py:24
  87.7 8.4 %collective-permute-start.5 = (f32[1,66,258]{2,1,0:T(8,128)S(1)}, f32[1,66,258]{2,1,0:T(8,128)}, u32[]{:S(2)}, u32[]{:S(2)}) collective-permute-start(f32[1,66,258]{2,1,0:T(8,128)S(1)} %get-tuple-element.565), channel_id=1, source_target_pairs={{0,1},{1,2},{2,3},{4,5},{5,6},{6,7},{8,9},{9,10},{10,11},{12,13},{... | collective-permute-start | bytes 204344 | tf_op jit(solution)/shard_map/ppermute | solution.py:21
  114.8 10.5 %collective-permute-start.6 = (f32[6,3,1,33]{3,0,2,1:T(8,128)S(1)}, f32[6,3,1,33]{3,0,2,1:T(8,128)S(1)}, u32[]{:S(2)}, u32[]{:S(2)}) collective-permute-start(f32[6,3,1,33]{3,0,2,1:T(8,128)S(1)} %get-tuple-element.597), channel_id=1, source_target_pairs={{0,16},{16,32},{32,48},{48,64},{64,80},{80,96},{96,112},{112,128},... | collective-permute-start | bytes 7136 | tf_op jit(solution)/shard_map/ppermute | solution.py:21
  116.7 9.8 %collective-permute-start.7 = (f32[6,3,1,33]{3,0,2,1:T(8,128)S(1)}, f32[6,3,1,33]{3,0,2,1:T(8,128)S(1)}, u32[]{:S(2)}, u32[]{:S(2)}) collective-permute-start(f32[6,3,1,33]{3,0,2,1:T(8,128)S(1)} %get-tuple-element.598), channel_id=1, source_target_pairs={{16,0},{32,16},{48,32},{64,48},{80,64},{96,80},{112,96},{128,112},... | collective-permute-start | bytes 7136 | tf_op jit(solution)/shard_map/ppermute | solution.py:24
  126.6 16.3 %collective-permute-start.8 = (f32[6,3,11,1]{3,0,2,1:T(8,128)S(1)}, f32[6,3,11,1]{3,0,2,1:T(8,128)S(1)}, u32[]{:S(2)}, u32[]{:S(2)}) collective-permute-start(f32[6,3,11,1]{3,0,2,1:T(8,128)S(1)} %get-tuple-element.629), channel_id=1, source_target_pairs={{0,4},{4,8},{8,12},{1,5},{5,9},{9,13},{2,6},{6,10},{10,14},{3,7},{... | collective-permute-start | bytes 2384 | tf_op jit(solution)/shard_map/ppermute | solution.py:21
  131.2 11.7 %collective-permute-start.9 = (f32[6,3,11,1]{3,0,2,1:T(8,128)S(1)}, f32[6,3,11,1]{3,0,2,1:T(8,128)S(1)}, u32[]{:S(2)}, u32[]{:S(2)}) collective-permute-start(f32[6,3,11,1]{3,0,2,1:T(8,128)S(1)} %get-tuple-element.630), channel_id=1, source_target_pairs={{4,0},{8,4},{12,8},{5,1},{9,5},{13,9},{6,2},{10,6},{14,10},{7,3},{... | collective-permute-start | bytes 2384 | tf_op jit(solution)/shard_map/ppermute | solution.py:24
  132.5 19.6 %collective-permute-start.12 = (f32[16,8,256]{2,1,0:T(8,128)S(1)}, f32[16,8,256]{2,1,0:T(8,128)S(1)}, u32[]{:S(2)}, u32[]{:S(2)}) collective-permute-start(f32[16,8,256]{2,1,0:T(8,128)S(1)} %get-tuple-element.577), channel_id=1, source_target_pairs={{0,16},{16,32},{32,48},{48,64},{64,80},{80,96},{96,112},{112,128},... | collective-permute-start | bytes 393224 | tf_op jit(solution)/shard_map/ppermute | solution.py:21
  134.5 17.7 %collective-permute-start.13 = (f32[16,8,256]{2,1,0:T(8,128)S(1)}, f32[16,8,256]{2,1,0:T(8,128)S(1)}, u32[]{:S(2)}, u32[]{:S(2)}) collective-permute-start(f32[16,8,256]{2,1,0:T(8,128)S(1)} %get-tuple-element.578), channel_id=1, source_target_pairs={{16,0},{32,16},{48,32},{64,48},{80,64},{96,80},{112,96},{128,112},... | collective-permute-start | bytes 393224 | tf_op jit(solution)/shard_map/ppermute | solution.py:24
  154.9 8.1 %collective-permute-start.14 = (f32[16,80,8]{1,2,0:T(8,128)S(1)}, f32[16,80,8]{1,2,0:T(8,128)S(1)}, u32[]{:S(2)}, u32[]{:S(2)}) collective-permute-start(f32[16,80,8]{1,2,0:T(8,128)S(1)} %copy.163), channel_id=1, source_target_pairs={{0,4},{4,8},{8,12},{1,5},{5,9},{9,13},{2,6},{6,10},{10,14},{3,7},{... | collective-permute-start | bytes 122888 | tf_op jit(solution)/shard_map/ppermute | solution.py:21
  161.7 6.5 %collective-permute-start.15 = (f32[16,80,8]{1,2,0:T(8,128)}, f32[16,80,8]{1,2,0:T(8,128)}, u32[]{:S(2)}, u32[]{:S(2)}) collective-permute-start(f32[16,80,8]{1,2,0:T(8,128)} %copy.164), channel_id=1, source_target_pairs={{4,0},{8,4},{12,8},{5,1},{9,5},{13,9},{6,2},{10,6},{14,10},{7,3},{... | collective-permute-start | bytes 122888 | tf_op jit(solution)/shard_map/ppermute | solution.py:24
  174.0 18.7 %collective-permute-start.16 = (f32[8,80,272]{2,1,0:T(8,128)}, f32[8,80,272]{2,1,0:T(8,128)}, u32[]{:S(2)}, u32[]{:S(2)}) collective-permute-start(f32[8,80,272]{2,1,0:T(8,128)} %get-tuple-element.570), channel_id=1, source_target_pairs={{0,1},{1,2},{2,3},{4,5},{5,6},{6,7},{8,9},{9,10},{10,11},{12,13},{... | collective-permute-start | bytes 2088968 | tf_op jit(solution)/shard_map/ppermute | solution.py:21
  178.4 19.3 %collective-permute-start.17 = (f32[8,80,272]{2,1,0:T(8,128)}, f32[8,80,272]{2,1,0:T(8,128)}, u32[]{:S(2)}, u32[]{:S(2)}) collective-permute-start(f32[8,80,272]{2,1,0:T(8,128)} %get-tuple-element.571), channel_id=1, source_target_pairs={{1,0},{2,1},{3,2},{5,4},{6,5},{7,6},{9,8},{10,9},{11,10},{13,12},{... | collective-permute-start | bytes 2088968 | tf_op jit(solution)/shard_map/ppermute | solution.py:24
  207.9 10.5 %collective-permute-start.18 = (f32[3,3,1,33]{3,0,2,1:T(4,128)S(1)}, f32[3,3,1,33]{3,0,2,1:T(4,128)S(1)}, u32[]{:S(2)}, u32[]{:S(2)}) collective-permute-start(f32[3,3,1,33]{3,0,2,1:T(4,128)S(1)} %get-tuple-element.656), channel_id=1, source_target_pairs={{0,16},{16,32},{32,48},{48,64},{64,80},{80,96},{96,112},{112,128},... | collective-permute-start | bytes 3572 | tf_op jit(solution)/shard_map/ppermute | solution.py:21
  209.8 9.9 %collective-permute-start.19 = (f32[3,3,1,33]{3,0,2,1:T(4,128)S(1)}, f32[3,3,1,33]{3,0,2,1:T(4,128)S(1)}, u32[]{:S(2)}, u32[]{:S(2)}) collective-permute-start(f32[3,3,1,33]{3,0,2,1:T(4,128)S(1)} %get-tuple-element.657), channel_id=1, source_target_pairs={{16,0},{32,16},{48,32},{64,48},{80,64},{96,80},{112,96},{128,112},... | collective-permute-start | bytes 3572 | tf_op jit(solution)/shard_map/ppermute | solution.py:24
  258.9 10.5 %collective-permute-start.24 = (f32[3,3,1,33]{3,0,2,1:T(4,128)S(1)}, f32[3,3,1,33]{3,0,2,1:T(4,128)S(1)}, u32[]{:S(2)}, u32[]{:S(2)}) collective-permute-start(f32[3,3,1,33]{3,0,2,1:T(4,128)S(1)} %get-tuple-element.649), channel_id=1, source_target_pairs={{0,16},{16,32},{32,48},{48,64},{64,80},{80,96},{96,112},{112,128},... | collective-permute-start | bytes 3572 | tf_op jit(solution)/shard_map/ppermute | solution.py:21
  264.0 6.6 %collective-permute-start.25 = (f32[3,3,1,33]{3,0,2,1:T(4,128)S(1)}, f32[3,3,1,33]{3,0,2,1:T(4,128)S(1)}, u32[]{:S(2)}, u32[]{:S(2)}) collective-permute-start(f32[3,3,1,33]{3,0,2,1:T(4,128)S(1)} %get-tuple-element.650), channel_id=1, source_target_pairs={{16,0},{32,16},{48,32},{64,48},{80,64},{96,80},{112,96},{128,112},... | collective-permute-start | bytes 3572 | tf_op jit(solution)/shard_map/ppermute | solution.py:24
  308.2 10.5 %collective-permute-start.30 = (f32[3,3,1,33]{3,0,2,1:T(4,128)S(1)}, f32[3,3,1,33]{3,0,2,1:T(4,128)S(1)}, u32[]{:S(2)}, u32[]{:S(2)}) collective-permute-start(f32[3,3,1,33]{3,0,2,1:T(4,128)S(1)} %get-tuple-element.645), channel_id=1, source_target_pairs={{0,16},{16,32},{32,48},{48,64},{64,80},{80,96},{96,112},{112,128},... | collective-permute-start | bytes 3572 | tf_op jit(solution)/shard_map/ppermute | solution.py:21
  311.7 8.3 %collective-permute-start.31 = (f32[3,3,1,33]{3,0,2,1:T(4,128)S(1)}, f32[3,3,1,33]{3,0,2,1:T(4,128)S(1)}, u32[]{:S(2)}, u32[]{:S(2)}) collective-permute-start(f32[3,3,1,33]{3,0,2,1:T(4,128)S(1)} %get-tuple-element.646), channel_id=1, source_target_pairs={{16,0},{32,16},{48,32},{64,48},{80,64},{96,80},{112,96},{128,112},... | collective-permute-start | bytes 3572 | tf_op jit(solution)/shard_map/ppermute | solution.py:24
  329.6 6.8 %collective-permute-start.34 = (f32[3,1,11,35]{3,0,2,1:T(4,128)}, f32[3,1,11,35]{3,0,2,1:T(4,128)S(1)}, u32[]{:S(2)}, u32[]{:S(2)}) collective-permute-start(f32[3,1,11,35]{3,0,2,1:T(4,128)} %get-tuple-element.605), channel_id=1, source_target_pairs={{0,1},{1,2},{2,3},{4,5},{5,6},{6,7},{8,9},{9,10},{10,11},{12,13},{... | collective-permute-start | bytes 13868 | tf_op jit(solution)/shard_map/ppermute | solution.py:21
  360.3 10.5 %collective-permute-start.36 = (f32[3,3,1,33]{3,0,2,1:T(4,128)S(1)}, f32[3,3,1,33]{3,0,2,1:T(4,128)S(1)}, u32[]{:S(2)}, u32[]{:S(2)}) collective-permute-start(f32[3,3,1,33]{3,0,2,1:T(4,128)S(1)} %get-tuple-element.641), channel_id=1, source_target_pairs={{0,16},{16,32},{32,48},{48,64},{64,80},{80,96},{96,112},{112,128},... | collective-permute-start | bytes 3572 | tf_op jit(solution)/shard_map/ppermute | solution.py:21
  363.9 8.2 %collective-permute-start.37 = (f32[3,3,1,33]{3,0,2,1:T(4,128)S(1)}, f32[3,3,1,33]{3,0,2,1:T(4,128)S(1)}, u32[]{:S(2)}, u32[]{:S(2)}) collective-permute-start(f32[3,3,1,33]{3,0,2,1:T(4,128)S(1)} %get-tuple-element.642), channel_id=1, source_target_pairs={{16,0},{32,16},{48,32},{64,48},{80,64},{96,80},{112,96},{128,112},... | collective-permute-start | bytes 3572 | tf_op jit(solution)/shard_map/ppermute | solution.py:24
  410.0 10.5 %collective-permute-start.42 = (f32[3,3,1,33]{3,0,2,1:T(4,128)S(1)}, f32[3,3,1,33]{3,0,2,1:T(4,128)S(1)}, u32[]{:S(2)}, u32[]{:S(2)}) collective-permute-start(f32[3,3,1,33]{3,0,2,1:T(4,128)S(1)} %get-tuple-element.637), channel_id=1, source_target_pairs={{0,16},{16,32},{32,48},{48,64},{64,80},{80,96},{96,112},{112,128},... | collective-permute-start | bytes 3572 | tf_op jit(solution)/shard_map/ppermute | solution.py:21
  412.6 9.1 %collective-permute-start.43 = (f32[3,3,1,33]{3,0,2,1:T(4,128)S(1)}, f32[3,3,1,33]{3,0,2,1:T(4,128)S(1)}, u32[]{:S(2)}, u32[]{:S(2)}) collective-permute-start(f32[3,3,1,33]{3,0,2,1:T(4,128)S(1)} %get-tuple-element.638), channel_id=1, source_target_pairs={{16,0},{32,16},{48,32},{64,48},{80,64},{96,80},{112,96},{128,112},... | collective-permute-start | bytes 3572 | tf_op jit(solution)/shard_map/ppermute | solution.py:24
  462.2 10.5 %collective-permute-start.48 = (f32[3,3,1,33]{3,0,2,1:T(4,128)S(1)}, f32[3,3,1,33]{3,0,2,1:T(4,128)S(1)}, u32[]{:S(2)}, u32[]{:S(2)}) collective-permute-start(f32[3,3,1,33]{3,0,2,1:T(4,128)S(1)} %get-tuple-element.633), channel_id=1, source_target_pairs={{0,16},{16,32},{32,48},{48,64},{64,80},{80,96},{96,112},{112,128},... | collective-permute-start | bytes 3572 | tf_op jit(solution)/shard_map/ppermute | solution.py:21
  464.2 9.7 %collective-permute-start.49 = (f32[3,3,1,33]{3,0,2,1:T(4,128)S(1)}, f32[3,3,1,33]{3,0,2,1:T(4,128)S(1)}, u32[]{:S(2)}, u32[]{:S(2)}) collective-permute-start(f32[3,3,1,33]{3,0,2,1:T(4,128)S(1)} %get-tuple-element.634), channel_id=1, source_target_pairs={{16,0},{32,16},{48,32},{64,48},{80,64},{96,80},{112,96},{128,112},... | collective-permute-start | bytes 3572 | tf_op jit(solution)/shard_map/ppermute | solution.py:24
  475.8 6.4 %collective-permute-start.51 = (f32[3,3,11,1]{3,0,2,1:T(4,128)S(1)}, f32[3,3,11,1]{3,0,2,1:T(4,128)S(1)}, u32[]{:S(2)}, u32[]{:S(2)}) collective-permute-start(f32[3,3,11,1]{3,0,2,1:T(4,128)S(1)} %get-tuple-element.659), channel_id=1, source_target_pairs={{4,0},{8,4},{12,8},{5,1},{9,5},{13,9},{6,2},{10,6},{14,10},{7,3},{... | collective-permute-start | bytes 1196 | tf_op jit(solution)/shard_map/ppermute | solution.py:24
  (72 other events, 601.8 us)
where the time goes:
time: 519 us; the launch traced here: 511 us
  starting transfers between devices  201 us (39%)
  local copies, waits for them, and re-layouts  127 us (24%)
  waiting for transfers between devices  98 us (19%)
  other arithmetic  74.3 us (14%)
  between operations  10.8 us (2%)
    ppermute x27, starting transfers between devices, padded(): lax.ppermute(lax.slice_in_dim(block, 0, width, axis=dim), axis, backward)  92.1 us
    ppermute x27, starting transfers between devices, padded(): lax.ppermute(lax.slice_in_dim(block, block.shape[dim] - width, None, axis...  90.8 us
    ppermute x27, waiting for transfers between devices, padded(): lax.ppermute(lax.slice_in_dim(block, 0, width, axis=dim), axis, backward)  68.9 us
    mul x16, local copies, waits for them, and re-layouts, spread_axis(): upper * weight_shape(weights[1], ndim, axis)  24.5 us
    mul x17, local copies, waits for them, and re-layouts, spread_axis(): lower * weight_shape(weights[0], ndim, axis)  23.2 us
    scatter-add x7, local copies, waits for them, and re-layouts, fold_rims(): inner = inner.at[-1].add(moved[-1])  18.9 us
    all_to_all x1, waiting for transfers between devices, shards(): lax.all_to_all(image_slab, 'gx', split_axis=1, concat_axis=0, tiled=True)  18.1 us
    reshape x7, local copies, waits for them, and re-layouts, collect_axis(): blocks = field.reshape(split_shape)  16.3 us
  transfers between devices with their start and end apart: 56, of which 35 were waited for; matrix products, arithmetic and copies ran while one was open for 6% of the time, Pallas kernels for 0%

commit v1 on v0

v1 whole, which is shorter than its diff:
```python
import numpy as np

import jax
import jax.numpy as jnp
from jax import lax
from jax.sharding import PartitionSpec as P

ELEMENT = 8
DMAX = 8
ITERS = 2
SWEEPS = 3


DAMPING = 0.7
REGULARIZE = 4.0
HI = lax.Precision.HIGHEST


def shape_table(voxel_count, squared=False):
    voxel = np.arange(voxel_count)
    fraction = ((voxel % ELEMENT).astype(np.float32) + 0.5) / ELEMENT
    owning = voxel // ELEMENT
    nodes = np.arange(voxel_count // ELEMENT + 1)
    lower = (nodes[None, :] == owning[:, None]) * (1.0 - fraction)[:, None]
    upper = (nodes[None, :] == owning[:, None] + 1) * fraction[:, None]
    table = (lower + upper).astype(np.float32)
    if squared:
        table = table * table
    return jnp.asarray(table)


def z_weights(squared=False):
    fraction = (np.arange(ELEMENT, dtype=np.float32) + 0.5) / ELEMENT
    lower = 1.0 - fraction
    if squared:
        return lower * lower, fraction * fraction
    return lower, fraction


def neighbours(axis):
    count = lax.axis_size(axis)
    forward = [(i, i + 1) for i in range(count - 1)]
    backward = [(i + 1, i) for i in range(count - 1)]
    return forward, backward


def halo(block, axis, dim, width):
    forward, backward = neighbours(axis)
    size = block.shape[dim]
    low = lax.ppermute(lax.slice_in_dim(block, size - width, size, axis=dim), axis, forward)
    high = lax.ppermute(lax.slice_in_dim(block, 0, width, axis=dim), axis, backward)
    return jnp.concatenate([low, block, high], axis=dim)


def share(partial_value):
    value = partial_value
    for axis, dim in (("gz", 1), ("gx", 2), ("gy", 3)):
        forward, backward = neighbours(axis)
        size = value.shape[dim]
        first = lax.slice_in_dim(value, 0, 1, axis=dim)
        last = lax.slice_in_dim(value, size - 1, size, axis=dim)
        from_low = lax.ppermute(last, axis, forward)
        from_high = lax.ppermute(first, axis, backward)
        middle = lax.slice_in_dim(value, 1, size - 1, axis=dim)
        value = jnp.concatenate([first + from_low, middle, last + from_high], axis=dim)
    return value


def cut_range(array, axis, start, length):
    return lax.slice_in_dim(array, start, start + length, axis=axis)


def smooth(array, axis):
    length = array.shape[axis] - 2
    return (
        cut_range(array, axis, 0, length)
        + 2.0 * cut_range(array, axis, 1, length)
        + cut_range(array, axis, 2, length)
    ) * 0.25


def differ(array, axis):
    length = array.shape[axis] - 2
    return (cut_range(array, axis, 2, length) - cut_range(array, axis, 0, length)) * 0.5


def gradients(extended):
    along_z = smooth(smooth(differ(extended, 0), 1), 2)
    along_x = smooth(smooth(differ(extended, 1), 0), 2)
    along_y = smooth(smooth(differ(extended, 2), 0), 1)
    return jnp.stack([along_z, along_x, along_y])


def interp_xy(nodal, table_x, table_y):
    step = jnp.einsum("cabd,yd->caby", nodal, table_y, precision=HI)
    return jnp.einsum("caby,xb->caxy", step, table_x, precision=HI)


def expand_z(values, weights):
    lower, upper = weights
    count = values.shape[1] - 1
    low = values[:, :count, None]
    high = values[:, 1:, None]
    shape = (1, 1, ELEMENT, 1, 1)
    joined = low * lower.reshape(shape) + high * upper.reshape(shape)
    return joined.reshape((values.shape[0], count * ELEMENT) + values.shape[2:])


def interpolate(nodal, tables, weights):
    return expand_z(interp_xy(nodal, *tables), weights)


def reduce_z(field, weights):
    lower, upper = weights
    count = field.shape[1] // ELEMENT
    blocks = field.reshape((field.shape[0], count, ELEMENT) + field.shape[2:])
    shape = (1, 1, ELEMENT, 1, 1)
    low = jnp.sum(blocks * lower.reshape(shape), axis=2)
    high = jnp.sum(blocks * upper.reshape(shape), axis=2)
    parts = [low[:, :1]]
    for e in range(1, count):
        parts.append(high[:, e - 1 : e] + low[:, e : e + 1])
    parts.append(high[:, count - 1 :])
    return jnp.concatenate(parts, axis=1)


def restrict(field, tables, weights):
    table_x, table_y = tables
    step = reduce_z(field, weights)
    step = jnp.einsum("caxy,xb->caby", step, table_x, precision=HI)
    return jnp.einsum("caby,yd->cabd", step, table_y, precision=HI)


def invert(diag):
    a, b, c, d, e, f = (diag[0], diag[1], diag[2], diag[3], diag[4], diag[5])
    i00 = b * c - f * f
    i11 = a * c - e * e
    i22 = a * b - d * d
    i01 = e * f - d * c
    i02 = d * f - b * e
    i12 = d * e - a * f
    det = a * i00 + d * i01 + e * i02
    return jnp.stack([i00, i11, i22, i01, i02, i12]) / det


def apply_inverse(inverse, vector):
    out_z = inverse[0] * vector[0] + inverse[3] * vector[1] + inverse[4] * vector[2]
    out_x = inverse[3] * vector[0] + inverse[1] * vector[1] + inverse[5] * vector[2]
    out_y = inverse[4] * vector[0] + inverse[5] * vector[1] + inverse[2] * vector[2]
    return jnp.stack([out_z, out_x, out_y])


def bricks_of(image_slab, deformed_slab):
    both = jnp.concatenate([image_slab, deformed_slab], axis=0)
    both = halo(both, "gy", 2, DMAX)
    n_gx = lax.axis_size("gx")
    fields, nx, ny = both.shape
    bx = nx // n_gx
    main = both.reshape(fields, n_gx, bx, ny)
    zero = jnp.zeros((fields, 1, DMAX, ny), both.dtype)
    low = jnp.concatenate([zero, main[:, :-1, bx - DMAX :]], axis=1)
    high = jnp.concatenate([main[:, 1:, :DMAX], zero], axis=1)
    windows = jnp.concatenate([low, main, high], axis=2)
    windows = jnp.moveaxis(windows, 1, 0)
    brick = lax.all_to_all(windows, "gx", split_axis=0, concat_axis=0, tiled=True)
    image = brick[:, 0]
    deformed = brick[:, 1]
    image_ext = halo(image[:, DMAX - 1 : DMAX + bx + 1, DMAX - 1 : ny - DMAX + 1], "gz", 0, 1)
    deformed_ext = halo(deformed, "gz", 0, DMAX)
    return image_ext, deformed_ext


def shards(image_slab, deformed_slab, shifts):
    image_ext, deformed_ext = bricks_of(image_slab, deformed_slab)
    image = image_ext[1:-1, 1:-1, 1:-1]
    z_count, x_count, y_count = image.shape
    grads = gradients(image_ext)
    tables = (shape_table(x_count), shape_table(y_count))
    tables_sq = (shape_table(x_count, True), shape_table(y_count, True))
    weights = z_weights(False)
    weights_sq = z_weights(True)
    pairs = ((0, 0), (1, 1), (2, 2), (0, 1), (0, 2), (1, 2))

    def residual(moved, warped_now, offset):
        offset_float = offset.astype(jnp.float32)[:, None, None, None]
        return image - warped_now - jnp.sum(grads * (moved - offset_float), axis=0)

    def warp(iteration):
        offset = shifts[iteration, :, 0, 0, 0]
        starts = [DMAX + offset[0], DMAX + offset[1], DMAX + offset[2]]
        return lax.dynamic_slice(deformed_ext, starts, (z_count, x_count, y_count)), offset

    def operator(delta):
        inner = jnp.sum(grads * interpolate(delta, tables, weights), axis=0)
        return share(restrict(grads * inner[None], tables, weights))

    warped, offset = warp(0)
    resid = image - warped + jnp.sum(grads * offset.astype(jnp.float32)[:, None, None, None], axis=0)
    products = jnp.stack([grads[i] * grads[j] for i, j in pairs])
    first = jnp.concatenate(
        [restrict(products, tables_sq, weights_sq), restrict(grads * resid[None], tables, weights)],
        axis=0,
    )
    first = share(first)
    diag = first[:6] + REGULARIZE * jnp.array([1.0, 1.0, 1.0, 0.0, 0.0, 0.0], jnp.float32)[
        :, None, None, None
    ]
    inverse = invert(diag)
    rhs = first[6:]
    nodal = jnp.zeros((3, z_count // ELEMENT + 1, x_count // ELEMENT + 1, y_count // ELEMENT + 1), jnp.float32)
    for iteration in range(ITERS):
        if iteration > 0:
            warped, offset = warp(iteration)
            resid = residual(interpolate(nodal, tables, weights), warped, offset)
            rhs = share(restrict(grads * resid[None], tables, weights))
        delta = DAMPING * apply_inverse(inverse, rhs)
        for sweep in range(SWEEPS - 1):
            applied = operator(delta) + REGULARIZE * delta
            delta = delta + DAMPING * apply_inverse(inverse, rhs - applied)
        nodal = nodal + delta
    final = residual(interpolate(nodal, tables, weights), warped, offset)
    return (nodal, final)


def solution(mesh):
    return jax.shard_map(
        shards,
        mesh=mesh,
        in_specs=(
            P(("gz", "gx"), None, "gy"),
            P(("gz", "gx"), None, "gy"),
            P(None, None, "gz", "gx", "gy"),
        ),
        out_specs=(P(None, "gz", "gx", "gy"), P("gz", "gx", "gy")),
        check_vma=False,
    )
```

time: 519 us -> 387 us (0.75); the launches traced: 511 us -> 385 us
  waiting for transfers between devices: 98 us -> 204 us
  local copies, waits for them, and re-layouts: 127 us -> 21.7 us
  starting transfers between devices: 201 us -> 111 us
  other arithmetic: 74.3 us -> 26.7 us
  matrix products: 0 us -> 11.5 us
    ppermute x54 -> x42, starting transfers between devices: 183 us -> 99.9 us  [the longest x18 49.9 us: share(): from_low = lax.ppermute(last, axis, forward)]
    all_to_all x2 -> x1, waiting for transfers between devices: 18.1 us -> 85.3 us  [bricks_of(): lax.all_to_all(windows, 'gx', split_axis=0, concat_axis=0, tiled=True)]
    mul x33 -> x0, local copies, waits for them, and re-layouts: 47.7 us -> none  [the longest x16 24.5 us: spread_axis(): upper * weight_shape(weights[1], ndim, axis)]
    ppermute x54 -> x42, waiting for transfers between devices: 80 us -> 119 us  [the longest x18 59.6 us: share(): from_high = lax.ppermute(first, axis, backward)]
    scatter-add x14 -> x0, local copies, waits for them, and re-layouts: 23.4 us -> none  [the longest x7 18.9 us: fold_rims(): inner = inner.at[-1].add(moved[-1])]
    reduce_sum x25 -> x12, other arithmetic: 26.7 us -> 7.7 us  [the longest x7 4.75 us: reduce_z(): low = jnp.sum(blocks * lower.reshape(shape), axis=2)]
    reshape x7 -> x0, local copies, waits for them, and re-layouts: 16.3 us -> none  [collect_axis(): blocks = field.reshape(split_shape)]
    add x54 -> x27, other arithmetic: 15.4 us -> 2.39 us  [the longest x18 1.61 us: share(): first + from_low]
  transfers between devices with their start and end apart: 56 -> 43, of which waited for: 35 -> 39; matrix products, arithmetic and copies ran while one was open for 6% -> 3% of each run, Pallas kernels for 0% -> 0%
where the time goes in v1:
time: 387 us; the launch traced here: 385 us
  waiting for transfers between devices  204 us (53%)
  starting transfers between devices  111 us (29%)
  other arithmetic  26.7 us (7%)
  local copies, waits for them, and re-layouts  21.7 us (6%)
  matrix products  11.5 us (3%)
  between operations  9.63 us (2%)
    all_to_all x1, waiting for transfers between devices, bricks_of(): lax.all_to_all(windows, 'gx', split_axis=0, concat_axis=0, tiled=True)  85.3 us
    ppermute x18, waiting for transfers between devices, share(): from_high = lax.ppermute(first, axis, backward)  59.6 us
    ppermute x18, starting transfers between devices, share(): from_low = lax.ppermute(last, axis, forward)  49.9 us
    ppermute x18, waiting for transfers between devices, share(): from_low = lax.ppermute(last, axis, forward)  48.5 us
    ppermute x18, starting transfers between devices, share(): from_high = lax.ppermute(first, axis, backward)  34 us
    ppermute x3, starting transfers between devices, halo(): lax.ppermute(lax.slice_in_dim(block, size - width, size, axis=dim), axis,...  11.9 us
    all_to_all x1, starting transfers between devices, bricks_of(): lax.all_to_all(windows, 'gx', split_axis=0, concat_axis=0, tiled=True)  10.7 us
  transfers between devices with their start and end apart: 43, of which 39 were waited for; matrix products, arithmetic and copies ran while one was open for 3% of the time, Pallas kernels for 0%

profile of v1, /device:TPU:4, one launch (start us, length us, event | category | flops | bytes accessed | tf_op | source)
XLA Modules:
  0.0 384.5 jit_solution(1935956864529419492)
XLA Ops:
  6.3 3.8 collective-permute-start
  13.4 3.2 collective-permute-done.1
  17.9 3.3 pad_maximum_fusion.1
  24.0 10.7 %all-to-all-start = ((f32[16,2,80,272]{3,2,1,0:T(8,128)}), f32[16,2,80,272]{3,2,1,0:T(8,128)}, u32[]{:S(2)}, u32[]{:S(2)}) async-start(f32[16,2,80,272]{3,2,1,0:T(8,128)} %copy.49), calls=%async_computation | async-start | bytes 7864320 | tf_op jit(solution)/shard_map/all_to_all | solution.py:165
  39.9 85.3 %all-to-all-done = f32[16,2,80,272]{3,2,1,0:T(8,128)} async-done(((f32[16,2,80,272]{3,2,1,0:T(8,128)}), f32[16,2,80,272]{3,2,1,0:T(8,128)}, u32[]{:S(2)}, u32[]{:S(2)}) %all-to-all-start) | async-done | bytes 2785312 | tf_op jit(solution)/shard_map/all_to_all | solution.py:165
  127.7 3.5 collective-permute-start.3
  134.7 4.6 %collective-permute-start.4 = (f32[8,80,272]{2,1,0:T(8,128)S(1)}, f32[8,80,272]{2,1,0:T(8,128)S(1)}, u32[]{:S(2)}, u32[]{:S(2)}) collective-permute-start(f32[8,80,272]{2,1,0:T(8,128)S(1)} %get-tuple-element.48), channel_id=1, source_target_pairs={{0,1},{1,2},{2,3},{4,5},{5,6},{6,7},{8,9},{9,10},{10,11},{12,13},{... | collective-permute-start | bytes 2088968 | tf_op jit(solution)/shard_map/ppermute | solution.py:50
  150.9 4.5 %collective-permute-done.5 = f32[8,80,272]{2,1,0:T(8,128)S(1)} collective-permute-done((f32[8,80,272]{2,1,0:T(8,128)S(1)}, f32[8,80,272]{2,1,0:T(8,128)S(1)}, u32[]{:S(2)}, u32[]{:S(2)}) %collective-permute-start.5) | collective-permute-done | bytes 696352 | tf_op jit(solution)/shard_map/ppermute | solution.py:51
  158.3 3.4 collective-permute-start.6
  165.0 5.3 %collective-permute-done.7 = f32[9,1,9,33]{3,2,1,0:T(8,128)S(1)} collective-permute-done((f32[9,1,9,33]{3,2,1,0:T(8,128)S(1)}, f32[9,1,9,33]{3,2,1,0:T(8,128)S(1)}, u32[]{:S(2)}, u32[]{:S(2)}) %collective-permute-start.7) | collective-permute-done | bytes 10724 | tf_op jit(solution)/shard_map/ppermute | solution.py:63
  172.3 8.4 %collective-permute-start.9 = (f32[9,3,1,33]{3,2,1,0:T(1,128)S(1)}, f32[9,3,1,33]{3,2,1,0:T(1,128)S(1)}, u32[]{:S(2)}, u32[]{:S(2)}) collective-permute-start(f32[9,3,1,33]{3,2,1,0:T(1,128)S(1)} %get-tuple-element.119), channel_id=1, source_target_pairs={{16,0},{32,16},{48,32},{64,48},{80,64},{96,80},{112,96},{128,112},... | collective-permute-start | bytes 10700 | tf_op jit(solution)/shard_map/ppermute | solution.py:63
  182.4 10.7 %collective-permute-start.10 = (f32[9,3,9,1]{3,2,1,0:T(8,128)S(1)}, f32[9,3,9,1]{3,2,1,0:T(8,128)S(1)}, u32[]{:S(2)}, u32[]{:S(2)}) collective-permute-start(f32[9,3,9,1]{3,2,1,0:T(8,128)S(1)} %get-tuple-element.114), channel_id=1, source_target_pairs={{0,4},{4,8},{8,12},{1,5},{5,9},{9,13},{2,6},{6,10},{10,14},{3,7},{... | collective-permute-start | bytes 2924 | tf_op jit(solution)/shard_map/ppermute | solution.py:62
  194.7 3.9 %collective-permute-done.10 = f32[9,3,9,1]{3,2,1,0:T(8,128)S(1)} collective-permute-done((f32[9,3,9,1]{3,2,1,0:T(8,128)S(1)}, f32[9,3,9,1]{3,2,1,0:T(8,128)S(1)}, u32[]{:S(2)}, u32[]{:S(2)}) %collective-permute-start.10) | collective-permute-done | bytes 1004 | tf_op jit(solution)/shard_map/ppermute | solution.py:62
  198.6 4.7 %collective-permute-done.11 = f32[9,3,9,1]{3,2,1,0:T(8,128)S(1)} collective-permute-done((f32[9,3,9,1]{3,2,1,0:T(8,128)S(1)}, f32[9,3,9,1]{3,2,1,0:T(8,128)S(1)}, u32[]{:S(2)}, u32[]{:S(2)}) %collective-permute-start.11) | collective-permute-done | bytes 1004 | tf_op jit(solution)/shard_map/ppermute | solution.py:63
  207.1 3.9 %collective-permute-start.12 = (f32[3,1,9,33]{3,2,1,0:T(8,128)S(1)}, f32[3,1,9,33]{3,2,1,0:T(8,128)S(1)}, u32[]{:S(2)}, u32[]{:S(2)}) collective-permute-start(f32[3,1,9,33]{3,2,1,0:T(8,128)S(1)} %get-tuple-element.164), channel_id=1, source_target_pairs={{0,1},{1,2},{2,3},{4,5},{5,6},{6,7},{8,9},{9,10},{10,11},{12,13},{... | collective-permute-start | bytes 10700 | tf_op jit(solution)/shard_map/ppermute | solution.py:62
  212.5 4.2 %collective-permute-done.13 = f32[3,1,9,33]{3,2,1,0:T(8,128)S(1)} collective-permute-done((f32[3,1,9,33]{3,2,1,0:T(8,128)S(1)}, f32[3,1,9,33]{3,2,1,0:T(8,128)S(1)}, u32[]{:S(2)}, u32[]{:S(2)}) %collective-permute-start.13) | collective-permute-done | bytes 3596 | tf_op jit(solution)/shard_map/ppermute | solution.py:63
  218.7 7.8 %collective-permute-done.14 = f32[3,3,1,33]{3,2,1,0:T(1,128)S(1)} collective-permute-done((f32[3,3,1,33]{3,2,1,0:T(1,128)S(1)}, f32[3,3,1,33]{3,2,1,0:T(1,128)S(1)}, u32[]{:S(2)}, u32[]{:S(2)}) %collective-permute-start.14) | collective-permute-done | bytes 1220 | tf_op jit(solution)/shard_map/ppermute | solution.py:62
  229.8 3.2 collective-permute-start.16
  235.0 4.3 %collective-permute-done.17 = f32[3,3,9,1]{3,2,1,0:T(8,128)S(1)} collective-permute-done((f32[3,3,9,1]{3,2,1,0:T(8,128)S(1)}, f32[3,3,9,1]{3,2,1,0:T(8,128)S(1)}, u32[]{:S(2)}, u32[]{:S(2)}) %collective-permute-start.17) | collective-permute-done | bytes 356 | tf_op jit(solution)/shard_map/ppermute | solution.py:63
  243.3 3.2 collective-permute-start.18
  248.0 4.2 %collective-permute-done.19 = f32[3,1,9,33]{3,2,1,0:T(8,128)S(1)} collective-permute-done((f32[3,1,9,33]{3,2,1,0:T(8,128)S(1)}, f32[3,1,9,33]{3,2,1,0:T(8,128)S(1)}, u32[]{:S(2)}, u32[]{:S(2)}) %collective-permute-start.19) | collective-permute-done | bytes 3596 | tf_op jit(solution)/shard_map/ppermute | solution.py:63
  254.2 7.8 %collective-permute-done.20 = f32[3,3,1,33]{3,2,1,0:T(1,128)S(1)} collective-permute-done((f32[3,3,1,33]{3,2,1,0:T(1,128)S(1)}, f32[3,3,1,33]{3,2,1,0:T(1,128)S(1)}, u32[]{:S(2)}, u32[]{:S(2)}) %collective-permute-start.20) | collective-permute-done | bytes 1220 | tf_op jit(solution)/shard_map/ppermute | solution.py:62
  273.7 4.7 %collective-permute-done.23 = f32[3,3,9,1]{3,2,1,0:T(8,128)} collective-permute-done((f32[3,3,9,1]{3,2,1,0:T(8,128)}, f32[3,3,9,1]{3,2,1,0:T(8,128)}, u32[]{:S(2)}, u32[]{:S(2)}) %collective-permute-start.23) | collective-permute-done | bytes 356 | tf_op jit(solution)/shard_map/ppermute | solution.py:63
  290.4 4.2 %collective-permute-done.25 = f32[3,1,9,33]{3,2,1,0:T(8,128)S(1)} collective-permute-done((f32[3,1,9,33]{3,2,1,0:T(8,128)S(1)}, f32[3,1,9,33]{3,2,1,0:T(8,128)S(1)}, u32[]{:S(2)}, u32[]{:S(2)}) %collective-permute-start.25) | collective-permute-done | bytes 3596 | tf_op jit(solution)/shard_map/ppermute | solution.py:63
  296.5 7.8 %collective-permute-done.26 = f32[3,3,1,33]{3,2,1,0:T(1,128)S(1)} collective-permute-done((f32[3,3,1,33]{3,2,1,0:T(1,128)S(1)}, f32[3,3,1,33]{3,2,1,0:T(1,128)S(1)}, u32[]{:S(2)}, u32[]{:S(2)}) %collective-permute-start.26) | collective-permute-done | bytes 1220 | tf_op jit(solution)/shard_map/ppermute | solution.py:62
  311.3 4.3 %collective-permute-done.29 = f32[3,3,9,1]{3,2,1,0:T(8,128)S(1)} collective-permute-done((f32[3,3,9,1]{3,2,1,0:T(8,128)S(1)}, f32[3,3,9,1]{3,2,1,0:T(8,128)S(1)}, u32[]{:S(2)}, u32[]{:S(2)}) %collective-permute-start.29) | collective-permute-done | bytes 356 | tf_op jit(solution)/shard_map/ppermute | solution.py:63
  322.3 4.2 %collective-permute-done.31 = f32[3,1,9,33]{3,2,1,0:T(8,128)S(1)} collective-permute-done((f32[3,1,9,33]{3,2,1,0:T(8,128)S(1)}, f32[3,1,9,33]{3,2,1,0:T(8,128)S(1)}, u32[]{:S(2)}, u32[]{:S(2)}) %collective-permute-start.31) | collective-permute-done | bytes 3596 | tf_op jit(solution)/shard_map/ppermute | solution.py:63
  328.5 7.8 %collective-permute-done.32 = f32[3,3,1,33]{3,2,1,0:T(1,128)S(1)} collective-permute-done((f32[3,3,1,33]{3,2,1,0:T(1,128)S(1)}, f32[3,3,1,33]{3,2,1,0:T(1,128)S(1)}, u32[]{:S(2)}, u32[]{:S(2)}) %collective-permute-start.32) | collective-permute-done | bytes 1220 | tf_op jit(solution)/shard_map/ppermute | solution.py:62
  343.5 4.3 %collective-permute-done.35 = f32[3,3,9,1]{3,2,1,0:T(8,128)S(1)} collective-permute-done((f32[3,3,9,1]{3,2,1,0:T(8,128)S(1)}, f32[3,3,9,1]{3,2,1,0:T(8,128)S(1)}, u32[]{:S(2)}, u32[]{:S(2)}) %collective-permute-start.35) | collective-permute-done | bytes 356 | tf_op jit(solution)/shard_map/ppermute | solution.py:63
  354.6 4.2 %collective-permute-done.37 = f32[3,1,9,33]{3,2,1,0:T(8,128)S(1)} collective-permute-done((f32[3,1,9,33]{3,2,1,0:T(8,128)S(1)}, f32[3,1,9,33]{3,2,1,0:T(8,128)S(1)}, u32[]{:S(2)}, u32[]{:S(2)}) %collective-permute-start.37) | collective-permute-done | bytes 3596 | tf_op jit(solution)/shard_map/ppermute | solution.py:63
  360.8 7.8 %collective-permute-done.38 = f32[3,3,1,33]{3,2,1,0:T(1,128)S(1)} collective-permute-done((f32[3,3,1,33]{3,2,1,0:T(1,128)S(1)}, f32[3,3,1,33]{3,2,1,0:T(1,128)S(1)}, u32[]{:S(2)}, u32[]{:S(2)}) %collective-permute-start.38) | collective-permute-done | bytes 1220 | tf_op jit(solution)/shard_map/ppermute | solution.py:62
  375.8 4.3 %collective-permute-done.41 = f32[3,3,9,1]{3,2,1,0:T(8,128)S(1)} collective-permute-done((f32[3,3,9,1]{3,2,1,0:T(8,128)S(1)}, f32[3,3,9,1]{3,2,1,0:T(8,128)S(1)}, u32[]{:S(2)}, u32[]{:S(2)}) %collective-permute-start.41) | collective-permute-done | bytes 356 | tf_op jit(solution)/shard_map/ppermute | solution.py:63
  (265 shorter events, 127.2 us)
Async XLA Ops:
  6.3 5.7 %collective-permute-start = (f32[2,1024,8]{1,2,0:T(8,128)S(1)}, f32[2,1024,8]{1,2,0:T(8,128)S(1)}, u32[]{:S(2)}, u32[]{:S(2)}) collective-permute-start(f32[2,1024,8]{1,2,0:T(8,128)S(1)} %copy.45), channel_id=1, source_target_pairs={{0,4},{4,8},{8,12},{1,5},{5,9},{9,13},{2,6},{6,10},{10,14},{3,7},{... | collective-permute-start | bytes 196616 | tf_op jit(solution)/shard_map/ppermute | solution.py:50
  10.5 6.2 %collective-permute-start.1 = (f32[2,1024,8]{1,2,0:T(8,128)S(1)}, f32[2,1024,8]{1,2,0:T(8,128)S(1)}, u32[]{:S(2)}, u32[]{:S(2)}) collective-permute-start(f32[2,1024,8]{1,2,0:T(8,128)S(1)} %copy.46), channel_id=1, source_target_pairs={{4,0},{8,4},{12,8},{5,1},{9,5},{13,9},{6,2},{10,6},{14,10},{7,3},{... | collective-permute-start | bytes 196616 | tf_op jit(solution)/shard_map/ppermute | solution.py:51
  24.0 101.2 %all-to-all-start = ((f32[16,2,80,272]{3,2,1,0:T(8,128)}), f32[16,2,80,272]{3,2,1,0:T(8,128)}, u32[]{:S(2)}, u32[]{:S(2)}) async-start(f32[16,2,80,272]{3,2,1,0:T(8,128)} %copy.49), calls=%async_computation | async-start | bytes 7864320 | tf_op jit(solution)/shard_map/all_to_all | solution.py:165
  127.7 13.2 %collective-permute-start.3 = (f32[1,66,258]{2,1,0:T(8,128)S(1)}, f32[1,66,258]{2,1,0:T(8,128)S(1)}, u32[]{:S(2)}, u32[]{:S(2)}) collective-permute-start(f32[1,66,258]{2,1,0:T(8,128)S(1)} %get-tuple-element.59), channel_id=1, source_target_pairs={{0,1},{1,2},{2,3},{4,5},{5,6},{6,7},{8,9},{9,10},{10,11},{12,13},{... | collective-permute-start | bytes 204344 | tf_op jit(solution)/shard_map/ppermute | solution.py:50
  131.2 9.7 %collective-permute-start.2 = (f32[1,66,258]{2,1,0:T(8,128)S(1)}, f32[1,66,258]{2,1,0:T(8,128)S(1)}, u32[]{:S(2)}, u32[]{:S(2)}) collective-permute-start(f32[1,66,258]{2,1,0:T(8,128)S(1)} %get-tuple-element.60), channel_id=1, source_target_pairs={{1,0},{2,1},{3,2},{5,4},{6,5},{7,6},{9,8},{10,9},{11,10},{13,12},{... | collective-permute-start | bytes 204344 | tf_op jit(solution)/shard_map/ppermute | solution.py:51
  134.7 16.2 %collective-permute-start.4 = (f32[8,80,272]{2,1,0:T(8,128)S(1)}, f32[8,80,272]{2,1,0:T(8,128)S(1)}, u32[]{:S(2)}, u32[]{:S(2)}) collective-permute-start(f32[8,80,272]{2,1,0:T(8,128)S(1)} %get-tuple-element.48), channel_id=1, source_target_pairs={{0,1},{1,2},{2,3},{4,5},{5,6},{6,7},{8,9},{9,10},{10,11},{12,13},{... | collective-permute-start | bytes 2088968 | tf_op jit(solution)/shard_map/ppermute | solution.py:50
  139.4 16.0 %collective-permute-start.5 = (f32[8,80,272]{2,1,0:T(8,128)S(1)}, f32[8,80,272]{2,1,0:T(8,128)S(1)}, u32[]{:S(2)}, u32[]{:S(2)}) collective-permute-start(f32[8,80,272]{2,1,0:T(8,128)S(1)} %get-tuple-element.49), channel_id=1, source_target_pairs={{1,0},{2,1},{3,2},{5,4},{6,5},{7,6},{9,8},{10,9},{11,10},{13,12},{... | collective-permute-start | bytes 2088968 | tf_op jit(solution)/shard_map/ppermute | solution.py:51
  158.3 5.4 %collective-permute-start.6 = (f32[9,1,9,33]{3,2,1,0:T(8,128)S(1)}, f32[9,1,9,33]{3,2,1,0:T(8,128)S(1)}, u32[]{:S(2)}, u32[]{:S(2)}) collective-permute-start(f32[9,1,9,33]{3,2,1,0:T(8,128)S(1)} %fusion.61), channel_id=1, source_target_pairs={{0,1},{1,2},{2,3},{4,5},{5,6},{6,7},{8,9},{9,10},{10,11},{12,13},{... | collective-permute-start | bytes 32084 | tf_op jit(solution)/shard_map/ppermute | solution.py:62
  163.7 6.6 %collective-permute-start.7 = (f32[9,1,9,33]{3,2,1,0:T(8,128)S(1)}, f32[9,1,9,33]{3,2,1,0:T(8,128)S(1)}, u32[]{:S(2)}, u32[]{:S(2)}) collective-permute-start(f32[9,1,9,33]{3,2,1,0:T(8,128)S(1)} %get-tuple-element.42), channel_id=1, source_target_pairs={{1,0},{2,1},{3,2},{5,4},{6,5},{7,6},{9,8},{10,9},{11,10},{13,12},{... | collective-permute-start | bytes 32084 | tf_op jit(solution)/shard_map/ppermute | solution.py:63
  170.4 10.4 %collective-permute-start.8 = (f32[9,3,1,33]{3,2,1,0:T(1,128)S(1)}, f32[9,3,1,33]{3,2,1,0:T(1,128)S(1)}, u32[]{:S(2)}, u32[]{:S(2)}) collective-permute-start(f32[9,3,1,33]{3,2,1,0:T(1,128)S(1)} %get-tuple-element.118), channel_id=1, source_target_pairs={{0,16},{16,32},{32,48},{48,64},{64,80},{80,96},{96,112},{112,128},... | collective-permute-start | bytes 10700 | tf_op jit(solution)/shard_map/ppermute | solution.py:62
  172.3 9.9 %collective-permute-start.9 = (f32[9,3,1,33]{3,2,1,0:T(1,128)S(1)}, f32[9,3,1,33]{3,2,1,0:T(1,128)S(1)}, u32[]{:S(2)}, u32[]{:S(2)}) collective-permute-start(f32[9,3,1,33]{3,2,1,0:T(1,128)S(1)} %get-tuple-element.119), channel_id=1, source_target_pairs={{16,0},{32,16},{48,32},{64,48},{80,64},{96,80},{112,96},{128,112},... | collective-permute-start | bytes 10700 | tf_op jit(solution)/shard_map/ppermute | solution.py:63
  182.4 16.2 %collective-permute-start.10 = (f32[9,3,9,1]{3,2,1,0:T(8,128)S(1)}, f32[9,3,9,1]{3,2,1,0:T(8,128)S(1)}, u32[]{:S(2)}, u32[]{:S(2)}) collective-permute-start(f32[9,3,9,1]{3,2,1,0:T(8,128)S(1)} %get-tuple-element.114), channel_id=1, source_target_pairs={{0,4},{4,8},{8,12},{1,5},{5,9},{9,13},{2,6},{6,10},{10,14},{3,7},{... | collective-permute-start | bytes 2924 | tf_op jit(solution)/shard_map/ppermute | solution.py:62
  193.1 10.2 %collective-permute-start.11 = (f32[9,3,9,1]{3,2,1,0:T(8,128)S(1)}, f32[9,3,9,1]{3,2,1,0:T(8,128)S(1)}, u32[]{:S(2)}, u32[]{:S(2)}) collective-permute-start(f32[9,3,9,1]{3,2,1,0:T(8,128)S(1)} %get-tuple-element.115), channel_id=1, source_target_pairs={{4,0},{8,4},{12,8},{5,1},{9,5},{13,9},{6,2},{10,6},{14,10},{7,3},{... | collective-permute-start | bytes 2924 | tf_op jit(solution)/shard_map/ppermute | solution.py:63
  207.1 5.4 %collective-permute-start.12 = (f32[3,1,9,33]{3,2,1,0:T(8,128)S(1)}, f32[3,1,9,33]{3,2,1,0:T(8,128)S(1)}, u32[]{:S(2)}, u32[]{:S(2)}) collective-permute-start(f32[3,1,9,33]{3,2,1,0:T(8,128)S(1)} %get-tuple-element.164), channel_id=1, source_target_pairs={{0,1},{1,2},{2,3},{4,5},{5,6},{6,7},{8,9},{9,10},{10,11},{12,13},{... | collective-permute-start | bytes 10700 | tf_op jit(solution)/shard_map/ppermute | solution.py:62
  211.0 5.7 %collective-permute-start.13 = (f32[3,1,9,33]{3,2,1,0:T(8,128)S(1)}, f32[3,1,9,33]{3,2,1,0:T(8,128)S(1)}, u32[]{:S(2)}, u32[]{:S(2)}) collective-permute-start(f32[3,1,9,33]{3,2,1,0:T(8,128)S(1)} %get-tuple-element.165), channel_id=1, source_target_pairs={{1,0},{2,1},{3,2},{5,4},{6,5},{7,6},{9,8},{10,9},{11,10},{13,12},{... | collective-permute-start | bytes 10700 | tf_op jit(solution)/shard_map/ppermute | solution.py:63
  216.7 9.7 %collective-permute-start.14 = (f32[3,3,1,33]{3,2,1,0:T(1,128)S(1)}, f32[3,3,1,33]{3,2,1,0:T(1,128)S(1)}, u32[]{:S(2)}, u32[]{:S(2)}) collective-permute-start(f32[3,3,1,33]{3,2,1,0:T(1,128)S(1)} %pad_maximum_fusion.25), channel_id=1, source_target_pairs={{0,16},{16,32},{32,48},{48,64},{64,80},{80,96},{96,112},{112,128},... | collective-permute-start | bytes 3572 | tf_op jit(solution)/shard_map/ppermute | solution.py:62
  229.8 5.2 %collective-permute-start.16 = (f32[3,3,9,1]{3,2,1,0:T(8,128)S(1)}, f32[3,3,9,1]{3,2,1,0:T(8,128)S(1)}, u32[]{:S(2)}, u32[]{:S(2)}) collective-permute-start(f32[3,3,9,1]{3,2,1,0:T(8,128)S(1)} %get-tuple-element.159), channel_id=1, source_target_pairs={{0,4},{4,8},{8,12},{1,5},{5,9},{9,13},{2,6},{6,10},{10,14},{3,7},{... | collective-permute-start | bytes 980 | tf_op jit(solution)/shard_map/ppermute | solution.py:62
  233.0 6.2 %collective-permute-start.17 = (f32[3,3,9,1]{3,2,1,0:T(8,128)S(1)}, f32[3,3,9,1]{3,2,1,0:T(8,128)S(1)}, u32[]{:S(2)}, u32[]{:S(2)}) collective-permute-start(f32[3,3,9,1]{3,2,1,0:T(8,128)S(1)} %get-tuple-element.160), channel_id=1, source_target_pairs={{4,0},{8,4},{12,8},{5,1},{9,5},{13,9},{6,2},{10,6},{14,10},{7,3},{... | collective-permute-start | bytes 980 | tf_op jit(solution)/shard_map/ppermute | solution.py:63
  243.3 4.7 %collective-permute-start.18 = (f32[3,1,9,33]{3,2,1,0:T(8,128)S(1)}, f32[3,1,9,33]{3,2,1,0:T(8,128)S(1)}, u32[]{:S(2)}, u32[]{:S(2)}) collective-permute-start(f32[3,1,9,33]{3,2,1,0:T(8,128)S(1)} %get-tuple-element.155), channel_id=1, source_target_pairs={{0,1},{1,2},{2,3},{4,5},{5,6},{6,7},{8,9},{9,10},{10,11},{12,13},{... | collective-permute-start | bytes 10700 | tf_op jit(solution)/shard_map/ppermute | solution.py:62
  246.5 5.7 %collective-permute-start.19 = (f32[3,1,9,33]{3,2,1,0:T(8,128)S(1)}, f32[3,1,9,33]{3,2,1,0:T(8,128)S(1)}, u32[]{:S(2)}, u32[]{:S(2)}) collective-permute-start(f32[3,1,9,33]{3,2,1,0:T(8,128)S(1)} %get-tuple-element.156), channel_id=1, source_target_pairs={{1,0},{2,1},{3,2},{5,4},{6,5},{7,6},{9,8},{10,9},{11,10},{13,12},{... | collective-permute-start | bytes 10700 | tf_op jit(solution)/shard_map/ppermute | solution.py:63
  252.3 9.7 %collective-permute-start.20 = (f32[3,3,1,33]{3,2,1,0:T(1,128)S(1)}, f32[3,3,1,33]{3,2,1,0:T(1,128)S(1)}, u32[]{:S(2)}, u32[]{:S(2)}) collective-permute-start(f32[3,3,1,33]{3,2,1,0:T(1,128)S(1)} %pad_maximum_fusion.23), channel_id=1, source_target_pairs={{0,16},{16,32},{32,48},{48,64},{64,80},{80,96},{96,112},{112,128},... | collective-permute-start | bytes 3572 | tf_op jit(solution)/shard_map/ppermute | solution.py:62
  262.1 5.4 %collective-permute-start.21 = (f32[3,3,1,33]{3,2,1,0:T(1,128)S(1)}, f32[3,3,1,33]{3,2,1,0:T(1,128)S(1)}, u32[]{:S(2)}, u32[]{:S(2)}) collective-permute-start(f32[3,3,1,33]{3,2,1,0:T(1,128)S(1)} %get-tuple-element.29), channel_id=1, source_target_pairs={{16,0},{32,16},{48,32},{64,48},{80,64},{96,80},{112,96},{128,112},... | collective-permute-start | bytes 3572 | tf_op jit(solution)/shard_map/ppermute | solution.py:63
  271.8 6.6 %collective-permute-start.23 = (f32[3,3,9,1]{3,2,1,0:T(8,128)}, f32[3,3,9,1]{3,2,1,0:T(8,128)}, u32[]{:S(2)}, u32[]{:S(2)}) collective-permute-start(f32[3,3,9,1]{3,2,1,0:T(8,128)} %get-tuple-element.151), channel_id=1, source_target_pairs={{4,0},{8,4},{12,8},{5,1},{9,5},{13,9},{6,2},{10,6},{14,10},{7,3},{... | collective-permute-start | bytes 980 | tf_op jit(solution)/shard_map/ppermute | solution.py:63
  288.9 5.7 %collective-permute-start.25 = (f32[3,1,9,33]{3,2,1,0:T(8,128)S(1)}, f32[3,1,9,33]{3,2,1,0:T(8,128)S(1)}, u32[]{:S(2)}, u32[]{:S(2)}) collective-permute-start(f32[3,1,9,33]{3,2,1,0:T(8,128)S(1)} %get-tuple-element.147), channel_id=1, source_target_pairs={{1,0},{2,1},{3,2},{5,4},{6,5},{7,6},{9,8},{10,9},{11,10},{13,12},{... | collective-permute-start | bytes 10700 | tf_op jit(solution)/shard_map/ppermute | solution.py:63
  294.6 9.7 %collective-permute-start.26 = (f32[3,3,1,33]{3,2,1,0:T(1,128)S(1)}, f32[3,3,1,33]{3,2,1,0:T(1,128)S(1)}, u32[]{:S(2)}, u32[]{:S(2)}) collective-permute-start(f32[3,3,1,33]{3,2,1,0:T(1,128)S(1)} %pad_maximum_fusion.21), channel_id=1, source_target_pairs={{0,16},{16,32},{32,48},{48,64},{64,80},{80,96},{96,112},{112,128},... | collective-permute-start | bytes 3572 | tf_op jit(solution)/shard_map/ppermute | solution.py:62
  309.3 6.2 %collective-permute-start.29 = (f32[3,3,9,1]{3,2,1,0:T(8,128)S(1)}, f32[3,3,9,1]{3,2,1,0:T(8,128)S(1)}, u32[]{:S(2)}, u32[]{:S(2)}) collective-permute-start(f32[3,3,9,1]{3,2,1,0:T(8,128)S(1)} %get-tuple-element.142), channel_id=1, source_target_pairs={{4,0},{8,4},{12,8},{5,1},{9,5},{13,9},{6,2},{10,6},{14,10},{7,3},{... | collective-permute-start | bytes 980 | tf_op jit(solution)/shard_map/ppermute | solution.py:63
  320.8 5.7 %collective-permute-start.31 = (f32[3,1,9,33]{3,2,1,0:T(8,128)S(1)}, f32[3,1,9,33]{3,2,1,0:T(8,128)S(1)}, u32[]{:S(2)}, u32[]{:S(2)}) collective-permute-start(f32[3,1,9,33]{3,2,1,0:T(8,128)S(1)} %get-tuple-element.138), channel_id=1, source_target_pairs={{1,0},{2,1},{3,2},{5,4},{6,5},{7,6},{9,8},{10,9},{11,10},{13,12},{... | collective-permute-start | bytes 10700 | tf_op jit(solution)/shard_map/ppermute | solution.py:63
  326.5 9.8 %collective-permute-start.32 = (f32[3,3,1,33]{3,2,1,0:T(1,128)S(1)}, f32[3,3,1,33]{3,2,1,0:T(1,128)S(1)}, u32[]{:S(2)}, u32[]{:S(2)}) collective-permute-start(f32[3,3,1,33]{3,2,1,0:T(1,128)S(1)} %pad_maximum_fusion.19), channel_id=1, source_target_pairs={{0,16},{16,32},{32,48},{48,64},{64,80},{80,96},{96,112},{112,128},... | collective-permute-start | bytes 3572 | tf_op jit(solution)/shard_map/ppermute | solution.py:62
  341.6 6.2 %collective-permute-start.35 = (f32[3,3,9,1]{3,2,1,0:T(8,128)S(1)}, f32[3,3,9,1]{3,2,1,0:T(8,128)S(1)}, u32[]{:S(2)}, u32[]{:S(2)}) collective-permute-start(f32[3,3,9,1]{3,2,1,0:T(8,128)S(1)} %get-tuple-element.133), channel_id=1, source_target_pairs={{4,0},{8,4},{12,8},{5,1},{9,5},{13,9},{6,2},{10,6},{14,10},{7,3},{... | collective-permute-start | bytes 980 | tf_op jit(solution)/shard_map/ppermute | solution.py:63
  353.1 5.7 %collective-permute-start.37 = (f32[3,1,9,33]{3,2,1,0:T(8,128)S(1)}, f32[3,1,9,33]{3,2,1,0:T(8,128)S(1)}, u32[]{:S(2)}, u32[]{:S(2)}) collective-permute-start(f32[3,1,9,33]{3,2,1,0:T(8,128)S(1)} %get-tuple-element.129), channel_id=1, source_target_pairs={{1,0},{2,1},{3,2},{5,4},{6,5},{7,6},{9,8},{10,9},{11,10},{13,12},{... | collective-permute-start | bytes 10700 | tf_op jit(solution)/shard_map/ppermute | solution.py:63
  358.9 9.8 %collective-permute-start.38 = (f32[3,3,1,33]{3,2,1,0:T(1,128)S(1)}, f32[3,3,1,33]{3,2,1,0:T(1,128)S(1)}, u32[]{:S(2)}, u32[]{:S(2)}) collective-permute-start(f32[3,3,1,33]{3,2,1,0:T(1,128)S(1)} %pad_maximum_fusion.17), channel_id=1, source_target_pairs={{0,16},{16,32},{32,48},{48,64},{64,80},{80,96},{96,112},{112,128},... | collective-permute-start | bytes 3572 | tf_op jit(solution)/shard_map/ppermute | solution.py:62
  373.9 6.2 %collective-permute-start.41 = (f32[3,3,9,1]{3,2,1,0:T(8,128)S(1)}, f32[3,3,9,1]{3,2,1,0:T(8,128)S(1)}, u32[]{:S(2)}, u32[]{:S(2)}) collective-permute-start(f32[3,3,9,1]{3,2,1,0:T(8,128)S(1)} %get-tuple-element.124), channel_id=1, source_target_pairs={{4,0},{8,4},{12,8},{5,1},{9,5},{13,9},{6,2},{10,6},{14,10},{7,3},{... | collective-permute-start | bytes 980 | tf_op jit(solution)/shard_map/ppermute | solution.py:63
  (32 other events, 237.1 us)

commit v2 on v1

--- a/solution.py
+++ b/solution.py
@@ -163,10 +163,17 @@
     windows = jnp.concatenate([low, main, high], axis=2)
     windows = jnp.moveaxis(windows, 1, 0)
     brick = lax.all_to_all(windows, "gx", split_axis=0, concat_axis=0, tiled=True)
+    forward, backward = neighbours("gz")
+    bz = brick.shape[0]
     image = brick[:, 0]
     deformed = brick[:, 1]
-    image_ext = halo(image[:, DMAX - 1 : DMAX + bx + 1, DMAX - 1 : ny - DMAX + 1], "gz", 0, 1)
-    deformed_ext = halo(deformed, "gz", 0, DMAX)
+    to_high = jnp.concatenate([deformed[bz - DMAX :], image[bz - 1 :]], axis=0)
+    to_low = jnp.concatenate([deformed[:DMAX], image[:1]], axis=0)
+    from_low = lax.ppermute(to_high, "gz", forward)
+    from_high = lax.ppermute(to_low, "gz", backward)
+    deformed_ext = jnp.concatenate([from_low[:DMAX], deformed, from_high[:DMAX]], axis=0)
+    image_ext = jnp.concatenate([from_low[DMAX:], image, from_high[DMAX:]], axis=0)
+    image_ext = image_ext[:, DMAX - 1 : DMAX + bx + 1, DMAX - 1 : ny - DMAX + 1]
     return image_ext, deformed_ext
 
 

time: 387 us -> 390 us (level)
  blocking collectives: 0 us -> 101 us
  waiting for transfers between devices: 204 us -> 127 us
  starting transfers between devices: 111 us -> 89.1 us
    all_to_all x0 -> x1, blocking collectives: none -> 101 us  [bricks_of(): lax.all_to_all(windows, 'gx', split_axis=0, concat_axis=0, tiled=True)]
    all_to_all x1 -> x0, waiting for transfers between devices: 85.3 us -> none  [bricks_of(): lax.all_to_all(windows, 'gx', split_axis=0, concat_axis=0, tiled=True)]
    ppermute x0 -> x2, waiting for transfers between devices: none -> 16.1 us  [the longest x1 13.6 us: bricks_of(): from_high = lax.ppermute(to_low, 'gz', backward)]
    all_to_all x1 -> x0, starting transfers between devices: 10.7 us -> none  [bricks_of(): lax.all_to_all(windows, 'gx', split_axis=0, concat_axis=0, tiled=True)]
    ppermute x3 -> x1, starting transfers between devices: 11.9 us -> 3.83 us  [halo(): lax.ppermute(lax.slice_in_dim(block, size - width, size, axis=dim), axis,...]
    ppermute x0 -> x2, starting transfers between devices: none -> 6.08 us  [the longest x1 4.78 us: bricks_of(): from_low = lax.ppermute(to_high, 'gz', forward)]
    ppermute x18, starting transfers between devices: 49.9 us -> 43.9 us  [share(): from_low = lax.ppermute(last, axis, forward)]
  transfers between devices with their start and end apart: 43 -> 40, of which waited for: 39 -> 38; matrix products, arithmetic and copies ran while one was open for 3% -> 1% of each run, Pallas kernels for 0% -> 0%
where the time goes in v2:
time: 390 us; the launch traced here: 387 us
  waiting for transfers between devices  127 us (33%)
  blocking collectives  101 us (26%)
  starting transfers between devices  89.1 us (23%)
  other arithmetic  28.9 us (7%)
  local copies, waits for them, and re-layouts  19.9 us (5%)
  matrix products  11.5 us (3%)
  between operations  9.54 us (2%)
    all_to_all x1, blocking collectives, bricks_of(): lax.all_to_all(windows, 'gx', split_axis=0, concat_axis=0, tiled=True)  101 us
    ppermute x18, waiting for transfers between devices, share(): from_high = lax.ppermute(first, axis, backward)  59 us
    ppermute x18, waiting for transfers between devices, share(): from_low = lax.ppermute(last, axis, forward)  47.8 us
    ppermute x18, starting transfers between devices, share(): from_low = lax.ppermute(last, axis, forward)  43.9 us
    ppermute x18, starting transfers between devices, share(): from_high = lax.ppermute(first, axis, backward)  34 us
    ppermute x1, waiting for transfers between devices, bricks_of(): from_high = lax.ppermute(to_low, 'gz', backward)  13.6 us
  transfers between devices with their start and end apart: 40, of which 38 were waited for; matrix products, arithmetic and copies ran while one was open for 1% of the time, Pallas kernels for 0%

profile of v2, /device:TPU:4, one launch (start us, length us, event | category | flops | bytes accessed | tf_op | source)
XLA Modules:
  0.0 387.0 jit_solution(12991424805322420066)
XLA Ops:
  6.1 3.8 collective-permute-start
  12.1 4.2 %collective-permute-done.1 = f32[2,1024,8]{1,2,0:T(8,128)S(1)} collective-permute-done((f32[2,1024,8]{1,2,0:T(8,128)S(1)}, f32[2,1024,8]{1,2,0:T(8,128)S(1)}, u32[]{:S(2)}, u32[]{:S(2)}) %collective-permute-start.1) | collective-permute-done | bytes 65568 | tf_op jit(solution)/shard_map/ppermute | solution.py:51
  20.8 100.6 %all_to_all.5 = f32[16,2,80,272]{3,2,1,0:T(8,128)S(1)} all-to-all(f32[16,2,80,272]{3,2,1,0:T(8,128)S(1)} %copy.44), channel_id=1, replica_groups=mesh['gx'=16,'gy'=4,'gz'=4] {'gx'}, dimensions={0} | all-to-all | bytes 5570560 | tf_op jit(solution)/shard_map/all_to_all | solution.py:165
  125.9 4.8 %collective-permute-start.3 = (f32[9,80,272]{2,1,0:T(8,128)}, f32[9,80,272]{2,1,0:T(8,128)S(1)}, u32[]{:S(2)}, u32[]{:S(2)}) collective-permute-start(f32[9,80,272]{2,1,0:T(8,128)} %pad_maximum_fusion.7), channel_id=1, source_target_pairs={{0,1},{1,2},{2,3},{4,5},{5,6},{6,7},{8,9},{9,10},{10,11},{12,13},{... | collective-permute-start | bytes 2350088 | tf_op jit(solution)/shard_map/ppermute | solution.py:172
  135.6 2.4 slice_bitcast_fusion
  138.0 13.6 %collective-permute-done.2 = f32[9,80,272]{2,1,0:T(8,128)S(1)} collective-permute-done((f32[9,80,272]{2,1,0:T(8,128)S(1)}, f32[9,80,272]{2,1,0:T(8,128)S(1)}, u32[]{:S(2)}, u32[]{:S(2)}) %collective-permute-start.2) | collective-permute-done | bytes 783392 | tf_op jit(solution)/shard_map/ppermute | solution.py:173
  151.6 2.5 collective-permute-done.3
  168.0 4.3 %collective-permute-start.4 = (f32[9,1,9,33]{3,2,1,0:T(8,128)S(1)}, f32[9,1,9,33]{3,2,1,0:T(8,128)S(1)}, u32[]{:S(2)}, u32[]{:S(2)}) collective-permute-start(f32[9,1,9,33]{3,2,1,0:T(8,128)S(1)} %fusion.61), channel_id=1, source_target_pairs={{0,1},{1,2},{2,3},{4,5},{5,6},{6,7},{8,9},{9,10},{10,11},{12,13},{... | collective-permute-start | bytes 32084 | tf_op jit(solution)/shard_map/ppermute | solution.py:62
  175.6 5.3 %collective-permute-done.5 = f32[9,1,9,33]{3,2,1,0:T(8,128)S(1)} collective-permute-done((f32[9,1,9,33]{3,2,1,0:T(8,128)S(1)}, f32[9,1,9,33]{3,2,1,0:T(8,128)S(1)}, u32[]{:S(2)}, u32[]{:S(2)}) %collective-permute-start.5) | collective-permute-done | bytes 10724 | tf_op jit(solution)/shard_map/ppermute | solution.py:63
  182.9 8.4 %collective-permute-start.7 = (f32[9,3,1,33]{3,2,1,0:T(1,128)S(1)}, f32[9,3,1,33]{3,2,1,0:T(1,128)S(1)}, u32[]{:S(2)}, u32[]{:S(2)}) collective-permute-start(f32[9,3,1,33]{3,2,1,0:T(1,128)S(1)} %get-tuple-element.119), channel_id=1, source_target_pairs={{16,0},{32,16},{48,32},{64,48},{80,64},{96,80},{112,96},{128,112},... | collective-permute-start | bytes 10700 | tf_op jit(solution)/shard_map/ppermute | solution.py:63
  192.9 3.3 collective-permute-start.8
  197.8 3.2 collective-permute-done.8
  201.0 4.1 %collective-permute-done.9 = f32[9,3,9,1]{3,2,1,0:T(8,128)S(1)} collective-permute-done((f32[9,3,9,1]{3,2,1,0:T(8,128)S(1)}, f32[9,3,9,1]{3,2,1,0:T(8,128)S(1)}, u32[]{:S(2)}, u32[]{:S(2)}) %collective-permute-start.9) | collective-permute-done | bytes 1004 | tf_op jit(solution)/shard_map/ppermute | solution.py:63
  208.9 3.9 %collective-permute-start.10 = (f32[3,1,9,33]{3,2,1,0:T(8,128)S(1)}, f32[3,1,9,33]{3,2,1,0:T(8,128)S(1)}, u32[]{:S(2)}, u32[]{:S(2)}) collective-permute-start(f32[3,1,9,33]{3,2,1,0:T(8,128)S(1)} %get-tuple-element.164), channel_id=1, source_target_pairs={{0,1},{1,2},{2,3},{4,5},{5,6},{6,7},{8,9},{9,10},{10,11},{12,13},{... | collective-permute-start | bytes 10700 | tf_op jit(solution)/shard_map/ppermute | solution.py:62
  214.3 4.2 %collective-permute-done.11 = f32[3,1,9,33]{3,2,1,0:T(8,128)S(1)} collective-permute-done((f32[3,1,9,33]{3,2,1,0:T(8,128)S(1)}, f32[3,1,9,33]{3,2,1,0:T(8,128)S(1)}, u32[]{:S(2)}, u32[]{:S(2)}) %collective-permute-start.11) | collective-permute-done | bytes 3596 | tf_op jit(solution)/shard_map/ppermute | solution.py:63
  220.5 7.8 %collective-permute-done.12 = f32[3,3,1,33]{3,2,1,0:T(1,128)S(1)} collective-permute-done((f32[3,3,1,33]{3,2,1,0:T(1,128)S(1)}, f32[3,3,1,33]{3,2,1,0:T(1,128)S(1)}, u32[]{:S(2)}, u32[]{:S(2)}) %collective-permute-start.12) | collective-permute-done | bytes 1220 | tf_op jit(solution)/shard_map/ppermute | solution.py:62
  231.7 3.4 collective-permute-start.14
  237.1 4.3 %collective-permute-done.15 = f32[3,3,9,1]{3,2,1,0:T(8,128)S(1)} collective-permute-done((f32[3,3,9,1]{3,2,1,0:T(8,128)S(1)}, f32[3,3,9,1]{3,2,1,0:T(8,128)S(1)}, u32[]{:S(2)}, u32[]{:S(2)}) %collective-permute-start.15) | collective-permute-done | bytes 356 | tf_op jit(solution)/shard_map/ppermute | solution.py:63
  245.3 3.5 collective-permute-start.16
  250.3 4.2 %collective-permute-done.17 = f32[3,1,9,33]{3,2,1,0:T(8,128)S(1)} collective-permute-done((f32[3,1,9,33]{3,2,1,0:T(8,128)S(1)}, f32[3,1,9,33]{3,2,1,0:T(8,128)S(1)}, u32[]{:S(2)}, u32[]{:S(2)}) %collective-permute-start.17) | collective-permute-done | bytes 3596 | tf_op jit(solution)/shard_map/ppermute | solution.py:63
  256.6 7.8 %collective-permute-done.18 = f32[3,3,1,33]{3,2,1,0:T(1,128)S(1)} collective-permute-done((f32[3,3,1,33]{3,2,1,0:T(1,128)S(1)}, f32[3,3,1,33]{3,2,1,0:T(1,128)S(1)}, u32[]{:S(2)}, u32[]{:S(2)}) %collective-permute-start.18) | collective-permute-done | bytes 1220 | tf_op jit(solution)/shard_map/ppermute | solution.py:62
  271.5 2.8 collective-permute-start.20
  276.2 4.7 %collective-permute-done.21 = f32[3,3,9,1]{3,2,1,0:T(8,128)} collective-permute-done((f32[3,3,9,1]{3,2,1,0:T(8,128)}, f32[3,3,9,1]{3,2,1,0:T(8,128)}, u32[]{:S(2)}, u32[]{:S(2)}) %collective-permute-start.21) | collective-permute-done | bytes 356 | tf_op jit(solution)/shard_map/ppermute | solution.py:63
  292.8 4.2 %collective-permute-done.23 = f32[3,1,9,33]{3,2,1,0:T(8,128)S(1)} collective-permute-done((f32[3,1,9,33]{3,2,1,0:T(8,128)S(1)}, f32[3,1,9,33]{3,2,1,0:T(8,128)S(1)}, u32[]{:S(2)}, u32[]{:S(2)}) %collective-permute-start.23) | collective-permute-done | bytes 3596 | tf_op jit(solution)/shard_map/ppermute | solution.py:63
  299.0 7.8 %collective-permute-done.24 = f32[3,3,1,33]{3,2,1,0:T(1,128)S(1)} collective-permute-done((f32[3,3,1,33]{3,2,1,0:T(1,128)S(1)}, f32[3,3,1,33]{3,2,1,0:T(1,128)S(1)}, u32[]{:S(2)}, u32[]{:S(2)}) %collective-permute-start.24) | collective-permute-done | bytes 1220 | tf_op jit(solution)/shard_map/ppermute | solution.py:62
  313.7 4.3 %collective-permute-done.27 = f32[3,3,9,1]{3,2,1,0:T(8,128)S(1)} collective-permute-done((f32[3,3,9,1]{3,2,1,0:T(8,128)S(1)}, f32[3,3,9,1]{3,2,1,0:T(8,128)S(1)}, u32[]{:S(2)}, u32[]{:S(2)}) %collective-permute-start.27) | collective-permute-done | bytes 356 | tf_op jit(solution)/shard_map/ppermute | solution.py:63
  324.8 4.2 %collective-permute-done.29 = f32[3,1,9,33]{3,2,1,0:T(8,128)S(1)} collective-permute-done((f32[3,1,9,33]{3,2,1,0:T(8,128)S(1)}, f32[3,1,9,33]{3,2,1,0:T(8,128)S(1)}, u32[]{:S(2)}, u32[]{:S(2)}) %collective-permute-start.29) | collective-permute-done | bytes 3596 | tf_op jit(solution)/shard_map/ppermute | solution.py:63
  330.9 7.8 %collective-permute-done.30 = f32[3,3,1,33]{3,2,1,0:T(1,128)S(1)} collective-permute-done((f32[3,3,1,33]{3,2,1,0:T(1,128)S(1)}, f32[3,3,1,33]{3,2,1,0:T(1,128)S(1)}, u32[]{:S(2)}, u32[]{:S(2)}) %collective-permute-start.30) | collective-permute-done | bytes 1220 | tf_op jit(solution)/shard_map/ppermute | solution.py:62
  346.0 4.3 %collective-permute-done.33 = f32[3,3,9,1]{3,2,1,0:T(8,128)S(1)} collective-permute-done((f32[3,3,9,1]{3,2,1,0:T(8,128)S(1)}, f32[3,3,9,1]{3,2,1,0:T(8,128)S(1)}, u32[]{:S(2)}, u32[]{:S(2)}) %collective-permute-start.33) | collective-permute-done | bytes 356 | tf_op jit(solution)/shard_map/ppermute | solution.py:63
  357.1 4.2 %collective-permute-done.35 = f32[3,1,9,33]{3,2,1,0:T(8,128)S(1)} collective-permute-done((f32[3,1,9,33]{3,2,1,0:T(8,128)S(1)}, f32[3,1,9,33]{3,2,1,0:T(8,128)S(1)}, u32[]{:S(2)}, u32[]{:S(2)}) %collective-permute-start.35) | collective-permute-done | bytes 3596 | tf_op jit(solution)/shard_map/ppermute | solution.py:63
  363.3 7.8 %collective-permute-done.36 = f32[3,3,1,33]{3,2,1,0:T(1,128)S(1)} collective-permute-done((f32[3,3,1,33]{3,2,1,0:T(1,128)S(1)}, f32[3,3,1,33]{3,2,1,0:T(1,128)S(1)}, u32[]{:S(2)}, u32[]{:S(2)}) %collective-permute-start.36) | collective-permute-done | bytes 1220 | tf_op jit(solution)/shard_map/ppermute | solution.py:62
  378.3 4.3 %collective-permute-done.39 = f32[3,3,9,1]{3,2,1,0:T(8,128)S(1)} collective-permute-done((f32[3,3,9,1]{3,2,1,0:T(8,128)S(1)}, f32[3,3,9,1]{3,2,1,0:T(8,128)S(1)}, u32[]{:S(2)}, u32[]{:S(2)}) %collective-permute-start.39) | collective-permute-done | bytes 356 | tf_op jit(solution)/shard_map/ppermute | solution.py:63
  (271 shorter events, 121.2 us)
Async XLA Ops:
  6.1 5.7 %collective-permute-start = (f32[2,1024,8]{1,2,0:T(8,128)S(1)}, f32[2,1024,8]{1,2,0:T(8,128)S(1)}, u32[]{:S(2)}, u32[]{:S(2)}) collective-permute-start(f32[2,1024,8]{1,2,0:T(8,128)S(1)} %copy.40), channel_id=1, source_target_pairs={{0,4},{4,8},{8,12},{1,5},{5,9},{9,13},{2,6},{6,10},{10,14},{3,7},{... | collective-permute-start | bytes 196616 | tf_op jit(solution)/shard_map/ppermute | solution.py:50
  10.2 6.2 %collective-permute-start.1 = (f32[2,1024,8]{1,2,0:T(8,128)S(1)}, f32[2,1024,8]{1,2,0:T(8,128)S(1)}, u32[]{:S(2)}, u32[]{:S(2)}) collective-permute-start(f32[2,1024,8]{1,2,0:T(8,128)S(1)} %copy.41), channel_id=1, source_target_pairs={{4,0},{8,4},{12,8},{5,1},{9,5},{13,9},{6,2},{10,6},{14,10},{7,3},{... | collective-permute-start | bytes 196616 | tf_op jit(solution)/shard_map/ppermute | solution.py:51
  123.5 28.1 %collective-permute-start.2 = (f32[9,80,272]{2,1,0:T(8,128)S(1)}, f32[9,80,272]{2,1,0:T(8,128)S(1)}, u32[]{:S(2)}, u32[]{:S(2)}) collective-permute-start(f32[9,80,272]{2,1,0:T(8,128)S(1)} %pad_maximum_fusion.6), channel_id=1, source_target_pairs={{1,0},{2,1},{3,2},{5,4},{6,5},{7,6},{9,8},{10,9},{11,10},{13,12},{... | collective-permute-start | bytes 2350088 | tf_op jit(solution)/shard_map/ppermute | solution.py:173
  125.9 28.3 %collective-permute-start.3 = (f32[9,80,272]{2,1,0:T(8,128)}, f32[9,80,272]{2,1,0:T(8,128)S(1)}, u32[]{:S(2)}, u32[]{:S(2)}) collective-permute-start(f32[9,80,272]{2,1,0:T(8,128)} %pad_maximum_fusion.7), channel_id=1, source_target_pairs={{0,1},{1,2},{2,3},{4,5},{5,6},{6,7},{8,9},{9,10},{10,11},{12,13},{... | collective-permute-start | bytes 2350088 | tf_op jit(solution)/shard_map/ppermute | solution.py:172
  168.0 6.3 %collective-permute-start.4 = (f32[9,1,9,33]{3,2,1,0:T(8,128)S(1)}, f32[9,1,9,33]{3,2,1,0:T(8,128)S(1)}, u32[]{:S(2)}, u32[]{:S(2)}) collective-permute-start(f32[9,1,9,33]{3,2,1,0:T(8,128)S(1)} %fusion.61), channel_id=1, source_target_pairs={{0,1},{1,2},{2,3},{4,5},{5,6},{6,7},{8,9},{9,10},{10,11},{12,13},{... | collective-permute-start | bytes 32084 | tf_op jit(solution)/shard_map/ppermute | solution.py:62
  174.3 6.6 %collective-permute-start.5 = (f32[9,1,9,33]{3,2,1,0:T(8,128)S(1)}, f32[9,1,9,33]{3,2,1,0:T(8,128)S(1)}, u32[]{:S(2)}, u32[]{:S(2)}) collective-permute-start(f32[9,1,9,33]{3,2,1,0:T(8,128)S(1)} %get-tuple-element.42), channel_id=1, source_target_pairs={{1,0},{2,1},{3,2},{5,4},{6,5},{7,6},{9,8},{10,9},{11,10},{13,12},{... | collective-permute-start | bytes 32084 | tf_op jit(solution)/shard_map/ppermute | solution.py:63
  180.9 10.4 %collective-permute-start.6 = (f32[9,3,1,33]{3,2,1,0:T(1,128)S(1)}, f32[9,3,1,33]{3,2,1,0:T(1,128)S(1)}, u32[]{:S(2)}, u32[]{:S(2)}) collective-permute-start(f32[9,3,1,33]{3,2,1,0:T(1,128)S(1)} %get-tuple-element.118), channel_id=1, source_target_pairs={{0,16},{16,32},{32,48},{48,64},{64,80},{80,96},{96,112},{112,128},... | collective-permute-start | bytes 10700 | tf_op jit(solution)/shard_map/ppermute | solution.py:62
  182.9 9.9 %collective-permute-start.7 = (f32[9,3,1,33]{3,2,1,0:T(1,128)S(1)}, f32[9,3,1,33]{3,2,1,0:T(1,128)S(1)}, u32[]{:S(2)}, u32[]{:S(2)}) collective-permute-start(f32[9,3,1,33]{3,2,1,0:T(1,128)S(1)} %get-tuple-element.119), channel_id=1, source_target_pairs={{16,0},{32,16},{48,32},{64,48},{80,64},{96,80},{112,96},{128,112},... | collective-permute-start | bytes 10700 | tf_op jit(solution)/shard_map/ppermute | solution.py:63
  192.9 8.1 %collective-permute-start.8 = (f32[9,3,9,1]{3,2,1,0:T(8,128)S(1)}, f32[9,3,9,1]{3,2,1,0:T(8,128)S(1)}, u32[]{:S(2)}, u32[]{:S(2)}) collective-permute-start(f32[9,3,9,1]{3,2,1,0:T(8,128)S(1)} %get-tuple-element.114), channel_id=1, source_target_pairs={{0,4},{4,8},{8,12},{1,5},{5,9},{9,13},{2,6},{6,10},{10,14},{3,7},{... | collective-permute-start | bytes 2924 | tf_op jit(solution)/shard_map/ppermute | solution.py:62
  196.2 8.9 %collective-permute-start.9 = (f32[9,3,9,1]{3,2,1,0:T(8,128)S(1)}, f32[9,3,9,1]{3,2,1,0:T(8,128)S(1)}, u32[]{:S(2)}, u32[]{:S(2)}) collective-permute-start(f32[9,3,9,1]{3,2,1,0:T(8,128)S(1)} %get-tuple-element.115), channel_id=1, source_target_pairs={{4,0},{8,4},{12,8},{5,1},{9,5},{13,9},{6,2},{10,6},{14,10},{7,3},{... | collective-permute-start | bytes 2924 | tf_op jit(solution)/shard_map/ppermute | solution.py:63
  208.9 5.4 %collective-permute-start.10 = (f32[3,1,9,33]{3,2,1,0:T(8,128)S(1)}, f32[3,1,9,33]{3,2,1,0:T(8,128)S(1)}, u32[]{:S(2)}, u32[]{:S(2)}) collective-permute-start(f32[3,1,9,33]{3,2,1,0:T(8,128)S(1)} %get-tuple-element.164), channel_id=1, source_target_pairs={{0,1},{1,2},{2,3},{4,5},{5,6},{6,7},{8,9},{9,10},{10,11},{12,13},{... | collective-permute-start | bytes 10700 | tf_op jit(solution)/shard_map/ppermute | solution.py:62
  212.8 5.7 %collective-permute-start.11 = (f32[3,1,9,33]{3,2,1,0:T(8,128)S(1)}, f32[3,1,9,33]{3,2,1,0:T(8,128)S(1)}, u32[]{:S(2)}, u32[]{:S(2)}) collective-permute-start(f32[3,1,9,33]{3,2,1,0:T(8,128)S(1)} %get-tuple-element.165), channel_id=1, source_target_pairs={{1,0},{2,1},{3,2},{5,4},{6,5},{7,6},{9,8},{10,9},{11,10},{13,12},{... | collective-permute-start | bytes 10700 | tf_op jit(solution)/shard_map/ppermute | solution.py:63
  218.6 9.7 %collective-permute-start.12 = (f32[3,3,1,33]{3,2,1,0:T(1,128)S(1)}, f32[3,3,1,33]{3,2,1,0:T(1,128)S(1)}, u32[]{:S(2)}, u32[]{:S(2)}) collective-permute-start(f32[3,3,1,33]{3,2,1,0:T(1,128)S(1)} %pad_maximum_fusion.27), channel_id=1, source_target_pairs={{0,16},{16,32},{32,48},{48,64},{64,80},{80,96},{96,112},{112,128},... | collective-permute-start | bytes 3572 | tf_op jit(solution)/shard_map/ppermute | solution.py:62
  231.7 5.4 %collective-permute-start.14 = (f32[3,3,9,1]{3,2,1,0:T(8,128)S(1)}, f32[3,3,9,1]{3,2,1,0:T(8,128)S(1)}, u32[]{:S(2)}, u32[]{:S(2)}) collective-permute-start(f32[3,3,9,1]{3,2,1,0:T(8,128)S(1)} %get-tuple-element.159), channel_id=1, source_target_pairs={{0,4},{4,8},{8,12},{1,5},{5,9},{9,13},{2,6},{6,10},{10,14},{3,7},{... | collective-permute-start | bytes 980 | tf_op jit(solution)/shard_map/ppermute | solution.py:62
  235.1 6.2 %collective-permute-start.15 = (f32[3,3,9,1]{3,2,1,0:T(8,128)S(1)}, f32[3,3,9,1]{3,2,1,0:T(8,128)S(1)}, u32[]{:S(2)}, u32[]{:S(2)}) collective-permute-start(f32[3,3,9,1]{3,2,1,0:T(8,128)S(1)} %get-tuple-element.160), channel_id=1, source_target_pairs={{4,0},{8,4},{12,8},{5,1},{9,5},{13,9},{6,2},{10,6},{14,10},{7,3},{... | collective-permute-start | bytes 980 | tf_op jit(solution)/shard_map/ppermute | solution.py:63
  245.3 5.0 %collective-permute-start.16 = (f32[3,1,9,33]{3,2,1,0:T(8,128)S(1)}, f32[3,1,9,33]{3,2,1,0:T(8,128)S(1)}, u32[]{:S(2)}, u32[]{:S(2)}) collective-permute-start(f32[3,1,9,33]{3,2,1,0:T(8,128)S(1)} %get-tuple-element.155), channel_id=1, source_target_pairs={{0,1},{1,2},{2,3},{4,5},{5,6},{6,7},{8,9},{9,10},{10,11},{12,13},{... | collective-permute-start | bytes 10700 | tf_op jit(solution)/shard_map/ppermute | solution.py:62
  248.8 5.7 %collective-permute-start.17 = (f32[3,1,9,33]{3,2,1,0:T(8,128)S(1)}, f32[3,1,9,33]{3,2,1,0:T(8,128)S(1)}, u32[]{:S(2)}, u32[]{:S(2)}) collective-permute-start(f32[3,1,9,33]{3,2,1,0:T(8,128)S(1)} %get-tuple-element.156), channel_id=1, source_target_pairs={{1,0},{2,1},{3,2},{5,4},{6,5},{7,6},{9,8},{10,9},{11,10},{13,12},{... | collective-permute-start | bytes 10700 | tf_op jit(solution)/shard_map/ppermute | solution.py:63
  254.6 9.7 %collective-permute-start.18 = (f32[3,3,1,33]{3,2,1,0:T(1,128)S(1)}, f32[3,3,1,33]{3,2,1,0:T(1,128)S(1)}, u32[]{:S(2)}, u32[]{:S(2)}) collective-permute-start(f32[3,3,1,33]{3,2,1,0:T(1,128)S(1)} %pad_maximum_fusion.25), channel_id=1, source_target_pairs={{0,16},{16,32},{32,48},{48,64},{64,80},{80,96},{96,112},{112,128},... | collective-permute-start | bytes 3572 | tf_op jit(solution)/shard_map/ppermute | solution.py:62
  264.4 5.5 %collective-permute-start.19 = (f32[3,3,1,33]{3,2,1,0:T(1,128)S(1)}, f32[3,3,1,33]{3,2,1,0:T(1,128)S(1)}, u32[]{:S(2)}, u32[]{:S(2)}) collective-permute-start(f32[3,3,1,33]{3,2,1,0:T(1,128)S(1)} %get-tuple-element.29), channel_id=1, source_target_pairs={{16,0},{32,16},{48,32},{64,48},{80,64},{96,80},{112,96},{128,112},... | collective-permute-start | bytes 3572 | tf_op jit(solution)/shard_map/ppermute | solution.py:63
  271.5 4.7 %collective-permute-start.20 = (f32[3,3,9,1]{3,2,1,0:T(8,128)}, f32[3,3,9,1]{3,2,1,0:T(8,128)}, u32[]{:S(2)}, u32[]{:S(2)}) collective-permute-start(f32[3,3,9,1]{3,2,1,0:T(8,128)} %get-tuple-element.150), channel_id=1, source_target_pairs={{0,4},{4,8},{8,12},{1,5},{5,9},{9,13},{2,6},{6,10},{10,14},{3,7},{... | collective-permute-start | bytes 980 | tf_op jit(solution)/shard_map/ppermute | solution.py:62
  274.3 6.6 %collective-permute-start.21 = (f32[3,3,9,1]{3,2,1,0:T(8,128)}, f32[3,3,9,1]{3,2,1,0:T(8,128)}, u32[]{:S(2)}, u32[]{:S(2)}) collective-permute-start(f32[3,3,9,1]{3,2,1,0:T(8,128)} %get-tuple-element.151), channel_id=1, source_target_pairs={{4,0},{8,4},{12,8},{5,1},{9,5},{13,9},{6,2},{10,6},{14,10},{7,3},{... | collective-permute-start | bytes 980 | tf_op jit(solution)/shard_map/ppermute | solution.py:63
  291.3 5.7 %collective-permute-start.23 = (f32[3,1,9,33]{3,2,1,0:T(8,128)S(1)}, f32[3,1,9,33]{3,2,1,0:T(8,128)S(1)}, u32[]{:S(2)}, u32[]{:S(2)}) collective-permute-start(f32[3,1,9,33]{3,2,1,0:T(8,128)S(1)} %get-tuple-element.147), channel_id=1, source_target_pairs={{1,0},{2,1},{3,2},{5,4},{6,5},{7,6},{9,8},{10,9},{11,10},{13,12},{... | collective-permute-start | bytes 10700 | tf_op jit(solution)/shard_map/ppermute | solution.py:63
  297.1 9.8 %collective-permute-start.24 = (f32[3,3,1,33]{3,2,1,0:T(1,128)S(1)}, f32[3,3,1,33]{3,2,1,0:T(1,128)S(1)}, u32[]{:S(2)}, u32[]{:S(2)}) collective-permute-start(f32[3,3,1,33]{3,2,1,0:T(1,128)S(1)} %pad_maximum_fusion.23), channel_id=1, source_target_pairs={{0,16},{16,32},{32,48},{48,64},{64,80},{80,96},{96,112},{112,128},... | collective-permute-start | bytes 3572 | tf_op jit(solution)/shard_map/ppermute | solution.py:62
  311.7 6.2 %collective-permute-start.27 = (f32[3,3,9,1]{3,2,1,0:T(8,128)S(1)}, f32[3,3,9,1]{3,2,1,0:T(8,128)S(1)}, u32[]{:S(2)}, u32[]{:S(2)}) collective-permute-start(f32[3,3,9,1]{3,2,1,0:T(8,128)S(1)} %get-tuple-element.142), channel_id=1, source_target_pairs={{4,0},{8,4},{12,8},{5,1},{9,5},{13,9},{6,2},{10,6},{14,10},{7,3},{... | collective-permute-start | bytes 980 | tf_op jit(solution)/shard_map/ppermute | solution.py:63
  323.2 5.7 %collective-permute-start.29 = (f32[3,1,9,33]{3,2,1,0:T(8,128)S(1)}, f32[3,1,9,33]{3,2,1,0:T(8,128)S(1)}, u32[]{:S(2)}, u32[]{:S(2)}) collective-permute-start(f32[3,1,9,33]{3,2,1,0:T(8,128)S(1)} %get-tuple-element.138), channel_id=1, source_target_pairs={{1,0},{2,1},{3,2},{5,4},{6,5},{7,6},{9,8},{10,9},{11,10},{13,12},{... | collective-permute-start | bytes 10700 | tf_op jit(solution)/shard_map/ppermute | solution.py:63
  329.0 9.7 %collective-permute-start.30 = (f32[3,3,1,33]{3,2,1,0:T(1,128)S(1)}, f32[3,3,1,33]{3,2,1,0:T(1,128)S(1)}, u32[]{:S(2)}, u32[]{:S(2)}) collective-permute-start(f32[3,3,1,33]{3,2,1,0:T(1,128)S(1)} %pad_maximum_fusion.21), channel_id=1, source_target_pairs={{0,16},{16,32},{32,48},{48,64},{64,80},{80,96},{96,112},{112,128},... | collective-permute-start | bytes 3572 | tf_op jit(solution)/shard_map/ppermute | solution.py:62
  342.1 3.9 %collective-permute-start.32 = (f32[3,3,9,1]{3,2,1,0:T(8,128)S(1)}, f32[3,3,9,1]{3,2,1,0:T(8,128)S(1)}, u32[]{:S(2)}, u32[]{:S(2)}) collective-permute-start(f32[3,3,9,1]{3,2,1,0:T(8,128)S(1)} %get-tuple-element.132), channel_id=1, source_target_pairs={{0,4},{4,8},{8,12},{1,5},{5,9},{9,13},{2,6},{6,10},{10,14},{3,7},{... | collective-permute-start | bytes 980 | tf_op jit(solution)/shard_map/ppermute | solution.py:62
  344.0 6.2 %collective-permute-start.33 = (f32[3,3,9,1]{3,2,1,0:T(8,128)S(1)}, f32[3,3,9,1]{3,2,1,0:T(8,128)S(1)}, u32[]{:S(2)}, u32[]{:S(2)}) collective-permute-start(f32[3,3,9,1]{3,2,1,0:T(8,128)S(1)} %get-tuple-element.133), channel_id=1, source_target_pairs={{4,0},{8,4},{12,8},{5,1},{9,5},{13,9},{6,2},{10,6},{14,10},{7,3},{... | collective-permute-start | bytes 980 | tf_op jit(solution)/shard_map/ppermute | solution.py:63
  355.6 5.7 %collective-permute-start.35 = (f32[3,1,9,33]{3,2,1,0:T(8,128)S(1)}, f32[3,1,9,33]{3,2,1,0:T(8,128)S(1)}, u32[]{:S(2)}, u32[]{:S(2)}) collective-permute-start(f32[3,1,9,33]{3,2,1,0:T(8,128)S(1)} %get-tuple-element.129), channel_id=1, source_target_pairs={{1,0},{2,1},{3,2},{5,4},{6,5},{7,6},{9,8},{10,9},{11,10},{13,12},{... | collective-permute-start | bytes 10700 | tf_op jit(solution)/shard_map/ppermute | solution.py:63
  361.3 9.7 %collective-permute-start.36 = (f32[3,3,1,33]{3,2,1,0:T(1,128)S(1)}, f32[3,3,1,33]{3,2,1,0:T(1,128)S(1)}, u32[]{:S(2)}, u32[]{:S(2)}) collective-permute-start(f32[3,3,1,33]{3,2,1,0:T(1,128)S(1)} %pad_maximum_fusion.19), channel_id=1, source_target_pairs={{0,16},{16,32},{32,48},{48,64},{64,80},{80,96},{96,112},{112,128},... | collective-permute-start | bytes 3572 | tf_op jit(solution)/shard_map/ppermute | solution.py:62
  374.4 3.9 %collective-permute-start.38 = (f32[3,3,9,1]{3,2,1,0:T(8,128)S(1)}, f32[3,3,9,1]{3,2,1,0:T(8,128)S(1)}, u32[]{:S(2)}, u32[]{:S(2)}) collective-permute-start(f32[3,3,9,1]{3,2,1,0:T(8,128)S(1)} %get-tuple-element.123), channel_id=1, source_target_pairs={{0,4},{4,8},{8,12},{1,5},{5,9},{9,13},{2,6},{6,10},{10,14},{3,7},{... | collective-permute-start | bytes 980 | tf_op jit(solution)/shard_map/ppermute | solution.py:62
  376.4 6.2 %collective-permute-start.39 = (f32[3,3,9,1]{3,2,1,0:T(8,128)S(1)}, f32[3,3,9,1]{3,2,1,0:T(8,128)S(1)}, u32[]{:S(2)}, u32[]{:S(2)}) collective-permute-start(f32[3,3,9,1]{3,2,1,0:T(8,128)S(1)} %get-tuple-element.124), channel_id=1, source_target_pairs={{4,0},{8,4},{12,8},{5,1},{9,5},{13,9},{6,2},{10,6},{14,10},{7,3},{... | collective-permute-start | bytes 980 | tf_op jit(solution)/shard_map/ppermute | solution.py:63
  (33 other events, 214.5 us)

commit v3 on v2

--- a/solution.py
+++ b/solution.py
@@ -151,29 +151,22 @@
 
 
 def bricks_of(image_slab, deformed_slab):
-    both = jnp.concatenate([image_slab, deformed_slab], axis=0)
-    both = halo(both, "gy", 2, DMAX)
-    n_gx = lax.axis_size("gx")
-    fields, nx, ny = both.shape
-    bx = nx // n_gx
-    main = both.reshape(fields, n_gx, bx, ny)
-    zero = jnp.zeros((fields, 1, DMAX, ny), both.dtype)
-    low = jnp.concatenate([zero, main[:, :-1, bx - DMAX :]], axis=1)
-    high = jnp.concatenate([main[:, 1:, :DMAX], zero], axis=1)
-    windows = jnp.concatenate([low, main, high], axis=2)
-    windows = jnp.moveaxis(windows, 1, 0)
-    brick = lax.all_to_all(windows, "gx", split_axis=0, concat_axis=0, tiled=True)
+    image = lax.all_to_all(image_slab, "gx", split_axis=1, concat_axis=0, tiled=True)
+    deformed = lax.all_to_all(deformed_slab, "gx", split_axis=1, concat_axis=0, tiled=True)
+    both = jnp.stack([image, deformed])
+    both = halo(both, "gy", 3, DMAX)
+    both = halo(both, "gx", 2, DMAX)
     forward, backward = neighbours("gz")
-    bz = brick.shape[0]
-    image = brick[:, 0]
-    deformed = brick[:, 1]
+    bz, nx, ny = both.shape[1:]
+    image = both[0]
+    deformed = both[1]
     to_high = jnp.concatenate([deformed[bz - DMAX :], image[bz - 1 :]], axis=0)
     to_low = jnp.concatenate([deformed[:DMAX], image[:1]], axis=0)
     from_low = lax.ppermute(to_high, "gz", forward)
     from_high = lax.ppermute(to_low, "gz", backward)
     deformed_ext = jnp.concatenate([from_low[:DMAX], deformed, from_high[:DMAX]], axis=0)
     image_ext = jnp.concatenate([from_low[DMAX:], image, from_high[DMAX:]], axis=0)
-    image_ext = image_ext[:, DMAX - 1 : DMAX + bx + 1, DMAX - 1 : ny - DMAX + 1]
+    image_ext = image_ext[:, DMAX - 1 : nx - DMAX + 1, DMAX - 1 : ny - DMAX + 1]
     return image_ext, deformed_ext
 
 

time: 390 us -> 546 us (1.40); the launches traced: 387 us -> 536 us
  local copies, waits for them, and re-layouts: 19.9 us -> 131 us
  blocking collectives: 101 us -> 0 us
  other arithmetic: 28.9 us -> 84.1 us
  waiting for transfers between devices: 127 us -> 167 us
  starting transfers between devices: 89.1 us -> 125 us
  matrix products: 11.5 us -> 17.5 us
    all_to_all x1 -> x0, blocking collectives: 101 us -> none  [bricks_of(): lax.all_to_all(windows, 'gx', split_axis=0, concat_axis=0, tiled=True)]
    unnamed x55 -> x199, local copies, waits for them, and re-layouts: 6.55 us -> 60.4 us
    all_to_all x0 -> x2, waiting for transfers between devices: none -> 35.1 us  [the longest x1 18 us: bricks_of(): lax.all_to_all(deformed_slab, 'gx', split_axis=1, concat_axis=0, tiled=True)]
    slice x1 -> x18, local copies, waits for them, and re-layouts: 0.05 us -> 19.9 us  [the longest x6 8.43 us: expand_z(): high = values[:, 1:, None]]
    all_to_all x0 -> x2, starting transfers between devices: none -> 18.2 us  [the longest x1 11.4 us: bricks_of(): lax.all_to_all(deformed_slab, 'gx', split_axis=1, concat_axis=0, tiled=True)]
    reduce_sum x7, other arithmetic: 4.75 us -> 21.4 us  [reduce_z(): low = jnp.sum(blocks * lower.reshape(shape), axis=2)]
    ppermute x1 -> x2, starting transfers between devices: 3.83 us -> 18 us  [halo(): lax.ppermute(lax.slice_in_dim(block, size - width, size, axis=dim), axis,...]
    ppermute x1 -> x2, waiting for transfers between devices: 0.29 us -> 14.1 us  [halo(): lax.ppermute(lax.slice_in_dim(block, size - width, size, axis=dim), axis,...]
  transfers between devices with their start and end apart: 40 -> 44, of which waited for: 38 -> 41; matrix products, arithmetic and copies ran while one was open for 1% -> 3% of each run, Pallas kernels for 0% -> 0%
where the time goes in v3:
time: 546 us; the launch traced here: 536 us
  waiting for transfers between devices  167 us (31%)
  local copies, waits for them, and re-layouts  131 us (24%)
  starting transfers between devices  125 us (23%)
  other arithmetic  84.1 us (15%)
  matrix products  17.5 us (3%)
  between operations  10.5 us (2%)
    unnamed x199, local copies, waits for them, and re-layouts  60.4 us
    ppermute x18, waiting for transfers between devices, share(): from_high = lax.ppermute(first, axis, backward)  59.2 us
    ppermute x18, waiting for transfers between devices, share(): from_low = lax.ppermute(last, axis, forward)  47.2 us
    ppermute x18, starting transfers between devices, share(): from_low = lax.ppermute(last, axis, forward)  45.6 us
    ppermute x18, starting transfers between devices, share(): from_high = lax.ppermute(first, axis, backward)  34.2 us
    reduce_sum x7, other arithmetic, reduce_z(): low = jnp.sum(blocks * lower.reshape(shape), axis=2)  21.4 us
    all_to_all x1, waiting for transfers between devices, bricks_of(): lax.all_to_all(deformed_slab, 'gx', split_axis=1, concat_axis=0, tiled=True)  18 us
    ppermute x2, starting transfers between devices, halo(): lax.ppermute(lax.slice_in_dim(block, size - width, size, axis=dim), axis,...  18 us
  transfers between devices with their start and end apart: 44, of which 41 were waited for; matrix products, arithmetic and copies ran while one was open for 3% of the time, Pallas kernels for 0%

profile of v3, /device:TPU:4, one launch (start us, length us, event | category | flops | bytes accessed | tf_op | source)
XLA Modules:
  0.0 536.1 jit_solution(17858841931184547508)
XLA Ops:
  4.0 11.4 %all-to-all-start.1 = ((f32[1,1024,256]{2,0,1:T(1,128)}), f32[1,1024,256]{2,0,1:T(1,128)S(1)}, u32[]{:S(2)}, u32[]{:S(2)}) async-start(f32[1,1024,256]{2,0,1:T(1,128)} %copy.56), calls=%async_computation.1 | async-start | bytes 2097152 | tf_op jit(solution)/shard_map/all_to_all | solution.py:155
  17.5 18.0 %all-to-all-done.1 = f32[1,1024,256]{2,0,1:T(1,128)S(1)} async-done(((f32[1,1024,256]{2,0,1:T(1,128)}), f32[1,1024,256]{2,0,1:T(1,128)S(1)}, u32[]{:S(2)}, u32[]{:S(2)}) %all-to-all-start.1) | async-done | bytes 1048608 | tf_op jit(solution)/shard_map/all_to_all | solution.py:155
  35.6 6.8 %all-to-all-start = ((f32[1,1024,256]{2,0,1:T(1,128)}), f32[1,1024,256]{2,0,1:T(1,128)}, u32[]{:S(2)}, u32[]{:S(2)}) async-start(f32[1,1024,256]{2,0,1:T(1,128)} %copy.55), calls=%async_computation | async-start | bytes 2097152 | tf_op jit(solution)/shard_map/all_to_all | solution.py:154
  43.3 17.1 %all-to-all-done = f32[1,1024,256]{2,0,1:T(1,128)} async-done(((f32[1,1024,256]{2,0,1:T(1,128)}), f32[1,1024,256]{2,0,1:T(1,128)}, u32[]{:S(2)}, u32[]{:S(2)}) %all-to-all-start) | async-done | bytes 1048608 | tf_op jit(solution)/shard_map/all_to_all | solution.py:154
  66.7 15.6 %collective-permute-start = (f32[2,16,64,8]{2,3,1,0:T(8,128)S(1)}, f32[2,16,64,8]{2,3,1,0:T(8,128)S(1)}, u32[]{:S(2)}, u32[]{:S(2)}) collective-permute-start(f32[2,16,64,8]{2,3,1,0:T(8,128)S(1)} %get-tuple-element.59), channel_id=1, source_target_pairs={{0,4},{4,8},{8,12},{1,5},{5,9},{9,13},{2,6},{6,10},{10,14},{3,7},{... | collective-permute-start | bytes 196616 | tf_op jit(solution)/shard_map/ppermute | solution.py:50
  85.6 5.0 fusion.117
  105.1 13.0 %collective-permute-done.2 = f32[2,16,8,272]{3,2,1,0:T(8,128)} collective-permute-done((f32[2,16,8,272]{3,2,1,0:T(8,128)}, f32[2,16,8,272]{3,2,1,0:T(8,128)}, u32[]{:S(2)}, u32[]{:S(2)}) %collective-permute-start.2) | collective-permute-done | bytes 278560 | tf_op jit(solution)/shard_map/ppermute | solution.py:50
  121.8 6.1 %pad_maximum_fusion.2 = f32[2,16,80,272]{2,3,1,0:T(8,128)S(1)} fusion(f32[2,16,8,272]{2,3,1,0:T(8,128)} %copy.62, f32[2,16,64,8]{2,3,1,0:T(8,128)S(1)} %collective-permute-done.1, f32[1,16,64,256]{2,3,1,0:T(8,128)S(1)} %copy.58, f32[1,16,64,256]{2,3,1,0:T(8,128)} %copy.57, f32[2,16,64,8]{2,3,1,0:T(8,128)S(1)} %collective-permute-done, f32[2,16,8,272]{2,3,1,0:T(8,128)} %copy.61), kind=kLoop, calls=%fused_computation.24 | loop fusion | flops 3481600 | bytes 5570560 | tf_op jit(solution)/shard_map/concatenate | solution.py:52
  135.7 4.8 collective-permute-start.5
  145.5 4.7 slice_bitcast_fusion
  150.2 9.6 %collective-permute-done.4 = f32[9,80,272]{2,1,0:T(8,128)} collective-permute-done((f32[9,80,272]{2,1,0:T(8,128)}, f32[9,80,272]{2,1,0:T(8,128)}, u32[]{:S(2)}, u32[]{:S(2)}) %collective-permute-start.4) | collective-permute-done | bytes 783392 | tf_op jit(solution)/shard_map/ppermute | solution.py:166
  182.3 7.9 %multiply_reduce_fusion.1 = (f32[6,2,64,256]{2,3,1,0:T(8,128)S(1)}, f32[6,2,64,256]{2,3,1,0:T(8,128)S(1)}) fusion(f32[6,2,8,64,256]{3,4,2,1,0:T(8,128)} %constant_dynamic-update-slice_fusion, f32[8]{0:T(128)S(1)} %copy-done.74, f32[8]{0:T(128)S(1)} %copy-done.75), kind=kLoop, calls=%fused_computation.1 | loop fusion | flops 5898240 | bytes 7864384 | tf_op jit(solution)/shard_map/reduce_sum | solution.py:118
  226.9 4.4 collective-permute-start.6
  234.6 5.3 collective-permute-done.7
  241.9 8.4 %collective-permute-start.9 = (f32[9,3,1,33]{3,2,1,0:T(1,128)S(1)}, f32[9,3,1,33]{3,2,1,0:T(1,128)S(1)}, u32[]{:S(2)}, u32[]{:S(2)}) collective-permute-start(f32[9,3,1,33]{3,2,1,0:T(1,128)S(1)} %get-tuple-element.126), channel_id=1, source_target_pairs={{16,0},{32,16},{48,32},{64,48},{80,64},{96,80},{112,96},{128,112},... | collective-permute-start | bytes 10700 | tf_op jit(solution)/shard_map/ppermute | solution.py:63
  252.0 4.6 collective-permute-start.10
  260.8 4.7 collective-permute-done.11
  294.3 4.4 collective-permute-done.13
  300.8 7.8 %collective-permute-done.14 = f32[3,3,1,33]{3,2,1,0:T(1,128)S(1)} collective-permute-done((f32[3,3,1,33]{3,2,1,0:T(1,128)S(1)}, f32[3,3,1,33]{3,2,1,0:T(1,128)S(1)}, u32[]{:S(2)}, u32[]{:S(2)}) %collective-permute-start.14) | collective-permute-done | bytes 1220 | tf_op jit(solution)/shard_map/ppermute | solution.py:62
  317.6 4.3 collective-permute-done.17
  346.3 4.2 collective-permute-done.19
  352.4 7.8 %collective-permute-done.20 = f32[3,3,1,33]{3,2,1,0:T(1,128)S(1)} collective-permute-done((f32[3,3,1,33]{3,2,1,0:T(1,128)S(1)}, f32[3,3,1,33]{3,2,1,0:T(1,128)S(1)}, u32[]{:S(2)}, u32[]{:S(2)}) %collective-permute-start.20) | collective-permute-done | bytes 1220 | tf_op jit(solution)/shard_map/ppermute | solution.py:62
  369.9 4.1 collective-permute-done.23
  399.5 4.2 collective-permute-done.25
  405.7 7.8 %collective-permute-done.26 = f32[3,3,1,33]{3,2,1,0:T(1,128)S(1)} collective-permute-done((f32[3,3,1,33]{3,2,1,0:T(1,128)S(1)}, f32[3,3,1,33]{3,2,1,0:T(1,128)S(1)}, u32[]{:S(2)}, u32[]{:S(2)}) %collective-permute-start.26) | collective-permute-done | bytes 1220 | tf_op jit(solution)/shard_map/ppermute | solution.py:62
  421.0 4.3 collective-permute-done.29
  447.4 4.2 collective-permute-done.31
  453.5 7.8 %collective-permute-done.32 = f32[3,3,1,33]{3,2,1,0:T(1,128)S(1)} collective-permute-done((f32[3,3,1,33]{3,2,1,0:T(1,128)S(1)}, f32[3,3,1,33]{3,2,1,0:T(1,128)S(1)}, u32[]{:S(2)}, u32[]{:S(2)}) %collective-permute-start.32) | collective-permute-done | bytes 1220 | tf_op jit(solution)/shard_map/ppermute | solution.py:62
  468.6 4.3 collective-permute-done.35
  494.9 4.2 collective-permute-done.37
  501.1 7.8 %collective-permute-done.38 = f32[3,3,1,33]{3,2,1,0:T(1,128)S(1)} collective-permute-done((f32[3,3,1,33]{3,2,1,0:T(1,128)S(1)}, f32[3,3,1,33]{3,2,1,0:T(1,128)S(1)}, u32[]{:S(2)}, u32[]{:S(2)}) %collective-permute-start.38) | collective-permute-done | bytes 1220 | tf_op jit(solution)/shard_map/ppermute | solution.py:62
  516.2 4.3 collective-permute-done.41
  (447 shorter events, 296.6 us)
Async XLA Ops:
  4.0 31.6 %all-to-all-start.1 = ((f32[1,1024,256]{2,0,1:T(1,128)}), f32[1,1024,256]{2,0,1:T(1,128)S(1)}, u32[]{:S(2)}, u32[]{:S(2)}) async-start(f32[1,1024,256]{2,0,1:T(1,128)} %copy.56), calls=%async_computation.1 | async-start | bytes 2097152 | tf_op jit(solution)/shard_map/all_to_all | solution.py:155
  35.6 24.8 %all-to-all-start = ((f32[1,1024,256]{2,0,1:T(1,128)}), f32[1,1024,256]{2,0,1:T(1,128)}, u32[]{:S(2)}, u32[]{:S(2)}) async-start(f32[1,1024,256]{2,0,1:T(1,128)} %copy.55), calls=%async_computation | async-start | bytes 2097152 | tf_op jit(solution)/shard_map/all_to_all | solution.py:154
  65.4 18.7 %collective-permute-start.1 = (f32[2,16,64,8]{2,3,1,0:T(8,128)S(1)}, f32[2,16,64,8]{2,3,1,0:T(8,128)S(1)}, u32[]{:S(2)}, u32[]{:S(2)}) collective-permute-start(f32[2,16,64,8]{2,3,1,0:T(8,128)S(1)} %get-tuple-element.60), channel_id=1, source_target_pairs={{4,0},{8,4},{12,8},{5,1},{9,5},{13,9},{6,2},{10,6},{14,10},{7,3},{... | collective-permute-start | bytes 196616 | tf_op jit(solution)/shard_map/ppermute | solution.py:51
  66.7 18.6 %collective-permute-start = (f32[2,16,64,8]{2,3,1,0:T(8,128)S(1)}, f32[2,16,64,8]{2,3,1,0:T(8,128)S(1)}, u32[]{:S(2)}, u32[]{:S(2)}) collective-permute-start(f32[2,16,64,8]{2,3,1,0:T(8,128)S(1)} %get-tuple-element.59), channel_id=1, source_target_pairs={{0,4},{4,8},{8,12},{1,5},{5,9},{9,13},{2,6},{6,10},{10,14},{3,7},{... | collective-permute-start | bytes 196616 | tf_op jit(solution)/shard_map/ppermute | solution.py:50
  93.9 8.3 %collective-permute-start.3 = (f32[2,16,8,272]{3,2,1,0:T(8,128)S(1)}, f32[2,16,8,272]{3,2,1,0:T(8,128)S(1)}, u32[]{:S(2)}, u32[]{:S(2)}) collective-permute-start(f32[2,16,8,272]{3,2,1,0:T(8,128)S(1)} %copy.60), channel_id=1, source_target_pairs={{16,0},{32,16},{48,32},{64,48},{80,64},{96,80},{112,96},{128,112},... | collective-permute-start | bytes 835592 | tf_op jit(solution)/shard_map/ppermute | solution.py:51
  99.8 18.2 %collective-permute-start.2 = (f32[2,16,8,272]{3,2,1,0:T(8,128)}, f32[2,16,8,272]{3,2,1,0:T(8,128)}, u32[]{:S(2)}, u32[]{:S(2)}) collective-permute-start(f32[2,16,8,272]{3,2,1,0:T(8,128)} %copy.59), channel_id=1, source_target_pairs={{0,16},{16,32},{32,48},{48,64},{64,80},{80,96},{96,112},{112,128},... | collective-permute-start | bytes 835592 | tf_op jit(solution)/shard_map/ppermute | solution.py:50
  133.7 26.0 %collective-permute-start.4 = (f32[9,80,272]{2,1,0:T(8,128)}, f32[9,80,272]{2,1,0:T(8,128)}, u32[]{:S(2)}, u32[]{:S(2)}) collective-permute-start(f32[9,80,272]{2,1,0:T(8,128)} %copy.63), channel_id=1, source_target_pairs={{1,0},{2,1},{3,2},{5,4},{6,5},{7,6},{9,8},{10,9},{11,10},{13,12},{... | collective-permute-start | bytes 2350088 | tf_op jit(solution)/shard_map/ppermute | solution.py:166
  135.7 25.6 %collective-permute-start.5 = (f32[9,80,272]{2,1,0:T(8,128)S(1)}, f32[9,80,272]{2,1,0:T(8,128)S(1)}, u32[]{:S(2)}, u32[]{:S(2)}) collective-permute-start(f32[9,80,272]{2,1,0:T(8,128)S(1)} %copy.65), channel_id=1, source_target_pairs={{0,1},{1,2},{2,3},{4,5},{5,6},{6,7},{8,9},{9,10},{10,11},{12,13},{... | collective-permute-start | bytes 2350088 | tf_op jit(solution)/shard_map/ppermute | solution.py:165
  226.9 6.4 %collective-permute-start.6 = (f32[9,1,9,33]{3,2,1,0:T(8,128)S(1)}, f32[9,1,9,33]{3,2,1,0:T(8,128)S(1)}, u32[]{:S(2)}, u32[]{:S(2)}) collective-permute-start(f32[9,1,9,33]{3,2,1,0:T(8,128)S(1)} %fusion.60), channel_id=1, source_target_pairs={{0,1},{1,2},{2,3},{4,5},{5,6},{6,7},{8,9},{9,10},{10,11},{12,13},{... | collective-permute-start | bytes 32084 | tf_op jit(solution)/shard_map/ppermute | solution.py:62
  233.3 6.6 %collective-permute-start.7 = (f32[9,1,9,33]{3,2,1,0:T(8,128)S(1)}, f32[9,1,9,33]{3,2,1,0:T(8,128)S(1)}, u32[]{:S(2)}, u32[]{:S(2)}) collective-permute-start(f32[9,1,9,33]{3,2,1,0:T(8,128)S(1)} %get-tuple-element.42), channel_id=1, source_target_pairs={{1,0},{2,1},{3,2},{5,4},{6,5},{7,6},{9,8},{10,9},{11,10},{13,12},{... | collective-permute-start | bytes 32084 | tf_op jit(solution)/shard_map/ppermute | solution.py:63
  240.0 10.4 %collective-permute-start.8 = (f32[9,3,1,33]{3,2,1,0:T(1,128)S(1)}, f32[9,3,1,33]{3,2,1,0:T(1,128)S(1)}, u32[]{:S(2)}, u32[]{:S(2)}) collective-permute-start(f32[9,3,1,33]{3,2,1,0:T(1,128)S(1)} %get-tuple-element.125), channel_id=1, source_target_pairs={{0,16},{16,32},{32,48},{48,64},{64,80},{80,96},{96,112},{112,128},... | collective-permute-start | bytes 10700 | tf_op jit(solution)/shard_map/ppermute | solution.py:62
  241.9 9.9 %collective-permute-start.9 = (f32[9,3,1,33]{3,2,1,0:T(1,128)S(1)}, f32[9,3,1,33]{3,2,1,0:T(1,128)S(1)}, u32[]{:S(2)}, u32[]{:S(2)}) collective-permute-start(f32[9,3,1,33]{3,2,1,0:T(1,128)S(1)} %get-tuple-element.126), channel_id=1, source_target_pairs={{16,0},{32,16},{48,32},{64,48},{80,64},{96,80},{112,96},{128,112},... | collective-permute-start | bytes 10700 | tf_op jit(solution)/shard_map/ppermute | solution.py:63
  252.0 8.8 %collective-permute-start.10 = (f32[9,3,9,1]{3,2,1,0:T(8,128)S(1)}, f32[9,3,9,1]{3,2,1,0:T(8,128)S(1)}, u32[]{:S(2)}, u32[]{:S(2)}) collective-permute-start(f32[9,3,9,1]{3,2,1,0:T(8,128)S(1)} %get-tuple-element.121), channel_id=1, source_target_pairs={{0,4},{4,8},{8,12},{1,5},{5,9},{9,13},{2,6},{6,10},{10,14},{3,7},{... | collective-permute-start | bytes 2924 | tf_op jit(solution)/shard_map/ppermute | solution.py:62
  256.6 8.8 %collective-permute-start.11 = (f32[9,3,9,1]{3,2,1,0:T(8,128)S(1)}, f32[9,3,9,1]{3,2,1,0:T(8,128)S(1)}, u32[]{:S(2)}, u32[]{:S(2)}) collective-permute-start(f32[9,3,9,1]{3,2,1,0:T(8,128)S(1)} %get-tuple-element.122), channel_id=1, source_target_pairs={{4,0},{8,4},{12,8},{5,1},{9,5},{13,9},{6,2},{10,6},{14,10},{7,3},{... | collective-permute-start | bytes 2924 | tf_op jit(solution)/shard_map/ppermute | solution.py:63
  288.9 5.4 %collective-permute-start.12 = (f32[3,1,9,33]{3,2,1,0:T(8,128)S(1)}, f32[3,1,9,33]{3,2,1,0:T(8,128)S(1)}, u32[]{:S(2)}, u32[]{:S(2)}) collective-permute-start(f32[3,1,9,33]{3,2,1,0:T(8,128)S(1)} %get-tuple-element.171), channel_id=1, source_target_pairs={{0,1},{1,2},{2,3},{4,5},{5,6},{6,7},{8,9},{9,10},{10,11},{12,13},{... | collective-permute-start | bytes 10700 | tf_op jit(solution)/shard_map/ppermute | solution.py:62
  292.8 5.9 %collective-permute-start.13 = (f32[3,1,9,33]{3,2,1,0:T(8,128)S(1)}, f32[3,1,9,33]{3,2,1,0:T(8,128)S(1)}, u32[]{:S(2)}, u32[]{:S(2)}) collective-permute-start(f32[3,1,9,33]{3,2,1,0:T(8,128)S(1)} %get-tuple-element.172), channel_id=1, source_target_pairs={{1,0},{2,1},{3,2},{5,4},{6,5},{7,6},{9,8},{10,9},{11,10},{13,12},{... | collective-permute-start | bytes 10700 | tf_op jit(solution)/shard_map/ppermute | solution.py:63
  298.8 9.7 %collective-permute-start.14 = (f32[3,3,1,33]{3,2,1,0:T(1,128)S(1)}, f32[3,3,1,33]{3,2,1,0:T(1,128)S(1)}, u32[]{:S(2)}, u32[]{:S(2)}) collective-permute-start(f32[3,3,1,33]{3,2,1,0:T(1,128)S(1)} %pad_maximum_fusion.30), channel_id=1, source_target_pairs={{0,16},{16,32},{32,48},{48,64},{64,80},{80,96},{96,112},{112,128},... | collective-permute-start | bytes 3572 | tf_op jit(solution)/shard_map/ppermute | solution.py:62
  311.9 5.8 %collective-permute-start.16 = (f32[3,3,9,1]{3,2,1,0:T(8,128)S(1)}, f32[3,3,9,1]{3,2,1,0:T(8,128)S(1)}, u32[]{:S(2)}, u32[]{:S(2)}) collective-permute-start(f32[3,3,9,1]{3,2,1,0:T(8,128)S(1)} %get-tuple-element.166), channel_id=1, source_target_pairs={{0,4},{4,8},{8,12},{1,5},{5,9},{9,13},{2,6},{6,10},{10,14},{3,7},{... | collective-permute-start | bytes 980 | tf_op jit(solution)/shard_map/ppermute | solution.py:62
  315.7 6.2 %collective-permute-start.17 = (f32[3,3,9,1]{3,2,1,0:T(8,128)S(1)}, f32[3,3,9,1]{3,2,1,0:T(8,128)S(1)}, u32[]{:S(2)}, u32[]{:S(2)}) collective-permute-start(f32[3,3,9,1]{3,2,1,0:T(8,128)S(1)} %get-tuple-element.167), channel_id=1, source_target_pairs={{4,0},{8,4},{12,8},{5,1},{9,5},{13,9},{6,2},{10,6},{14,10},{7,3},{... | collective-permute-start | bytes 980 | tf_op jit(solution)/shard_map/ppermute | solution.py:63
  344.8 5.7 %collective-permute-start.19 = (f32[3,1,9,33]{3,2,1,0:T(8,128)S(1)}, f32[3,1,9,33]{3,2,1,0:T(8,128)S(1)}, u32[]{:S(2)}, u32[]{:S(2)}) collective-permute-start(f32[3,1,9,33]{3,2,1,0:T(8,128)S(1)} %get-tuple-element.163), channel_id=1, source_target_pairs={{1,0},{2,1},{3,2},{5,4},{6,5},{7,6},{9,8},{10,9},{11,10},{13,12},{... | collective-permute-start | bytes 10700 | tf_op jit(solution)/shard_map/ppermute | solution.py:63
  350.5 9.7 %collective-permute-start.20 = (f32[3,3,1,33]{3,2,1,0:T(1,128)S(1)}, f32[3,3,1,33]{3,2,1,0:T(1,128)S(1)}, u32[]{:S(2)}, u32[]{:S(2)}) collective-permute-start(f32[3,3,1,33]{3,2,1,0:T(1,128)S(1)} %pad_maximum_fusion.28), channel_id=1, source_target_pairs={{0,16},{16,32},{32,48},{48,64},{64,80},{80,96},{96,112},{112,128},... | collective-permute-start | bytes 3572 | tf_op jit(solution)/shard_map/ppermute | solution.py:62
  360.3 5.4 %collective-permute-start.21 = (f32[3,3,1,33]{3,2,1,0:T(1,128)S(1)}, f32[3,3,1,33]{3,2,1,0:T(1,128)S(1)}, u32[]{:S(2)}, u32[]{:S(2)}) collective-permute-start(f32[3,3,1,33]{3,2,1,0:T(1,128)S(1)} %get-tuple-element.29), channel_id=1, source_target_pairs={{16,0},{32,16},{48,32},{64,48},{80,64},{96,80},{112,96},{128,112},... | collective-permute-start | bytes 3572 | tf_op jit(solution)/shard_map/ppermute | solution.py:63
  367.8 6.3 %collective-permute-start.23 = (f32[3,3,9,1]{3,2,1,0:T(8,128)S(1)}, f32[3,3,9,1]{3,2,1,0:T(8,128)S(1)}, u32[]{:S(2)}, u32[]{:S(2)}) collective-permute-start(f32[3,3,9,1]{3,2,1,0:T(8,128)S(1)} %get-tuple-element.158), channel_id=1, source_target_pairs={{4,0},{8,4},{12,8},{5,1},{9,5},{13,9},{6,2},{10,6},{14,10},{7,3},{... | collective-permute-start | bytes 980 | tf_op jit(solution)/shard_map/ppermute | solution.py:63
  398.0 5.7 %collective-permute-start.25 = (f32[3,1,9,33]{3,2,1,0:T(8,128)S(1)}, f32[3,1,9,33]{3,2,1,0:T(8,128)S(1)}, u32[]{:S(2)}, u32[]{:S(2)}) collective-permute-start(f32[3,1,9,33]{3,2,1,0:T(8,128)S(1)} %get-tuple-element.154), channel_id=1, source_target_pairs={{1,0},{2,1},{3,2},{5,4},{6,5},{7,6},{9,8},{10,9},{11,10},{13,12},{... | collective-permute-start | bytes 10700 | tf_op jit(solution)/shard_map/ppermute | solution.py:63
  403.8 9.7 %collective-permute-start.26 = (f32[3,3,1,33]{3,2,1,0:T(1,128)S(1)}, f32[3,3,1,33]{3,2,1,0:T(1,128)S(1)}, u32[]{:S(2)}, u32[]{:S(2)}) collective-permute-start(f32[3,3,1,33]{3,2,1,0:T(1,128)S(1)} %pad_maximum_fusion.26), channel_id=1, source_target_pairs={{0,16},{16,32},{32,48},{48,64},{64,80},{80,96},{96,112},{112,128},... | collective-permute-start | bytes 3572 | tf_op jit(solution)/shard_map/ppermute | solution.py:62
  419.1 6.2 %collective-permute-start.29 = (f32[3,3,9,1]{3,2,1,0:T(8,128)S(1)}, f32[3,3,9,1]{3,2,1,0:T(8,128)S(1)}, u32[]{:S(2)}, u32[]{:S(2)}) collective-permute-start(f32[3,3,9,1]{3,2,1,0:T(8,128)S(1)} %get-tuple-element.149), channel_id=1, source_target_pairs={{4,0},{8,4},{12,8},{5,1},{9,5},{13,9},{6,2},{10,6},{14,10},{7,3},{... | collective-permute-start | bytes 980 | tf_op jit(solution)/shard_map/ppermute | solution.py:63
  445.8 5.7 %collective-permute-start.31 = (f32[3,1,9,33]{3,2,1,0:T(8,128)S(1)}, f32[3,1,9,33]{3,2,1,0:T(8,128)S(1)}, u32[]{:S(2)}, u32[]{:S(2)}) collective-permute-start(f32[3,1,9,33]{3,2,1,0:T(8,128)S(1)} %get-tuple-element.145), channel_id=1, source_target_pairs={{1,0},{2,1},{3,2},{5,4},{6,5},{7,6},{9,8},{10,9},{11,10},{13,12},{... | collective-permute-start | bytes 10700 | tf_op jit(solution)/shard_map/ppermute | solution.py:63
  451.6 9.7 %collective-permute-start.32 = (f32[3,3,1,33]{3,2,1,0:T(1,128)S(1)}, f32[3,3,1,33]{3,2,1,0:T(1,128)S(1)}, u32[]{:S(2)}, u32[]{:S(2)}) collective-permute-start(f32[3,3,1,33]{3,2,1,0:T(1,128)S(1)} %pad_maximum_fusion.24), channel_id=1, source_target_pairs={{0,16},{16,32},{32,48},{48,64},{64,80},{80,96},{96,112},{112,128},... | collective-permute-start | bytes 3572 | tf_op jit(solution)/shard_map/ppermute | solution.py:62
  466.6 6.2 %collective-permute-start.35 = (f32[3,3,9,1]{3,2,1,0:T(8,128)S(1)}, f32[3,3,9,1]{3,2,1,0:T(8,128)S(1)}, u32[]{:S(2)}, u32[]{:S(2)}) collective-permute-start(f32[3,3,9,1]{3,2,1,0:T(8,128)S(1)} %get-tuple-element.140), channel_id=1, source_target_pairs={{4,0},{8,4},{12,8},{5,1},{9,5},{13,9},{6,2},{10,6},{14,10},{7,3},{... | collective-permute-start | bytes 980 | tf_op jit(solution)/shard_map/ppermute | solution.py:63
  493.4 5.7 %collective-permute-start.37 = (f32[3,1,9,33]{3,2,1,0:T(8,128)S(1)}, f32[3,1,9,33]{3,2,1,0:T(8,128)S(1)}, u32[]{:S(2)}, u32[]{:S(2)}) collective-permute-start(f32[3,1,9,33]{3,2,1,0:T(8,128)S(1)} %get-tuple-element.136), channel_id=1, source_target_pairs={{1,0},{2,1},{3,2},{5,4},{6,5},{7,6},{9,8},{10,9},{11,10},{13,12},{... | collective-permute-start | bytes 10700 | tf_op jit(solution)/shard_map/ppermute | solution.py:63
  499.2 9.7 %collective-permute-start.38 = (f32[3,3,1,33]{3,2,1,0:T(1,128)S(1)}, f32[3,3,1,33]{3,2,1,0:T(1,128)S(1)}, u32[]{:S(2)}, u32[]{:S(2)}) collective-permute-start(f32[3,3,1,33]{3,2,1,0:T(1,128)S(1)} %pad_maximum_fusion.22), channel_id=1, source_target_pairs={{0,16},{16,32},{32,48},{48,64},{64,80},{80,96},{96,112},{112,128},... | collective-permute-start | bytes 3572 | tf_op jit(solution)/shard_map/ppermute | solution.py:62
  514.2 6.2 %collective-permute-start.41 = (f32[3,3,9,1]{3,2,1,0:T(8,128)S(1)}, f32[3,3,9,1]{3,2,1,0:T(8,128)S(1)}, u32[]{:S(2)}, u32[]{:S(2)}) collective-permute-start(f32[3,3,9,1]{3,2,1,0:T(8,128)S(1)} %get-tuple-element.131), channel_id=1, source_target_pairs={{4,0},{8,4},{12,8},{5,1},{9,5},{13,9},{6,2},{10,6},{14,10},{7,3},{... | collective-permute-start | bytes 980 | tf_op jit(solution)/shard_map/ppermute | solution.py:63
  (90 other events, 905.1 us)

commit v4 on v1

--- a/solution.py
+++ b/solution.py
@@ -214,9 +214,12 @@
             resid = residual(interpolate(nodal, tables, weights), warped, offset)
             rhs = share(restrict(grads * resid[None], tables, weights))
         delta = DAMPING * apply_inverse(inverse, rhs)
-        for sweep in range(SWEEPS - 1):
+
+        def sweep(_, delta, rhs=rhs):
             applied = operator(delta) + REGULARIZE * delta
-            delta = delta + DAMPING * apply_inverse(inverse, rhs - applied)
+            return delta + DAMPING * apply_inverse(inverse, rhs - applied)
+
+        delta = lax.fori_loop(0, SWEEPS - 1, sweep, delta)
         nodal = nodal + delta
     final = residual(interpolate(nodal, tables, weights), warped, offset)
     return (nodal, final)

time: 387 us -> 443 us (1.14)
  local copies, waits for them, and re-layouts: 21.7 us -> 48.1 us
  other arithmetic: 26.7 us -> 48.7 us
  matrix products: 11.5 us -> 20.9 us
  waiting for transfers between devices: 204 us -> 197 us
  starting transfers between devices: 111 us -> 116 us
    mul x0 -> x24, local copies, waits for them, and re-layouts: none -> 22 us  [expand_z(): joined = low * lower.reshape(shape) + high * upper.reshape(shape)]
    add x0 -> x4, other arithmetic: none -> 6.12 us  [sweep(): return delta + DAMPING * apply_inverse(inverse, rhs - applied)]
    ppermute x3, waiting for transfers between devices: 7.7 us -> 2.5 us  [halo(): lax.ppermute(lax.slice_in_dim(block, 0, width, axis=dim), axis, backward)]
    dot_general x6, matrix products: 2.32 us -> 7.04 us  [interp_xy(): step = jnp.einsum('cabd,yd->caby', nodal, table_y, precision=HI)]
    dot_general x7, matrix products: 1.97 us -> 6.66 us  [restrict(): return jnp.einsum('caby,yd->cabd', step, table_y, precision=HI)]
where the time goes in v4:
time: 443 us; the launch traced here: 440 us
  waiting for transfers between devices  197 us (44%)
  starting transfers between devices  116 us (26%)
  other arithmetic  48.7 us (11%)
  local copies, waits for them, and re-layouts  48.1 us (11%)
  matrix products  20.9 us (5%)
  between operations  9.33 us (2%)
    all_to_all x1, waiting for transfers between devices, bricks_of(): lax.all_to_all(windows, 'gx', split_axis=0, concat_axis=0, tiled=True)  86.3 us
    ppermute x18, waiting for transfers between devices, share(): from_high = lax.ppermute(first, axis, backward)  59.3 us
    ppermute x18, starting transfers between devices, share(): from_low = lax.ppermute(last, axis, forward)  52.3 us
    ppermute x18, waiting for transfers between devices, share(): from_low = lax.ppermute(last, axis, forward)  46.5 us
    ppermute x18, starting transfers between devices, share(): from_high = lax.ppermute(first, axis, backward)  34 us
    mul x24, local copies, waits for them, and re-layouts, expand_z(): joined = low * lower.reshape(shape) + high * upper.reshape(shape)  22 us
    ppermute x3, starting transfers between devices, halo(): lax.ppermute(lax.slice_in_dim(block, size - width, size, axis=dim), axis,...  13.9 us
    all_to_all x1, starting transfers between devices, bricks_of(): lax.all_to_all(windows, 'gx', split_axis=0, concat_axis=0, tiled=True)  11.6 us
  transfers between devices with their start and end apart: 43, of which 39 were waited for; matrix products, arithmetic and copies ran while one was open for 3% of the time, Pallas kernels for 0%

profile of v4, /device:TPU:4, one launch (start us, length us, event | category | flops | bytes accessed | tf_op | source)
XLA Modules:
  0.0 440.2 jit_solution(10132434952308955076)
XLA Ops:
  7.9 4.6 %collective-permute-start.12 = (f32[2,1024,8]{1,2,0:T(8,128)S(1)}, f32[2,1024,8]{1,2,0:T(8,128)S(1)}, u32[]{:S(2)}, u32[]{:S(2)}) collective-permute-start(f32[2,1024,8]{1,2,0:T(8,128)S(1)} %copy.39), channel_id=1, source_target_pairs={{0,4},{4,8},{8,12},{1,5},{5,9},{9,13},{2,6},{6,10},{10,14},{3,7},{... | collective-permute-start | bytes 196616 | tf_op jit(solution)/shard_map/ppermute | solution.py:50
  15.7 3.3 pad_maximum_fusion.5
  21.7 11.6 %all-to-all-start = ((f32[16,2,80,272]{3,2,1,0:T(8,128)}), f32[16,2,80,272]{3,2,1,0:T(8,128)}, u32[]{:S(2)}, u32[]{:S(2)}) async-start(f32[16,2,80,272]{3,2,1,0:T(8,128)} %copy.43), calls=%async_computation | async-start | bytes 7864320 | tf_op jit(solution)/shard_map/all_to_all | solution.py:165
  38.4 86.3 %all-to-all-done = f32[16,2,80,272]{3,2,1,0:T(8,128)} async-done(((f32[16,2,80,272]{3,2,1,0:T(8,128)}), f32[16,2,80,272]{3,2,1,0:T(8,128)}, u32[]{:S(2)}, u32[]{:S(2)}) %all-to-all-start) | async-done | bytes 2785312 | tf_op jit(solution)/shard_map/all_to_all | solution.py:165
  128.6 4.6 %collective-permute-start.15 = (f32[1,66,258]{2,1,0:T(8,128)S(1)}, f32[1,66,258]{2,1,0:T(8,128)S(1)}, u32[]{:S(2)}, u32[]{:S(2)}) collective-permute-start(f32[1,66,258]{2,1,0:T(8,128)S(1)} %get-tuple-element.317), channel_id=1, source_target_pairs={{0,1},{1,2},{2,3},{4,5},{5,6},{6,7},{8,9},{9,10},{10,11},{12,13},{... | collective-permute-start | bytes 204344 | tf_op jit(solution)/shard_map/ppermute | solution.py:50
  136.7 4.8 %collective-permute-start.16 = (f32[8,80,272]{2,1,0:T(8,128)S(1)}, f32[8,80,272]{2,1,0:T(8,128)S(1)}, u32[]{:S(2)}, u32[]{:S(2)}) collective-permute-start(f32[8,80,272]{2,1,0:T(8,128)S(1)} %get-tuple-element.304), channel_id=1, source_target_pairs={{0,1},{1,2},{2,3},{4,5},{5,6},{6,7},{8,9},{9,10},{10,11},{12,13},{... | collective-permute-start | bytes 2088968 | tf_op jit(solution)/shard_map/ppermute | solution.py:50
  148.9 2.5 collective-permute-done.17
  156.6 4.4 collective-permute-start.18
  164.3 5.3 %collective-permute-done.19 = f32[9,1,9,33]{3,2,1,0:T(8,128)S(1)} collective-permute-done((f32[9,1,9,33]{3,2,1,0:T(8,128)S(1)}, f32[9,1,9,33]{3,2,1,0:T(8,128)S(1)}, u32[]{:S(2)}, u32[]{:S(2)}) %collective-permute-start.19) | collective-permute-done | bytes 10724 | tf_op jit(solution)/shard_map/ppermute | solution.py:63
  171.6 8.4 %collective-permute-start.21 = (f32[9,3,1,33]{3,2,1,0:T(1,128)S(1)}, f32[9,3,1,33]{3,2,1,0:T(1,128)}, u32[]{:S(2)}, u32[]{:S(2)}) collective-permute-start(f32[9,3,1,33]{3,2,1,0:T(1,128)S(1)} %get-tuple-element.345), channel_id=1, source_target_pairs={{16,0},{32,16},{48,32},{64,48},{80,64},{96,80},{112,96},{128,112},... | collective-permute-start | bytes 10700 | tf_op jit(solution)/shard_map/ppermute | solution.py:63
  183.1 12.8 %collective-permute-start.22 = (f32[9,3,9,1]{3,2,1,0:T(8,128)}, f32[9,3,9,1]{3,2,1,0:T(8,128)}, u32[]{:S(2)}, u32[]{:S(2)}) collective-permute-start(f32[9,3,9,1]{3,2,1,0:T(8,128)} %get-tuple-element.340), channel_id=1, source_target_pairs={{0,4},{4,8},{8,12},{1,5},{5,9},{9,13},{2,6},{6,10},{10,14},{3,7},{... | collective-permute-start | bytes 2924 | tf_op jit(solution)/shard_map/ppermute | solution.py:62
  200.6 4.8 %collective-permute-done.23 = f32[9,3,9,1]{3,2,1,0:T(8,128)} collective-permute-done((f32[9,3,9,1]{3,2,1,0:T(8,128)}, f32[9,3,9,1]{3,2,1,0:T(8,128)}, u32[]{:S(2)}, u32[]{:S(2)}) %collective-permute-start.23) | collective-permute-done | bytes 1004 | tf_op jit(solution)/shard_map/ppermute | solution.py:63
  207.9 94.8 %while.24 = (s32[]{:T(128)}, f32[3,3,9,33]{3,2,1,0:T(8,128)}, f32[6,3,9,33]{3,2,1,0:T(8,128)}, f32[3,16,64,256]{3,2,1,0:T(8,128)S(1)}, f32[3,3,9,33]{3,2,1,0:T(8...) while((s32[]{:T(128)}, f32[3,3,9,33]{3,2,1,0:T(8,128)}, ...), condition=%wide.region_9.0_spmd.clone.clone, body=%wide.region_5.0_spmd.sunk.clone.clone.sunk | while | flops 56090916 | bytes 27506188 | solution.py:222
  219.7 3.9 collective-permute-start
  225.1 4.2 collective-permute-done.1
  231.3 7.8 %collective-permute-done.2 = f32[3,3,1,33]{3,2,1,0:T(1,128)S(1)} collective-permute-done((f32[3,3,1,33]{3,2,1,0:T(1,128)S(1)}, f32[3,3,1,33]{3,2,1,0:T(1,128)S(1)}, u32[]{:S(2)}, u32[]{:S(2)}) %collective-permute-start.2) | collective-permute-done | bytes 1220 | tf_op jit(solution)/shard_map/while/body/eval_jaxpr/ppermute | solution.py:62
  247.9 4.3 collective-permute-done.5
  267.4 3.5 collective-permute-start
  272.4 4.2 collective-permute-done.1
  278.6 7.8 %collective-permute-done.2 = f32[3,3,1,33]{3,2,1,0:T(1,128)S(1)} collective-permute-done((f32[3,3,1,33]{3,2,1,0:T(1,128)S(1)}, f32[3,3,1,33]{3,2,1,0:T(1,128)S(1)}, u32[]{:S(2)}, u32[]{:S(2)}) %collective-permute-start.2) | collective-permute-done | bytes 1220 | tf_op jit(solution)/shard_map/while/body/eval_jaxpr/ppermute | solution.py:62
  294.9 4.3 collective-permute-done.5
  315.0 4.2 collective-permute-done.25
  321.2 7.8 %collective-permute-done.26 = f32[3,3,1,33]{3,2,1,0:T(1,128)S(1)} collective-permute-done((f32[3,3,1,33]{3,2,1,0:T(1,128)S(1)}, f32[3,3,1,33]{3,2,1,0:T(1,128)S(1)}, u32[]{:S(2)}, u32[]{:S(2)}) %collective-permute-start.26) | collective-permute-done | bytes 1220 | tf_op jit(solution)/shard_map/ppermute | solution.py:62
  336.2 4.3 collective-permute-done.29
  341.4 90.4 %while.25 = (s32[]{:T(128)}, f32[3,3,9,33]{3,2,1,0:T(8,128)}, f32[6,3,9,33]{3,2,1,0:T(8,128)}, f32[3,16,64,256]{3,2,1,0:T(8,128)S(1)}, f32[3,3,9,33]{3,2,1,0:T(8...) while((s32[]{:T(128)}, f32[3,3,9,33]{3,2,1,0:T(8,128)}, ...), condition=%wide.region_17.0_spmd.clone.clone, body=%wide.region_13.0_spmd.sunk.clone.clone.sunk | while | flops 56090916 | bytes 27506188 | solution.py:222
  356.6 4.2 collective-permute-done.7
  362.8 7.8 %collective-permute-done.8 = f32[3,3,1,33]{3,2,1,0:T(1,128)S(1)} collective-permute-done((f32[3,3,1,33]{3,2,1,0:T(1,128)S(1)}, f32[3,3,1,33]{3,2,1,0:T(1,128)S(1)}, u32[]{:S(2)}, u32[]{:S(2)}) %collective-permute-start.8) | collective-permute-done | bytes 1220 | tf_op jit(solution)/shard_map/while/body/eval_jaxpr/ppermute | solution.py:62
  378.8 4.3 collective-permute-done.11
  401.8 4.2 collective-permute-done.7
  408.0 7.8 %collective-permute-done.8 = f32[3,3,1,33]{3,2,1,0:T(1,128)S(1)} collective-permute-done((f32[3,3,1,33]{3,2,1,0:T(1,128)S(1)}, f32[3,3,1,33]{3,2,1,0:T(1,128)S(1)}, u32[]{:S(2)}, u32[]{:S(2)}) %collective-permute-start.8) | collective-permute-done | bytes 1220 | tf_op jit(solution)/shard_map/while/body/eval_jaxpr/ppermute | solution.py:62
  424.0 4.3 collective-permute-done.11
  437.0 3.2 bitcast_subtract_fusion
  (338 shorter events, 184.5 us)
Async XLA Ops:
  6.3 6.2 %collective-permute-start.13 = (f32[2,1024,8]{1,2,0:T(8,128)S(1)}, f32[2,1024,8]{1,2,0:T(8,128)S(1)}, u32[]{:S(2)}, u32[]{:S(2)}) collective-permute-start(f32[2,1024,8]{1,2,0:T(8,128)S(1)} %copy.40), channel_id=1, source_target_pairs={{4,0},{8,4},{12,8},{5,1},{9,5},{13,9},{6,2},{10,6},{14,10},{7,3},{... | collective-permute-start | bytes 196616 | tf_op jit(solution)/shard_map/ppermute | solution.py:51
  7.9 6.4 %collective-permute-start.12 = (f32[2,1024,8]{1,2,0:T(8,128)S(1)}, f32[2,1024,8]{1,2,0:T(8,128)S(1)}, u32[]{:S(2)}, u32[]{:S(2)}) collective-permute-start(f32[2,1024,8]{1,2,0:T(8,128)S(1)} %copy.39), channel_id=1, source_target_pairs={{0,4},{4,8},{8,12},{1,5},{5,9},{9,13},{2,6},{6,10},{10,14},{3,7},{... | collective-permute-start | bytes 196616 | tf_op jit(solution)/shard_map/ppermute | solution.py:50
  21.7 103.0 %all-to-all-start = ((f32[16,2,80,272]{3,2,1,0:T(8,128)}), f32[16,2,80,272]{3,2,1,0:T(8,128)}, u32[]{:S(2)}, u32[]{:S(2)}) async-start(f32[16,2,80,272]{3,2,1,0:T(8,128)} %copy.43), calls=%async_computation | async-start | bytes 7864320 | tf_op jit(solution)/shard_map/all_to_all | solution.py:165
  127.3 14.2 %collective-permute-start.14 = (f32[1,66,258]{2,1,0:T(8,128)S(1)}, f32[1,66,258]{2,1,0:T(8,128)S(1)}, u32[]{:S(2)}, u32[]{:S(2)}) collective-permute-start(f32[1,66,258]{2,1,0:T(8,128)S(1)} %get-tuple-element.318), channel_id=1, source_target_pairs={{1,0},{2,1},{3,2},{5,4},{6,5},{7,6},{9,8},{10,9},{11,10},{13,12},{... | collective-permute-start | bytes 204344 | tf_op jit(solution)/shard_map/ppermute | solution.py:51
  128.6 12.9 %collective-permute-start.15 = (f32[1,66,258]{2,1,0:T(8,128)S(1)}, f32[1,66,258]{2,1,0:T(8,128)S(1)}, u32[]{:S(2)}, u32[]{:S(2)}) collective-permute-start(f32[1,66,258]{2,1,0:T(8,128)S(1)} %get-tuple-element.317), channel_id=1, source_target_pairs={{0,1},{1,2},{2,3},{4,5},{5,6},{6,7},{8,9},{9,10},{10,11},{12,13},{... | collective-permute-start | bytes 204344 | tf_op jit(solution)/shard_map/ppermute | solution.py:50
  135.4 16.0 %collective-permute-start.17 = (f32[8,80,272]{2,1,0:T(8,128)S(1)}, f32[8,80,272]{2,1,0:T(8,128)S(1)}, u32[]{:S(2)}, u32[]{:S(2)}) collective-permute-start(f32[8,80,272]{2,1,0:T(8,128)S(1)} %get-tuple-element.305), channel_id=1, source_target_pairs={{1,0},{2,1},{3,2},{5,4},{6,5},{7,6},{9,8},{10,9},{11,10},{13,12},{... | collective-permute-start | bytes 2088968 | tf_op jit(solution)/shard_map/ppermute | solution.py:51
  136.7 16.2 %collective-permute-start.16 = (f32[8,80,272]{2,1,0:T(8,128)S(1)}, f32[8,80,272]{2,1,0:T(8,128)S(1)}, u32[]{:S(2)}, u32[]{:S(2)}) collective-permute-start(f32[8,80,272]{2,1,0:T(8,128)S(1)} %get-tuple-element.304), channel_id=1, source_target_pairs={{0,1},{1,2},{2,3},{4,5},{5,6},{6,7},{8,9},{9,10},{10,11},{12,13},{... | collective-permute-start | bytes 2088968 | tf_op jit(solution)/shard_map/ppermute | solution.py:50
  156.6 6.4 %collective-permute-start.18 = (f32[9,1,9,33]{3,2,1,0:T(8,128)S(1)}, f32[9,1,9,33]{3,2,1,0:T(8,128)S(1)}, u32[]{:S(2)}, u32[]{:S(2)}) collective-permute-start(f32[9,1,9,33]{3,2,1,0:T(8,128)S(1)} %fusion.62), channel_id=1, source_target_pairs={{0,1},{1,2},{2,3},{4,5},{5,6},{6,7},{8,9},{9,10},{10,11},{12,13},{... | collective-permute-start | bytes 32084 | tf_op jit(solution)/shard_map/ppermute | solution.py:62
  163.0 6.6 %collective-permute-start.19 = (f32[9,1,9,33]{3,2,1,0:T(8,128)S(1)}, f32[9,1,9,33]{3,2,1,0:T(8,128)S(1)}, u32[]{:S(2)}, u32[]{:S(2)}) collective-permute-start(f32[9,1,9,33]{3,2,1,0:T(8,128)S(1)} %get-tuple-element.264), channel_id=1, source_target_pairs={{1,0},{2,1},{3,2},{5,4},{6,5},{7,6},{9,8},{10,9},{11,10},{13,12},{... | collective-permute-start | bytes 32084 | tf_op jit(solution)/shard_map/ppermute | solution.py:63
  169.6 11.7 %collective-permute-start.20 = (f32[9,3,1,33]{3,2,1,0:T(1,128)S(1)}, f32[9,3,1,33]{3,2,1,0:T(1,128)S(1)}, u32[]{:S(2)}, u32[]{:S(2)}) collective-permute-start(f32[9,3,1,33]{3,2,1,0:T(1,128)S(1)} %get-tuple-element.344), channel_id=1, source_target_pairs={{0,16},{16,32},{32,48},{48,64},{64,80},{80,96},{96,112},{112,128},... | collective-permute-start | bytes 10700 | tf_op jit(solution)/shard_map/ppermute | solution.py:62
  171.6 9.9 %collective-permute-start.21 = (f32[9,3,1,33]{3,2,1,0:T(1,128)S(1)}, f32[9,3,1,33]{3,2,1,0:T(1,128)}, u32[]{:S(2)}, u32[]{:S(2)}) collective-permute-start(f32[9,3,1,33]{3,2,1,0:T(1,128)S(1)} %get-tuple-element.345), channel_id=1, source_target_pairs={{16,0},{32,16},{48,32},{64,48},{80,64},{96,80},{112,96},{128,112},... | collective-permute-start | bytes 10700 | tf_op jit(solution)/shard_map/ppermute | solution.py:63
  183.1 17.6 %collective-permute-start.22 = (f32[9,3,9,1]{3,2,1,0:T(8,128)}, f32[9,3,9,1]{3,2,1,0:T(8,128)}, u32[]{:S(2)}, u32[]{:S(2)}) collective-permute-start(f32[9,3,9,1]{3,2,1,0:T(8,128)} %get-tuple-element.340), channel_id=1, source_target_pairs={{0,4},{4,8},{8,12},{1,5},{5,9},{9,13},{2,6},{6,10},{10,14},{3,7},{... | collective-permute-start | bytes 2924 | tf_op jit(solution)/shard_map/ppermute | solution.py:62
  195.9 9.5 %collective-permute-start.23 = (f32[9,3,9,1]{3,2,1,0:T(8,128)}, f32[9,3,9,1]{3,2,1,0:T(8,128)}, u32[]{:S(2)}, u32[]{:S(2)}) collective-permute-start(f32[9,3,9,1]{3,2,1,0:T(8,128)} %get-tuple-element.341), channel_id=1, source_target_pairs={{4,0},{8,4},{12,8},{5,1},{9,5},{13,9},{6,2},{10,6},{14,10},{7,3},{... | collective-permute-start | bytes 2924 | tf_op jit(solution)/shard_map/ppermute | solution.py:63
  219.7 5.4 %collective-permute-start = (f32[3,1,9,33]{3,2,1,0:T(8,128)S(1)}, f32[3,1,9,33]{3,2,1,0:T(8,128)S(1)}, u32[]{:S(2)}, u32[]{:S(2)}) collective-permute-start(f32[3,1,9,33]{3,2,1,0:T(8,128)S(1)} %get-tuple-element.472), channel_id=1, source_target_pairs={{0,1},{1,2},{2,3},{4,5},{5,6},{6,7},{8,9},{9,10},{10,11},{12,13},{... | collective-permute-start | bytes 10700 | tf_op jit(solution)/shard_map/while/body/eval_jaxpr/ppermute | solution.py:62
  223.6 5.7 %collective-permute-start.1 = (f32[3,1,9,33]{3,2,1,0:T(8,128)S(1)}, f32[3,1,9,33]{3,2,1,0:T(8,128)S(1)}, u32[]{:S(2)}, u32[]{:S(2)}) collective-permute-start(f32[3,1,9,33]{3,2,1,0:T(8,128)S(1)} %get-tuple-element.473), channel_id=1, source_target_pairs={{1,0},{2,1},{3,2},{5,4},{6,5},{7,6},{9,8},{10,9},{11,10},{13,12},{... | collective-permute-start | bytes 10700 | tf_op jit(solution)/shard_map/while/body/eval_jaxpr/ppermute | solution.py:63
  229.3 9.7 %collective-permute-start.2 = (f32[3,3,1,33]{3,2,1,0:T(1,128)S(1)}, f32[3,3,1,33]{3,2,1,0:T(1,128)S(1)}, u32[]{:S(2)}, u32[]{:S(2)}) collective-permute-start(f32[3,3,1,33]{3,2,1,0:T(1,128)S(1)} %pad_maximum_fusion.28), channel_id=1, source_target_pairs={{0,16},{16,32},{32,48},{48,64},{64,80},{80,96},{96,112},{112,128},... | collective-permute-start | bytes 3572 | tf_op jit(solution)/shard_map/while/body/eval_jaxpr/ppermute | solution.py:62
  243.1 4.8 %collective-permute-start.4 = (f32[3,3,9,1]{3,2,1,0:T(8,128)}, f32[3,3,9,1]{3,2,1,0:T(8,128)S(1)}, u32[]{:S(2)}, u32[]{:S(2)}) collective-permute-start(f32[3,3,9,1]{3,2,1,0:T(8,128)} %get-tuple-element.479), channel_id=1, source_target_pairs={{0,4},{4,8},{8,12},{1,5},{5,9},{9,13},{2,6},{6,10},{10,14},{3,7},{... | collective-permute-start | bytes 980 | tf_op jit(solution)/shard_map/while/body/eval_jaxpr/ppermute | solution.py:62
  245.6 6.6 %collective-permute-start.5 = (f32[3,3,9,1]{3,2,1,0:T(8,128)}, f32[3,3,9,1]{3,2,1,0:T(8,128)}, u32[]{:S(2)}, u32[]{:S(2)}) collective-permute-start(f32[3,3,9,1]{3,2,1,0:T(8,128)} %get-tuple-element.480), channel_id=1, source_target_pairs={{4,0},{8,4},{12,8},{5,1},{9,5},{13,9},{6,2},{10,6},{14,10},{7,3},{... | collective-permute-start | bytes 980 | tf_op jit(solution)/shard_map/while/body/eval_jaxpr/ppermute | solution.py:63
  267.4 5.0 %collective-permute-start = (f32[3,1,9,33]{3,2,1,0:T(8,128)S(1)}, f32[3,1,9,33]{3,2,1,0:T(8,128)S(1)}, u32[]{:S(2)}, u32[]{:S(2)}) collective-permute-start(f32[3,1,9,33]{3,2,1,0:T(8,128)S(1)} %get-tuple-element.472), channel_id=1, source_target_pairs={{0,1},{1,2},{2,3},{4,5},{5,6},{6,7},{8,9},{9,10},{10,11},{12,13},{... | collective-permute-start | bytes 10700 | tf_op jit(solution)/shard_map/while/body/eval_jaxpr/ppermute | solution.py:62
  270.9 5.7 %collective-permute-start.1 = (f32[3,1,9,33]{3,2,1,0:T(8,128)S(1)}, f32[3,1,9,33]{3,2,1,0:T(8,128)S(1)}, u32[]{:S(2)}, u32[]{:S(2)}) collective-permute-start(f32[3,1,9,33]{3,2,1,0:T(8,128)S(1)} %get-tuple-element.473), channel_id=1, source_target_pairs={{1,0},{2,1},{3,2},{5,4},{6,5},{7,6},{9,8},{10,9},{11,10},{13,12},{... | collective-permute-start | bytes 10700 | tf_op jit(solution)/shard_map/while/body/eval_jaxpr/ppermute | solution.py:63
  276.7 9.7 %collective-permute-start.2 = (f32[3,3,1,33]{3,2,1,0:T(1,128)S(1)}, f32[3,3,1,33]{3,2,1,0:T(1,128)S(1)}, u32[]{:S(2)}, u32[]{:S(2)}) collective-permute-start(f32[3,3,1,33]{3,2,1,0:T(1,128)S(1)} %pad_maximum_fusion.28), channel_id=1, source_target_pairs={{0,16},{16,32},{32,48},{48,64},{64,80},{80,96},{96,112},{112,128},... | collective-permute-start | bytes 3572 | tf_op jit(solution)/shard_map/while/body/eval_jaxpr/ppermute | solution.py:62
  290.4 4.5 %collective-permute-start.4 = (f32[3,3,9,1]{3,2,1,0:T(8,128)}, f32[3,3,9,1]{3,2,1,0:T(8,128)S(1)}, u32[]{:S(2)}, u32[]{:S(2)}) collective-permute-start(f32[3,3,9,1]{3,2,1,0:T(8,128)} %get-tuple-element.479), channel_id=1, source_target_pairs={{0,4},{4,8},{8,12},{1,5},{5,9},{9,13},{2,6},{6,10},{10,14},{3,7},{... | collective-permute-start | bytes 980 | tf_op jit(solution)/shard_map/while/body/eval_jaxpr/ppermute | solution.py:62
  292.6 6.6 %collective-permute-start.5 = (f32[3,3,9,1]{3,2,1,0:T(8,128)}, f32[3,3,9,1]{3,2,1,0:T(8,128)}, u32[]{:S(2)}, u32[]{:S(2)}) collective-permute-start(f32[3,3,9,1]{3,2,1,0:T(8,128)} %get-tuple-element.480), channel_id=1, source_target_pairs={{4,0},{8,4},{12,8},{5,1},{9,5},{13,9},{6,2},{10,6},{14,10},{7,3},{... | collective-permute-start | bytes 980 | tf_op jit(solution)/shard_map/while/body/eval_jaxpr/ppermute | solution.py:63
  313.5 5.7 %collective-permute-start.25 = (f32[3,1,9,33]{3,2,1,0:T(8,128)S(1)}, f32[3,1,9,33]{3,2,1,0:T(8,128)S(1)}, u32[]{:S(2)}, u32[]{:S(2)}) collective-permute-start(f32[3,1,9,33]{3,2,1,0:T(8,128)S(1)} %get-tuple-element.355), channel_id=1, source_target_pairs={{1,0},{2,1},{3,2},{5,4},{6,5},{7,6},{9,8},{10,9},{11,10},{13,12},{... | collective-permute-start | bytes 10700 | tf_op jit(solution)/shard_map/ppermute | solution.py:63
  319.3 9.7 %collective-permute-start.26 = (f32[3,3,1,33]{3,2,1,0:T(1,128)S(1)}, f32[3,3,1,33]{3,2,1,0:T(1,128)S(1)}, u32[]{:S(2)}, u32[]{:S(2)}) collective-permute-start(f32[3,3,1,33]{3,2,1,0:T(1,128)S(1)} %pad_maximum_fusion.18), channel_id=1, source_target_pairs={{0,16},{16,32},{32,48},{48,64},{64,80},{80,96},{96,112},{112,128},... | collective-permute-start | bytes 3572 | tf_op jit(solution)/shard_map/ppermute | solution.py:62
  334.3 6.2 %collective-permute-start.29 = (f32[3,3,9,1]{3,2,1,0:T(8,128)S(1)}, f32[3,3,9,1]{3,2,1,0:T(8,128)S(1)}, u32[]{:S(2)}, u32[]{:S(2)}) collective-permute-start(f32[3,3,9,1]{3,2,1,0:T(8,128)S(1)} %get-tuple-element.350), channel_id=1, source_target_pairs={{4,0},{8,4},{12,8},{5,1},{9,5},{13,9},{6,2},{10,6},{14,10},{7,3},{... | collective-permute-start | bytes 980 | tf_op jit(solution)/shard_map/ppermute | solution.py:63
  355.1 5.7 %collective-permute-start.7 = (f32[3,1,9,33]{3,2,1,0:T(8,128)S(1)}, f32[3,1,9,33]{3,2,1,0:T(8,128)S(1)}, u32[]{:S(2)}, u32[]{:S(2)}) collective-permute-start(f32[3,1,9,33]{3,2,1,0:T(8,128)S(1)} %get-tuple-element.499), channel_id=1, source_target_pairs={{1,0},{2,1},{3,2},{5,4},{6,5},{7,6},{9,8},{10,9},{11,10},{13,12},{... | collective-permute-start | bytes 10700 | tf_op jit(solution)/shard_map/while/body/eval_jaxpr/ppermute | solution.py:63
  360.9 9.7 %collective-permute-start.8 = (f32[3,3,1,33]{3,2,1,0:T(1,128)S(1)}, f32[3,3,1,33]{3,2,1,0:T(1,128)S(1)}, u32[]{:S(2)}, u32[]{:S(2)}) collective-permute-start(f32[3,3,1,33]{3,2,1,0:T(1,128)S(1)} %pad_maximum_fusion.29), channel_id=1, source_target_pairs={{0,16},{16,32},{32,48},{48,64},{64,80},{80,96},{96,112},{112,128},... | collective-permute-start | bytes 3572 | tf_op jit(solution)/shard_map/while/body/eval_jaxpr/ppermute | solution.py:62
  376.5 6.6 %collective-permute-start.11 = (f32[3,3,9,1]{3,2,1,0:T(8,128)}, f32[3,3,9,1]{3,2,1,0:T(8,128)}, u32[]{:S(2)}, u32[]{:S(2)}) collective-permute-start(f32[3,3,9,1]{3,2,1,0:T(8,128)} %get-tuple-element.506), channel_id=1, source_target_pairs={{4,0},{8,4},{12,8},{5,1},{9,5},{13,9},{6,2},{10,6},{14,10},{7,3},{... | collective-permute-start | bytes 980 | tf_op jit(solution)/shard_map/while/body/eval_jaxpr/ppermute | solution.py:63
  400.3 5.7 %collective-permute-start.7 = (f32[3,1,9,33]{3,2,1,0:T(8,128)S(1)}, f32[3,1,9,33]{3,2,1,0:T(8,128)S(1)}, u32[]{:S(2)}, u32[]{:S(2)}) collective-permute-start(f32[3,1,9,33]{3,2,1,0:T(8,128)S(1)} %get-tuple-element.499), channel_id=1, source_target_pairs={{1,0},{2,1},{3,2},{5,4},{6,5},{7,6},{9,8},{10,9},{11,10},{13,12},{... | collective-permute-start | bytes 10700 | tf_op jit(solution)/shard_map/while/body/eval_jaxpr/ppermute | solution.py:63
  406.1 9.7 %collective-permute-start.8 = (f32[3,3,1,33]{3,2,1,0:T(1,128)S(1)}, f32[3,3,1,33]{3,2,1,0:T(1,128)S(1)}, u32[]{:S(2)}, u32[]{:S(2)}) collective-permute-start(f32[3,3,1,33]{3,2,1,0:T(1,128)S(1)} %pad_maximum_fusion.29), channel_id=1, source_target_pairs={{0,16},{16,32},{32,48},{48,64},{64,80},{80,96},{96,112},{112,128},... | collective-permute-start | bytes 3572 | tf_op jit(solution)/shard_map/while/body/eval_jaxpr/ppermute | solution.py:62
  421.7 6.6 %collective-permute-start.11 = (f32[3,3,9,1]{3,2,1,0:T(8,128)}, f32[3,3,9,1]{3,2,1,0:T(8,128)}, u32[]{:S(2)}, u32[]{:S(2)}) collective-permute-start(f32[3,3,9,1]{3,2,1,0:T(8,128)} %get-tuple-element.506), channel_id=1, source_target_pairs={{4,0},{8,4},{12,8},{5,1},{9,5},{13,9},{6,2},{10,6},{14,10},{7,3},{... | collective-permute-start | bytes 980 | tf_op jit(solution)/shard_map/while/body/eval_jaxpr/ppermute | solution.py:63
  (53 other events, 508.9 us)

commit v5 on v1

--- a/solution.py
+++ b/solution.py
@@ -152,7 +152,6 @@
 
 def bricks_of(image_slab, deformed_slab):
     both = jnp.concatenate([image_slab, deformed_slab], axis=0)
-    both = halo(both, "gy", 2, DMAX)
     n_gx = lax.axis_size("gx")
     fields, nx, ny = both.shape
     bx = nx // n_gx
@@ -163,6 +162,8 @@
     windows = jnp.concatenate([low, main, high], axis=2)
     windows = jnp.moveaxis(windows, 1, 0)
     brick = lax.all_to_all(windows, "gx", split_axis=0, concat_axis=0, tiled=True)
+    brick = halo(brick, "gy", 3, DMAX)
+    ny = brick.shape[3]
     image = brick[:, 0]
     deformed = brick[:, 1]
     image_ext = halo(image[:, DMAX - 1 : DMAX + bx + 1, DMAX - 1 : ny - DMAX + 1], "gz", 0, 1)

time: 387 us -> 357 us (0.922)
  waiting for transfers between devices: 204 us -> 184 us
  starting transfers between devices: 111 us -> 105 us
  local copies, waits for them, and re-layouts: 21.7 us -> 17.2 us
    all_to_all x1, waiting for transfers between devices: 85.3 us -> 61.6 us  [bricks_of(): lax.all_to_all(windows, 'gx', split_axis=0, concat_axis=0, tiled=True)]
    ppermute x3, waiting for transfers between devices: 3.28 us -> 10.7 us  [halo(): lax.ppermute(lax.slice_in_dim(block, size - width, size, axis=dim), axis,...]
    ppermute x18, starting transfers between devices: 49.9 us -> 42.6 us  [share(): from_low = lax.ppermute(last, axis, forward)]
  transfers between devices with their start and end apart: 43 -> 43, of which waited for: 39 -> 37; matrix products, arithmetic and copies ran while one was open for 3% -> 3% of each run, Pallas kernels for 0% -> 0%
where the time goes in v5:
time: 357 us; the launch traced here: 356 us
  waiting for transfers between devices  184 us (52%)
  starting transfers between devices  105 us (29%)
  other arithmetic  28.1 us (8%)
  local copies, waits for them, and re-layouts  17.2 us (5%)
  matrix products  11.5 us (3%)
  between operations  10.1 us (3%)
    all_to_all x1, waiting for transfers between devices, bricks_of(): lax.all_to_all(windows, 'gx', split_axis=0, concat_axis=0, tiled=True)  61.6 us
    ppermute x18, waiting for transfers between devices, share(): from_high = lax.ppermute(first, axis, backward)  59 us
    ppermute x18, waiting for transfers between devices, share(): from_low = lax.ppermute(last, axis, forward)  48.1 us
    ppermute x18, starting transfers between devices, share(): from_low = lax.ppermute(last, axis, forward)  42.6 us
    ppermute x18, starting transfers between devices, share(): from_high = lax.ppermute(first, axis, backward)  34 us
    ppermute x3, starting transfers between devices, halo(): lax.ppermute(lax.slice_in_dim(block, size - width, size, axis=dim), axis,...  12.6 us
    all_to_all x1, starting transfers between devices, bricks_of(): lax.all_to_all(windows, 'gx', split_axis=0, concat_axis=0, tiled=True)  11.6 us
    ppermute x3, waiting for transfers between devices, halo(): lax.ppermute(lax.slice_in_dim(block, size - width, size, axis=dim), axis,...  10.7 us
  transfers between devices with their start and end apart: 43, of which 37 were waited for; matrix products, arithmetic and copies ran while one was open for 3% of the time, Pallas kernels for 0%

profile of v5, /device:TPU:4, one launch (start us, length us, event | category | flops | bytes accessed | tf_op | source)
XLA Modules:
  0.0 355.5 jit_solution(4784283519985275263)
XLA Ops:
  4.3 11.6 %all-to-all-start = ((f32[16,2,80,256]{3,2,1,0:T(8,128)}), f32[16,2,80,256]{3,2,1,0:T(8,128)S(1)}, u32[]{:S(2)}, u32[]{:S(2)}) async-start(f32[16,2,80,256]{3,2,1,0:T(8,128)} %copy.44), calls=%async_computation | async-start | bytes 5242880 | tf_op jit(solution)/shard_map/all_to_all | solution.py:164
  16.5 61.6 %all-to-all-done = f32[16,2,80,256]{3,2,1,0:T(8,128)S(1)} async-done(((f32[16,2,80,256]{3,2,1,0:T(8,128)}), f32[16,2,80,256]{3,2,1,0:T(8,128)S(1)}, u32[]{:S(2)}, u32[]{:S(2)}) %all-to-all-start) | async-done | bytes 2621472 | tf_op jit(solution)/shard_map/all_to_all | solution.py:164
  84.6 4.6 %collective-permute-start = (f32[16,2,80,8]{2,3,1,0:T(8,128)S(1)}, f32[16,2,80,8]{2,3,1,0:T(8,128)S(1)}, u32[]{:S(2)}, u32[]{:S(2)}) collective-permute-start(f32[16,2,80,8]{2,3,1,0:T(8,128)S(1)} %copy.45), channel_id=1, source_target_pairs={{0,4},{4,8},{8,12},{1,5},{5,9},{9,13},{2,6},{6,10},{10,14},{3,7},{... | collective-permute-start | bytes 245768 | tf_op jit(solution)/shard_map/ppermute | solution.py:50
  96.7 3.1 pad_maximum_fusion
  100.2 3.5 collective-permute-start.3
  105.8 4.6 %collective-permute-start.4 = (f32[8,80,272]{2,1,0:T(8,128)S(1)}, f32[8,80,272]{2,1,0:T(8,128)S(1)}, u32[]{:S(2)}, u32[]{:S(2)}) collective-permute-start(f32[8,80,272]{2,1,0:T(8,128)S(1)} %get-tuple-element.48), channel_id=1, source_target_pairs={{0,1},{1,2},{2,3},{4,5},{5,6},{6,7},{8,9},{9,10},{10,11},{12,13},{... | collective-permute-start | bytes 2088968 | tf_op jit(solution)/shard_map/ppermute | solution.py:50
  119.0 10.7 %collective-permute-done.4 = f32[8,80,272]{2,1,0:T(8,128)S(1)} collective-permute-done((f32[8,80,272]{2,1,0:T(8,128)S(1)}, f32[8,80,272]{2,1,0:T(8,128)S(1)}, u32[]{:S(2)}, u32[]{:S(2)}) %collective-permute-start.4) | collective-permute-done | bytes 696352 | tf_op jit(solution)/shard_map/ppermute | solution.py:50
  129.7 4.2 %collective-permute-done.5 = f32[8,80,272]{2,1,0:T(8,128)S(1)} collective-permute-done((f32[8,80,272]{2,1,0:T(8,128)S(1)}, f32[8,80,272]{2,1,0:T(8,128)S(1)}, u32[]{:S(2)}, u32[]{:S(2)}) %collective-permute-start.5) | collective-permute-done | bytes 696352 | tf_op jit(solution)/shard_map/ppermute | solution.py:51
  136.9 3.4 collective-permute-start.6
  143.6 5.3 %collective-permute-done.7 = f32[9,1,9,33]{3,2,1,0:T(8,128)S(1)} collective-permute-done((f32[9,1,9,33]{3,2,1,0:T(8,128)S(1)}, f32[9,1,9,33]{3,2,1,0:T(8,128)S(1)}, u32[]{:S(2)}, u32[]{:S(2)}) %collective-permute-start.7) | collective-permute-done | bytes 10724 | tf_op jit(solution)/shard_map/ppermute | solution.py:63
  150.9 8.4 %collective-permute-start.9 = (f32[9,3,1,33]{3,2,1,0:T(1,128)S(1)}, f32[9,3,1,33]{3,2,1,0:T(1,128)S(1)}, u32[]{:S(2)}, u32[]{:S(2)}) collective-permute-start(f32[9,3,1,33]{3,2,1,0:T(1,128)S(1)} %get-tuple-element.119), channel_id=1, source_target_pairs={{16,0},{32,16},{48,32},{64,48},{80,64},{96,80},{112,96},{128,112},... | collective-permute-start | bytes 10700 | tf_op jit(solution)/shard_map/ppermute | solution.py:63
  161.0 3.6 %collective-permute-start.10 = (f32[9,3,9,1]{3,2,1,0:T(8,128)S(1)}, f32[9,3,9,1]{3,2,1,0:T(8,128)S(1)}, u32[]{:S(2)}, u32[]{:S(2)}) collective-permute-start(f32[9,3,9,1]{3,2,1,0:T(8,128)S(1)} %get-tuple-element.114), channel_id=1, source_target_pairs={{0,4},{4,8},{8,12},{1,5},{5,9},{9,13},{2,6},{6,10},{10,14},{3,7},{... | collective-permute-start | bytes 2924 | tf_op jit(solution)/shard_map/ppermute | solution.py:62
  166.3 3.6 %collective-permute-done.10 = f32[9,3,9,1]{3,2,1,0:T(8,128)S(1)} collective-permute-done((f32[9,3,9,1]{3,2,1,0:T(8,128)S(1)}, f32[9,3,9,1]{3,2,1,0:T(8,128)S(1)}, u32[]{:S(2)}, u32[]{:S(2)}) %collective-permute-start.10) | collective-permute-done | bytes 1004 | tf_op jit(solution)/shard_map/ppermute | solution.py:62
  169.9 4.1 %collective-permute-done.11 = f32[9,3,9,1]{3,2,1,0:T(8,128)S(1)} collective-permute-done((f32[9,3,9,1]{3,2,1,0:T(8,128)S(1)}, f32[9,3,9,1]{3,2,1,0:T(8,128)S(1)}, u32[]{:S(2)}, u32[]{:S(2)}) %collective-permute-start.11) | collective-permute-done | bytes 1004 | tf_op jit(solution)/shard_map/ppermute | solution.py:63
  177.7 3.9 %collective-permute-start.12 = (f32[3,1,9,33]{3,2,1,0:T(8,128)S(1)}, f32[3,1,9,33]{3,2,1,0:T(8,128)S(1)}, u32[]{:S(2)}, u32[]{:S(2)}) collective-permute-start(f32[3,1,9,33]{3,2,1,0:T(8,128)S(1)} %get-tuple-element.164), channel_id=1, source_target_pairs={{0,1},{1,2},{2,3},{4,5},{5,6},{6,7},{8,9},{9,10},{10,11},{12,13},{... | collective-permute-start | bytes 10700 | tf_op jit(solution)/shard_map/ppermute | solution.py:62
  183.2 4.2 %collective-permute-done.13 = f32[3,1,9,33]{3,2,1,0:T(8,128)S(1)} collective-permute-done((f32[3,1,9,33]{3,2,1,0:T(8,128)S(1)}, f32[3,1,9,33]{3,2,1,0:T(8,128)S(1)}, u32[]{:S(2)}, u32[]{:S(2)}) %collective-permute-start.13) | collective-permute-done | bytes 3596 | tf_op jit(solution)/shard_map/ppermute | solution.py:63
  189.3 7.8 %collective-permute-done.14 = f32[3,3,1,33]{3,2,1,0:T(1,128)S(1)} collective-permute-done((f32[3,3,1,33]{3,2,1,0:T(1,128)S(1)}, f32[3,3,1,33]{3,2,1,0:T(1,128)S(1)}, u32[]{:S(2)}, u32[]{:S(2)}) %collective-permute-start.14) | collective-permute-done | bytes 1220 | tf_op jit(solution)/shard_map/ppermute | solution.py:62
  200.5 2.9 collective-permute-start.16
  205.3 4.3 %collective-permute-done.17 = f32[3,3,9,1]{3,2,1,0:T(8,128)S(1)} collective-permute-done((f32[3,3,9,1]{3,2,1,0:T(8,128)S(1)}, f32[3,3,9,1]{3,2,1,0:T(8,128)S(1)}, u32[]{:S(2)}, u32[]{:S(2)}) %collective-permute-start.17) | collective-permute-done | bytes 356 | tf_op jit(solution)/shard_map/ppermute | solution.py:63
  213.6 3.2 collective-permute-start.18
  218.3 4.2 %collective-permute-done.19 = f32[3,1,9,33]{3,2,1,0:T(8,128)S(1)} collective-permute-done((f32[3,1,9,33]{3,2,1,0:T(8,128)S(1)}, f32[3,1,9,33]{3,2,1,0:T(8,128)S(1)}, u32[]{:S(2)}, u32[]{:S(2)}) %collective-permute-start.19) | collective-permute-done | bytes 3596 | tf_op jit(solution)/shard_map/ppermute | solution.py:63
  224.5 7.8 %collective-permute-done.20 = f32[3,3,1,33]{3,2,1,0:T(1,128)S(1)} collective-permute-done((f32[3,3,1,33]{3,2,1,0:T(1,128)S(1)}, f32[3,3,1,33]{3,2,1,0:T(1,128)S(1)}, u32[]{:S(2)}, u32[]{:S(2)}) %collective-permute-start.20) | collective-permute-done | bytes 1220 | tf_op jit(solution)/shard_map/ppermute | solution.py:62
  244.7 4.7 %collective-permute-done.23 = f32[3,3,9,1]{3,2,1,0:T(8,128)} collective-permute-done((f32[3,3,9,1]{3,2,1,0:T(8,128)}, f32[3,3,9,1]{3,2,1,0:T(8,128)}, u32[]{:S(2)}, u32[]{:S(2)}) %collective-permute-start.23) | collective-permute-done | bytes 356 | tf_op jit(solution)/shard_map/ppermute | solution.py:63
  261.3 4.2 %collective-permute-done.25 = f32[3,1,9,33]{3,2,1,0:T(8,128)S(1)} collective-permute-done((f32[3,1,9,33]{3,2,1,0:T(8,128)S(1)}, f32[3,1,9,33]{3,2,1,0:T(8,128)S(1)}, u32[]{:S(2)}, u32[]{:S(2)}) %collective-permute-start.25) | collective-permute-done | bytes 3596 | tf_op jit(solution)/shard_map/ppermute | solution.py:63
  267.5 7.8 %collective-permute-done.26 = f32[3,3,1,33]{3,2,1,0:T(1,128)S(1)} collective-permute-done((f32[3,3,1,33]{3,2,1,0:T(1,128)S(1)}, f32[3,3,1,33]{3,2,1,0:T(1,128)S(1)}, u32[]{:S(2)}, u32[]{:S(2)}) %collective-permute-start.26) | collective-permute-done | bytes 1220 | tf_op jit(solution)/shard_map/ppermute | solution.py:62
  282.3 4.3 %collective-permute-done.29 = f32[3,3,9,1]{3,2,1,0:T(8,128)S(1)} collective-permute-done((f32[3,3,9,1]{3,2,1,0:T(8,128)S(1)}, f32[3,3,9,1]{3,2,1,0:T(8,128)S(1)}, u32[]{:S(2)}, u32[]{:S(2)}) %collective-permute-start.29) | collective-permute-done | bytes 356 | tf_op jit(solution)/shard_map/ppermute | solution.py:63
  293.3 4.2 %collective-permute-done.31 = f32[3,1,9,33]{3,2,1,0:T(8,128)S(1)} collective-permute-done((f32[3,1,9,33]{3,2,1,0:T(8,128)S(1)}, f32[3,1,9,33]{3,2,1,0:T(8,128)S(1)}, u32[]{:S(2)}, u32[]{:S(2)}) %collective-permute-start.31) | collective-permute-done | bytes 3596 | tf_op jit(solution)/shard_map/ppermute | solution.py:63
  299.5 7.8 %collective-permute-done.32 = f32[3,3,1,33]{3,2,1,0:T(1,128)S(1)} collective-permute-done((f32[3,3,1,33]{3,2,1,0:T(1,128)S(1)}, f32[3,3,1,33]{3,2,1,0:T(1,128)S(1)}, u32[]{:S(2)}, u32[]{:S(2)}) %collective-permute-start.32) | collective-permute-done | bytes 1220 | tf_op jit(solution)/shard_map/ppermute | solution.py:62
  314.5 4.3 %collective-permute-done.35 = f32[3,3,9,1]{3,2,1,0:T(8,128)S(1)} collective-permute-done((f32[3,3,9,1]{3,2,1,0:T(8,128)S(1)}, f32[3,3,9,1]{3,2,1,0:T(8,128)S(1)}, u32[]{:S(2)}, u32[]{:S(2)}) %collective-permute-start.35) | collective-permute-done | bytes 356 | tf_op jit(solution)/shard_map/ppermute | solution.py:63
  325.6 4.2 %collective-permute-done.37 = f32[3,1,9,33]{3,2,1,0:T(8,128)S(1)} collective-permute-done((f32[3,1,9,33]{3,2,1,0:T(8,128)S(1)}, f32[3,1,9,33]{3,2,1,0:T(8,128)S(1)}, u32[]{:S(2)}, u32[]{:S(2)}) %collective-permute-start.37) | collective-permute-done | bytes 3596 | tf_op jit(solution)/shard_map/ppermute | solution.py:63
  331.8 7.8 %collective-permute-done.38 = f32[3,3,1,33]{3,2,1,0:T(1,128)S(1)} collective-permute-done((f32[3,3,1,33]{3,2,1,0:T(1,128)S(1)}, f32[3,3,1,33]{3,2,1,0:T(1,128)S(1)}, u32[]{:S(2)}, u32[]{:S(2)}) %collective-permute-start.38) | collective-permute-done | bytes 1220 | tf_op jit(solution)/shard_map/ppermute | solution.py:62
  346.8 4.3 %collective-permute-done.41 = f32[3,3,9,1]{3,2,1,0:T(8,128)S(1)} collective-permute-done((f32[3,3,9,1]{3,2,1,0:T(8,128)S(1)}, f32[3,3,9,1]{3,2,1,0:T(8,128)S(1)}, u32[]{:S(2)}, u32[]{:S(2)}) %collective-permute-start.41) | collective-permute-done | bytes 356 | tf_op jit(solution)/shard_map/ppermute | solution.py:63
  (262 shorter events, 121.1 us)
Async XLA Ops:
  4.3 73.7 %all-to-all-start = ((f32[16,2,80,256]{3,2,1,0:T(8,128)}), f32[16,2,80,256]{3,2,1,0:T(8,128)S(1)}, u32[]{:S(2)}, u32[]{:S(2)}) async-start(f32[16,2,80,256]{3,2,1,0:T(8,128)} %copy.44), calls=%async_computation | async-start | bytes 5242880 | tf_op jit(solution)/shard_map/all_to_all | solution.py:164
  83.3 11.9 %collective-permute-start.1 = (f32[16,2,80,8]{2,3,1,0:T(8,128)S(1)}, f32[16,2,80,8]{2,3,1,0:T(8,128)S(1)}, u32[]{:S(2)}, u32[]{:S(2)}) collective-permute-start(f32[16,2,80,8]{2,3,1,0:T(8,128)S(1)} %copy.46), channel_id=1, source_target_pairs={{4,0},{8,4},{12,8},{5,1},{9,5},{13,9},{6,2},{10,6},{14,10},{7,3},{... | collective-permute-start | bytes 245768 | tf_op jit(solution)/shard_map/ppermute | solution.py:51
  84.6 9.1 %collective-permute-start = (f32[16,2,80,8]{2,3,1,0:T(8,128)S(1)}, f32[16,2,80,8]{2,3,1,0:T(8,128)S(1)}, u32[]{:S(2)}, u32[]{:S(2)}) collective-permute-start(f32[16,2,80,8]{2,3,1,0:T(8,128)S(1)} %copy.45), channel_id=1, source_target_pairs={{0,4},{4,8},{8,12},{1,5},{5,9},{9,13},{2,6},{6,10},{10,14},{3,7},{... | collective-permute-start | bytes 245768 | tf_op jit(solution)/shard_map/ppermute | solution.py:50
  100.2 11.7 %collective-permute-start.3 = (f32[1,66,258]{2,1,0:T(8,128)S(1)}, f32[1,66,258]{2,1,0:T(8,128)S(1)}, u32[]{:S(2)}, u32[]{:S(2)}) collective-permute-start(f32[1,66,258]{2,1,0:T(8,128)S(1)} %get-tuple-element.59), channel_id=1, source_target_pairs={{0,1},{1,2},{2,3},{4,5},{5,6},{6,7},{8,9},{9,10},{10,11},{12,13},{... | collective-permute-start | bytes 204344 | tf_op jit(solution)/shard_map/ppermute | solution.py:50
  103.7 8.2 %collective-permute-start.2 = (f32[1,66,258]{2,1,0:T(8,128)S(1)}, f32[1,66,258]{2,1,0:T(8,128)S(1)}, u32[]{:S(2)}, u32[]{:S(2)}) collective-permute-start(f32[1,66,258]{2,1,0:T(8,128)S(1)} %get-tuple-element.60), channel_id=1, source_target_pairs={{1,0},{2,1},{3,2},{5,4},{6,5},{7,6},{9,8},{10,9},{11,10},{13,12},{... | collective-permute-start | bytes 204344 | tf_op jit(solution)/shard_map/ppermute | solution.py:51
  105.8 24.0 %collective-permute-start.4 = (f32[8,80,272]{2,1,0:T(8,128)S(1)}, f32[8,80,272]{2,1,0:T(8,128)S(1)}, u32[]{:S(2)}, u32[]{:S(2)}) collective-permute-start(f32[8,80,272]{2,1,0:T(8,128)S(1)} %get-tuple-element.48), channel_id=1, source_target_pairs={{0,1},{1,2},{2,3},{4,5},{5,6},{6,7},{8,9},{9,10},{10,11},{12,13},{... | collective-permute-start | bytes 2088968 | tf_op jit(solution)/shard_map/ppermute | solution.py:50
  110.4 23.5 %collective-permute-start.5 = (f32[8,80,272]{2,1,0:T(8,128)S(1)}, f32[8,80,272]{2,1,0:T(8,128)S(1)}, u32[]{:S(2)}, u32[]{:S(2)}) collective-permute-start(f32[8,80,272]{2,1,0:T(8,128)S(1)} %get-tuple-element.49), channel_id=1, source_target_pairs={{1,0},{2,1},{3,2},{5,4},{6,5},{7,6},{9,8},{10,9},{11,10},{13,12},{... | collective-permute-start | bytes 2088968 | tf_op jit(solution)/shard_map/ppermute | solution.py:51
  136.9 5.4 %collective-permute-start.6 = (f32[9,1,9,33]{3,2,1,0:T(8,128)S(1)}, f32[9,1,9,33]{3,2,1,0:T(8,128)S(1)}, u32[]{:S(2)}, u32[]{:S(2)}) collective-permute-start(f32[9,1,9,33]{3,2,1,0:T(8,128)S(1)} %fusion.61), channel_id=1, source_target_pairs={{0,1},{1,2},{2,3},{4,5},{5,6},{6,7},{8,9},{9,10},{10,11},{12,13},{... | collective-permute-start | bytes 32084 | tf_op jit(solution)/shard_map/ppermute | solution.py:62
  142.3 6.6 %collective-permute-start.7 = (f32[9,1,9,33]{3,2,1,0:T(8,128)S(1)}, f32[9,1,9,33]{3,2,1,0:T(8,128)S(1)}, u32[]{:S(2)}, u32[]{:S(2)}) collective-permute-start(f32[9,1,9,33]{3,2,1,0:T(8,128)S(1)} %get-tuple-element.42), channel_id=1, source_target_pairs={{1,0},{2,1},{3,2},{5,4},{6,5},{7,6},{9,8},{10,9},{11,10},{13,12},{... | collective-permute-start | bytes 32084 | tf_op jit(solution)/shard_map/ppermute | solution.py:63
  149.0 10.4 %collective-permute-start.8 = (f32[9,3,1,33]{3,2,1,0:T(1,128)S(1)}, f32[9,3,1,33]{3,2,1,0:T(1,128)S(1)}, u32[]{:S(2)}, u32[]{:S(2)}) collective-permute-start(f32[9,3,1,33]{3,2,1,0:T(1,128)S(1)} %get-tuple-element.118), channel_id=1, source_target_pairs={{0,16},{16,32},{32,48},{48,64},{64,80},{80,96},{96,112},{112,128},... | collective-permute-start | bytes 10700 | tf_op jit(solution)/shard_map/ppermute | solution.py:62
  150.9 9.9 %collective-permute-start.9 = (f32[9,3,1,33]{3,2,1,0:T(1,128)S(1)}, f32[9,3,1,33]{3,2,1,0:T(1,128)S(1)}, u32[]{:S(2)}, u32[]{:S(2)}) collective-permute-start(f32[9,3,1,33]{3,2,1,0:T(1,128)S(1)} %get-tuple-element.119), channel_id=1, source_target_pairs={{16,0},{32,16},{48,32},{64,48},{80,64},{96,80},{112,96},{128,112},... | collective-permute-start | bytes 10700 | tf_op jit(solution)/shard_map/ppermute | solution.py:63
  161.0 8.9 %collective-permute-start.10 = (f32[9,3,9,1]{3,2,1,0:T(8,128)S(1)}, f32[9,3,9,1]{3,2,1,0:T(8,128)S(1)}, u32[]{:S(2)}, u32[]{:S(2)}) collective-permute-start(f32[9,3,9,1]{3,2,1,0:T(8,128)S(1)} %get-tuple-element.114), channel_id=1, source_target_pairs={{0,4},{4,8},{8,12},{1,5},{5,9},{9,13},{2,6},{6,10},{10,14},{3,7},{... | collective-permute-start | bytes 2924 | tf_op jit(solution)/shard_map/ppermute | solution.py:62
  164.6 9.3 %collective-permute-start.11 = (f32[9,3,9,1]{3,2,1,0:T(8,128)S(1)}, f32[9,3,9,1]{3,2,1,0:T(8,128)S(1)}, u32[]{:S(2)}, u32[]{:S(2)}) collective-permute-start(f32[9,3,9,1]{3,2,1,0:T(8,128)S(1)} %get-tuple-element.115), channel_id=1, source_target_pairs={{4,0},{8,4},{12,8},{5,1},{9,5},{13,9},{6,2},{10,6},{14,10},{7,3},{... | collective-permute-start | bytes 2924 | tf_op jit(solution)/shard_map/ppermute | solution.py:63
  177.7 5.4 %collective-permute-start.12 = (f32[3,1,9,33]{3,2,1,0:T(8,128)S(1)}, f32[3,1,9,33]{3,2,1,0:T(8,128)S(1)}, u32[]{:S(2)}, u32[]{:S(2)}) collective-permute-start(f32[3,1,9,33]{3,2,1,0:T(8,128)S(1)} %get-tuple-element.164), channel_id=1, source_target_pairs={{0,1},{1,2},{2,3},{4,5},{5,6},{6,7},{8,9},{9,10},{10,11},{12,13},{... | collective-permute-start | bytes 10700 | tf_op jit(solution)/shard_map/ppermute | solution.py:62
  181.7 5.7 %collective-permute-start.13 = (f32[3,1,9,33]{3,2,1,0:T(8,128)S(1)}, f32[3,1,9,33]{3,2,1,0:T(8,128)S(1)}, u32[]{:S(2)}, u32[]{:S(2)}) collective-permute-start(f32[3,1,9,33]{3,2,1,0:T(8,128)S(1)} %get-tuple-element.165), channel_id=1, source_target_pairs={{1,0},{2,1},{3,2},{5,4},{6,5},{7,6},{9,8},{10,9},{11,10},{13,12},{... | collective-permute-start | bytes 10700 | tf_op jit(solution)/shard_map/ppermute | solution.py:63
  187.4 9.7 %collective-permute-start.14 = (f32[3,3,1,33]{3,2,1,0:T(1,128)S(1)}, f32[3,3,1,33]{3,2,1,0:T(1,128)S(1)}, u32[]{:S(2)}, u32[]{:S(2)}) collective-permute-start(f32[3,3,1,33]{3,2,1,0:T(1,128)S(1)} %pad_maximum_fusion.26), channel_id=1, source_target_pairs={{0,16},{16,32},{32,48},{48,64},{64,80},{80,96},{96,112},{112,128},... | collective-permute-start | bytes 3572 | tf_op jit(solution)/shard_map/ppermute | solution.py:62
  200.5 4.8 %collective-permute-start.16 = (f32[3,3,9,1]{3,2,1,0:T(8,128)S(1)}, f32[3,3,9,1]{3,2,1,0:T(8,128)S(1)}, u32[]{:S(2)}, u32[]{:S(2)}) collective-permute-start(f32[3,3,9,1]{3,2,1,0:T(8,128)S(1)} %get-tuple-element.159), channel_id=1, source_target_pairs={{0,4},{4,8},{8,12},{1,5},{5,9},{9,13},{2,6},{6,10},{10,14},{3,7},{... | collective-permute-start | bytes 980 | tf_op jit(solution)/shard_map/ppermute | solution.py:62
  203.4 6.2 %collective-permute-start.17 = (f32[3,3,9,1]{3,2,1,0:T(8,128)S(1)}, f32[3,3,9,1]{3,2,1,0:T(8,128)S(1)}, u32[]{:S(2)}, u32[]{:S(2)}) collective-permute-start(f32[3,3,9,1]{3,2,1,0:T(8,128)S(1)} %get-tuple-element.160), channel_id=1, source_target_pairs={{4,0},{8,4},{12,8},{5,1},{9,5},{13,9},{6,2},{10,6},{14,10},{7,3},{... | collective-permute-start | bytes 980 | tf_op jit(solution)/shard_map/ppermute | solution.py:63
  213.6 4.7 %collective-permute-start.18 = (f32[3,1,9,33]{3,2,1,0:T(8,128)S(1)}, f32[3,1,9,33]{3,2,1,0:T(8,128)S(1)}, u32[]{:S(2)}, u32[]{:S(2)}) collective-permute-start(f32[3,1,9,33]{3,2,1,0:T(8,128)S(1)} %get-tuple-element.155), channel_id=1, source_target_pairs={{0,1},{1,2},{2,3},{4,5},{5,6},{6,7},{8,9},{9,10},{10,11},{12,13},{... | collective-permute-start | bytes 10700 | tf_op jit(solution)/shard_map/ppermute | solution.py:62
  216.8 5.7 %collective-permute-start.19 = (f32[3,1,9,33]{3,2,1,0:T(8,128)S(1)}, f32[3,1,9,33]{3,2,1,0:T(8,128)S(1)}, u32[]{:S(2)}, u32[]{:S(2)}) collective-permute-start(f32[3,1,9,33]{3,2,1,0:T(8,128)S(1)} %get-tuple-element.156), channel_id=1, source_target_pairs={{1,0},{2,1},{3,2},{5,4},{6,5},{7,6},{9,8},{10,9},{11,10},{13,12},{... | collective-permute-start | bytes 10700 | tf_op jit(solution)/shard_map/ppermute | solution.py:63
  222.6 9.7 %collective-permute-start.20 = (f32[3,3,1,33]{3,2,1,0:T(1,128)S(1)}, f32[3,3,1,33]{3,2,1,0:T(1,128)S(1)}, u32[]{:S(2)}, u32[]{:S(2)}) collective-permute-start(f32[3,3,1,33]{3,2,1,0:T(1,128)S(1)} %pad_maximum_fusion.24), channel_id=1, source_target_pairs={{0,16},{16,32},{32,48},{48,64},{64,80},{80,96},{96,112},{112,128},... | collective-permute-start | bytes 3572 | tf_op jit(solution)/shard_map/ppermute | solution.py:62
  232.4 6.1 %collective-permute-start.21 = (f32[3,3,1,33]{3,2,1,0:T(1,128)S(1)}, f32[3,3,1,33]{3,2,1,0:T(1,128)S(1)}, u32[]{:S(2)}, u32[]{:S(2)}) collective-permute-start(f32[3,3,1,33]{3,2,1,0:T(1,128)S(1)} %get-tuple-element.29), channel_id=1, source_target_pairs={{16,0},{32,16},{48,32},{64,48},{80,64},{96,80},{112,96},{128,112},... | collective-permute-start | bytes 3572 | tf_op jit(solution)/shard_map/ppermute | solution.py:63
  242.8 6.6 %collective-permute-start.23 = (f32[3,3,9,1]{3,2,1,0:T(8,128)}, f32[3,3,9,1]{3,2,1,0:T(8,128)}, u32[]{:S(2)}, u32[]{:S(2)}) collective-permute-start(f32[3,3,9,1]{3,2,1,0:T(8,128)} %get-tuple-element.151), channel_id=1, source_target_pairs={{4,0},{8,4},{12,8},{5,1},{9,5},{13,9},{6,2},{10,6},{14,10},{7,3},{... | collective-permute-start | bytes 980 | tf_op jit(solution)/shard_map/ppermute | solution.py:63
  259.8 5.7 %collective-permute-start.25 = (f32[3,1,9,33]{3,2,1,0:T(8,128)S(1)}, f32[3,1,9,33]{3,2,1,0:T(8,128)S(1)}, u32[]{:S(2)}, u32[]{:S(2)}) collective-permute-start(f32[3,1,9,33]{3,2,1,0:T(8,128)S(1)} %get-tuple-element.147), channel_id=1, source_target_pairs={{1,0},{2,1},{3,2},{5,4},{6,5},{7,6},{9,8},{10,9},{11,10},{13,12},{... | collective-permute-start | bytes 10700 | tf_op jit(solution)/shard_map/ppermute | solution.py:63
  265.6 9.7 %collective-permute-start.26 = (f32[3,3,1,33]{3,2,1,0:T(1,128)S(1)}, f32[3,3,1,33]{3,2,1,0:T(1,128)S(1)}, u32[]{:S(2)}, u32[]{:S(2)}) collective-permute-start(f32[3,3,1,33]{3,2,1,0:T(1,128)S(1)} %pad_maximum_fusion.22), channel_id=1, source_target_pairs={{0,16},{16,32},{32,48},{48,64},{64,80},{80,96},{96,112},{112,128},... | collective-permute-start | bytes 3572 | tf_op jit(solution)/shard_map/ppermute | solution.py:62
  280.3 6.2 %collective-permute-start.29 = (f32[3,3,9,1]{3,2,1,0:T(8,128)S(1)}, f32[3,3,9,1]{3,2,1,0:T(8,128)S(1)}, u32[]{:S(2)}, u32[]{:S(2)}) collective-permute-start(f32[3,3,9,1]{3,2,1,0:T(8,128)S(1)} %get-tuple-element.142), channel_id=1, source_target_pairs={{4,0},{8,4},{12,8},{5,1},{9,5},{13,9},{6,2},{10,6},{14,10},{7,3},{... | collective-permute-start | bytes 980 | tf_op jit(solution)/shard_map/ppermute | solution.py:63
  291.8 5.7 %collective-permute-start.31 = (f32[3,1,9,33]{3,2,1,0:T(8,128)S(1)}, f32[3,1,9,33]{3,2,1,0:T(8,128)S(1)}, u32[]{:S(2)}, u32[]{:S(2)}) collective-permute-start(f32[3,1,9,33]{3,2,1,0:T(8,128)S(1)} %get-tuple-element.138), channel_id=1, source_target_pairs={{1,0},{2,1},{3,2},{5,4},{6,5},{7,6},{9,8},{10,9},{11,10},{13,12},{... | collective-permute-start | bytes 10700 | tf_op jit(solution)/shard_map/ppermute | solution.py:63
  297.5 9.7 %collective-permute-start.32 = (f32[3,3,1,33]{3,2,1,0:T(1,128)S(1)}, f32[3,3,1,33]{3,2,1,0:T(1,128)S(1)}, u32[]{:S(2)}, u32[]{:S(2)}) collective-permute-start(f32[3,3,1,33]{3,2,1,0:T(1,128)S(1)} %pad_maximum_fusion.20), channel_id=1, source_target_pairs={{0,16},{16,32},{32,48},{48,64},{64,80},{80,96},{96,112},{112,128},... | collective-permute-start | bytes 3572 | tf_op jit(solution)/shard_map/ppermute | solution.py:62
  312.6 6.2 %collective-permute-start.35 = (f32[3,3,9,1]{3,2,1,0:T(8,128)S(1)}, f32[3,3,9,1]{3,2,1,0:T(8,128)S(1)}, u32[]{:S(2)}, u32[]{:S(2)}) collective-permute-start(f32[3,3,9,1]{3,2,1,0:T(8,128)S(1)} %get-tuple-element.133), channel_id=1, source_target_pairs={{4,0},{8,4},{12,8},{5,1},{9,5},{13,9},{6,2},{10,6},{14,10},{7,3},{... | collective-permute-start | bytes 980 | tf_op jit(solution)/shard_map/ppermute | solution.py:63
  324.1 5.7 %collective-permute-start.37 = (f32[3,1,9,33]{3,2,1,0:T(8,128)S(1)}, f32[3,1,9,33]{3,2,1,0:T(8,128)S(1)}, u32[]{:S(2)}, u32[]{:S(2)}) collective-permute-start(f32[3,1,9,33]{3,2,1,0:T(8,128)S(1)} %get-tuple-element.129), channel_id=1, source_target_pairs={{1,0},{2,1},{3,2},{5,4},{6,5},{7,6},{9,8},{10,9},{11,10},{13,12},{... | collective-permute-start | bytes 10700 | tf_op jit(solution)/shard_map/ppermute | solution.py:63
  329.8 9.7 %collective-permute-start.38 = (f32[3,3,1,33]{3,2,1,0:T(1,128)S(1)}, f32[3,3,1,33]{3,2,1,0:T(1,128)S(1)}, u32[]{:S(2)}, u32[]{:S(2)}) collective-permute-start(f32[3,3,1,33]{3,2,1,0:T(1,128)S(1)} %pad_maximum_fusion.18), channel_id=1, source_target_pairs={{0,16},{16,32},{32,48},{48,64},{64,80},{80,96},{96,112},{112,128},... | collective-permute-start | bytes 3572 | tf_op jit(solution)/shard_map/ppermute | solution.py:62
  344.9 6.2 %collective-permute-start.41 = (f32[3,3,9,1]{3,2,1,0:T(8,128)S(1)}, f32[3,3,9,1]{3,2,1,0:T(8,128)S(1)}, u32[]{:S(2)}, u32[]{:S(2)}) collective-permute-start(f32[3,3,9,1]{3,2,1,0:T(8,128)S(1)} %get-tuple-element.124), channel_id=1, source_target_pairs={{4,0},{8,4},{12,8},{5,1},{9,5},{13,9},{6,2},{10,6},{14,10},{7,3},{... | collective-permute-start | bytes 980 | tf_op jit(solution)/shard_map/ppermute | solution.py:63
  (31 other events, 228.9 us)

commit v6 on v5

--- a/solution.py
+++ b/solution.py
@@ -155,14 +155,10 @@
     n_gx = lax.axis_size("gx")
     fields, nx, ny = both.shape
     bx = nx // n_gx
-    main = both.reshape(fields, n_gx, bx, ny)
-    zero = jnp.zeros((fields, 1, DMAX, ny), both.dtype)
-    low = jnp.concatenate([zero, main[:, :-1, bx - DMAX :]], axis=1)
-    high = jnp.concatenate([main[:, 1:, :DMAX], zero], axis=1)
-    windows = jnp.concatenate([low, main, high], axis=2)
-    windows = jnp.moveaxis(windows, 1, 0)
-    brick = lax.all_to_all(windows, "gx", split_axis=0, concat_axis=0, tiled=True)
+    blocks = jnp.moveaxis(both.reshape(fields, n_gx, bx, ny), 1, 0)
+    brick = lax.all_to_all(blocks, "gx", split_axis=0, concat_axis=0, tiled=True)
     brick = halo(brick, "gy", 3, DMAX)
+    brick = halo(brick, "gx", 2, DMAX)
     ny = brick.shape[3]
     image = brick[:, 0]
     deformed = brick[:, 1]

time: 357 us -> 368 us (1.031)
  blocking collectives: 0 us -> 62 us
  waiting for transfers between devices: 184 us -> 137 us
  local copies, waits for them, and re-layouts: 17.2 us -> 13.4 us
    all_to_all x0 -> x1, blocking collectives: none -> 62 us  [bricks_of(): lax.all_to_all(blocks, 'gx', split_axis=0, concat_axis=0, tiled=True)]
    all_to_all x1 -> x0, waiting for transfers between devices: 61.6 us -> none  [bricks_of(): lax.all_to_all(windows, 'gx', split_axis=0, concat_axis=0, tiled=True)]
    all_to_all x1 -> x0, starting transfers between devices: 11.6 us -> none  [bricks_of(): lax.all_to_all(windows, 'gx', split_axis=0, concat_axis=0, tiled=True)]
    ppermute x3 -> x4, waiting for transfers between devices: 10.7 us -> 19.8 us  [halo(): lax.ppermute(lax.slice_in_dim(block, size - width, size, axis=dim), axis,...]
    ppermute x3 -> x4, starting transfers between devices: 4.08 us -> 12.5 us  [halo(): lax.ppermute(lax.slice_in_dim(block, 0, width, axis=dim), axis, backward)]
    ppermute x3 -> x4, waiting for transfers between devices: 4.18 us -> 10.4 us  [halo(): lax.ppermute(lax.slice_in_dim(block, 0, width, axis=dim), axis, backward)]
    ppermute x3 -> x4, starting transfers between devices: 12.6 us -> 13.6 us  [halo(): lax.ppermute(lax.slice_in_dim(block, size - width, size, axis=dim), axis,...]
  transfers between devices with their start and end apart: 43 -> 44, of which waited for: 37 -> 40; matrix products, arithmetic and copies ran while one was open for 3% -> 3% of each run, Pallas kernels for 0% -> 0%
where the time goes in v6:
time: 368 us; the launch traced here: 366 us
  waiting for transfers between devices  137 us (37%)
  starting transfers between devices  103 us (28%)
  blocking collectives  62 us (17%)
  other arithmetic  29.4 us (8%)
  local copies, waits for them, and re-layouts  13.4 us (4%)
  matrix products  11.5 us (3%)
  between operations  9.96 us (3%)
    all_to_all x1, blocking collectives, bricks_of(): lax.all_to_all(blocks, 'gx', split_axis=0, concat_axis=0, tiled=True)  62 us
    ppermute x18, waiting for transfers between devices, share(): from_high = lax.ppermute(first, axis, backward)  59.1 us
    ppermute x18, waiting for transfers between devices, share(): from_low = lax.ppermute(last, axis, forward)  47.7 us
    ppermute x18, starting transfers between devices, share(): from_low = lax.ppermute(last, axis, forward)  42.9 us
    ppermute x18, starting transfers between devices, share(): from_high = lax.ppermute(first, axis, backward)  34 us
    ppermute x4, waiting for transfers between devices, halo(): lax.ppermute(lax.slice_in_dim(block, size - width, size, axis=dim), axis,...  19.8 us
    ppermute x4, starting transfers between devices, halo(): lax.ppermute(lax.slice_in_dim(block, size - width, size, axis=dim), axis,...  13.6 us
    ppermute x4, starting transfers between devices, halo(): lax.ppermute(lax.slice_in_dim(block, 0, width, axis=dim), axis, backward)  12.5 us
  transfers between devices with their start and end apart: 44, of which 40 were waited for; matrix products, arithmetic and copies ran while one was open for 3% of the time, Pallas kernels for 0%

profile of v6, /device:TPU:4, one launch (start us, length us, event | category | flops | bytes accessed | tf_op | source)
XLA Modules:
  0.0 366.4 jit_solution(11279228024704768704)
XLA Ops:
  2.5 62.0 %all_to_all.5 = f32[16,2,64,256]{3,2,1,0:T(8,128)S(1)} all-to-all(f32[16,2,64,256]{3,2,1,0:T(8,128)S(1)} %copy.44), channel_id=1, replica_groups=mesh['gx'=16,'gy'=4,'gz'=4] {'gx'}, dimensions={0} | all-to-all | bytes 4194304 | tf_op jit(solution)/shard_map/all_to_all | solution.py:159
  67.4 3.6 collective-permute-start
  74.1 4.2 %collective-permute-done.1 = f32[16,2,64,8]{2,3,1,0:T(8,128)} collective-permute-done((f32[16,2,64,8]{2,3,1,0:T(8,128)S(1)}, f32[16,2,64,8]{2,3,1,0:T(8,128)}, u32[]{:S(2)}, u32[]{:S(2)}) %collective-permute-start.1) | collective-permute-done | bytes 65568 | tf_op jit(solution)/shard_map/ppermute | solution.py:51
  84.7 8.4 %collective-permute-start.3 = (f32[16,2,8,272]{3,2,1,0:T(8,128)}, f32[16,2,8,272]{3,2,1,0:T(8,128)}, u32[]{:S(2)}, u32[]{:S(2)}) collective-permute-start(f32[16,2,8,272]{3,2,1,0:T(8,128)} %get-tuple-element.49), channel_id=1, source_target_pairs={{16,0},{32,16},{48,32},{64,48},{80,64},{96,80},{112,96},{128,112},... | collective-permute-start | bytes 835592 | tf_op jit(solution)/shard_map/ppermute | solution.py:51
  98.0 6.0 %collective-permute-done.2 = f32[16,2,8,272]{3,2,1,0:T(8,128)S(1)} collective-permute-done((f32[16,2,8,272]{3,2,1,0:T(8,128)}, f32[16,2,8,272]{3,2,1,0:T(8,128)S(1)}, u32[]{:S(2)}, u32[]{:S(2)}) %collective-permute-start.2) | collective-permute-done | bytes 278560 | tf_op jit(solution)/shard_map/ppermute | solution.py:50
  108.3 3.5 collective-permute-start.5
  113.9 4.6 %collective-permute-start.6 = (f32[8,80,272]{2,1,0:T(8,128)S(1)}, f32[8,80,272]{2,1,0:T(8,128)S(1)}, u32[]{:S(2)}, u32[]{:S(2)}) collective-permute-start(f32[8,80,272]{2,1,0:T(8,128)S(1)} %get-tuple-element.50), channel_id=1, source_target_pairs={{0,1},{1,2},{2,3},{4,5},{5,6},{6,7},{8,9},{9,10},{10,11},{12,13},{... | collective-permute-start | bytes 2088968 | tf_op jit(solution)/shard_map/ppermute | solution.py:50
  127.1 12.7 %collective-permute-done.6 = f32[8,80,272]{2,1,0:T(8,128)S(1)} collective-permute-done((f32[8,80,272]{2,1,0:T(8,128)S(1)}, f32[8,80,272]{2,1,0:T(8,128)S(1)}, u32[]{:S(2)}, u32[]{:S(2)}) %collective-permute-start.6) | collective-permute-done | bytes 696352 | tf_op jit(solution)/shard_map/ppermute | solution.py:50
  139.8 4.7 %collective-permute-done.7 = f32[8,80,272]{2,1,0:T(8,128)S(1)} collective-permute-done((f32[8,80,272]{2,1,0:T(8,128)S(1)}, f32[8,80,272]{2,1,0:T(8,128)S(1)}, u32[]{:S(2)}, u32[]{:S(2)}) %collective-permute-start.7) | collective-permute-done | bytes 696352 | tf_op jit(solution)/shard_map/ppermute | solution.py:51
  147.5 3.4 collective-permute-start.8
  154.3 5.4 %collective-permute-done.9 = f32[9,1,9,33]{3,2,1,0:T(8,128)S(1)} collective-permute-done((f32[9,1,9,33]{3,2,1,0:T(8,128)S(1)}, f32[9,1,9,33]{3,2,1,0:T(8,128)S(1)}, u32[]{:S(2)}, u32[]{:S(2)}) %collective-permute-start.9) | collective-permute-done | bytes 10724 | tf_op jit(solution)/shard_map/ppermute | solution.py:63
  161.7 8.4 %collective-permute-start.11 = (f32[9,3,1,33]{3,2,1,0:T(1,128)S(1)}, f32[9,3,1,33]{3,2,1,0:T(1,128)S(1)}, u32[]{:S(2)}, u32[]{:S(2)}) collective-permute-start(f32[9,3,1,33]{3,2,1,0:T(1,128)S(1)} %get-tuple-element.119), channel_id=1, source_target_pairs={{16,0},{32,16},{48,32},{64,48},{80,64},{96,80},{112,96},{128,112},... | collective-permute-start | bytes 10700 | tf_op jit(solution)/shard_map/ppermute | solution.py:63
  175.8 3.1 collective-permute-done.12
  178.9 4.1 %collective-permute-done.13 = f32[9,3,9,1]{3,2,1,0:T(8,128)S(1)} collective-permute-done((f32[9,3,9,1]{3,2,1,0:T(8,128)S(1)}, f32[9,3,9,1]{3,2,1,0:T(8,128)S(1)}, u32[]{:S(2)}, u32[]{:S(2)}) %collective-permute-start.13) | collective-permute-done | bytes 1004 | tf_op jit(solution)/shard_map/ppermute | solution.py:63
  186.8 3.9 %collective-permute-start.14 = (f32[3,1,9,33]{3,2,1,0:T(8,128)S(1)}, f32[3,1,9,33]{3,2,1,0:T(8,128)S(1)}, u32[]{:S(2)}, u32[]{:S(2)}) collective-permute-start(f32[3,1,9,33]{3,2,1,0:T(8,128)S(1)} %get-tuple-element.164), channel_id=1, source_target_pairs={{0,1},{1,2},{2,3},{4,5},{5,6},{6,7},{8,9},{9,10},{10,11},{12,13},{... | collective-permute-start | bytes 10700 | tf_op jit(solution)/shard_map/ppermute | solution.py:62
  192.2 4.2 %collective-permute-done.15 = f32[3,1,9,33]{3,2,1,0:T(8,128)S(1)} collective-permute-done((f32[3,1,9,33]{3,2,1,0:T(8,128)S(1)}, f32[3,1,9,33]{3,2,1,0:T(8,128)S(1)}, u32[]{:S(2)}, u32[]{:S(2)}) %collective-permute-start.15) | collective-permute-done | bytes 3596 | tf_op jit(solution)/shard_map/ppermute | solution.py:63
  198.4 7.8 %collective-permute-done.16 = f32[3,3,1,33]{3,2,1,0:T(1,128)S(1)} collective-permute-done((f32[3,3,1,33]{3,2,1,0:T(1,128)S(1)}, f32[3,3,1,33]{3,2,1,0:T(1,128)S(1)}, u32[]{:S(2)}, u32[]{:S(2)}) %collective-permute-start.16) | collective-permute-done | bytes 1220 | tf_op jit(solution)/shard_map/ppermute | solution.py:62
  214.5 4.3 %collective-permute-done.19 = f32[3,3,9,1]{3,2,1,0:T(8,128)S(1)} collective-permute-done((f32[3,3,9,1]{3,2,1,0:T(8,128)S(1)}, f32[3,3,9,1]{3,2,1,0:T(8,128)S(1)}, u32[]{:S(2)}, u32[]{:S(2)}) %collective-permute-start.19) | collective-permute-done | bytes 356 | tf_op jit(solution)/shard_map/ppermute | solution.py:63
  223.1 3.2 collective-permute-start.20
  227.8 4.2 %collective-permute-done.21 = f32[3,1,9,33]{3,2,1,0:T(8,128)S(1)} collective-permute-done((f32[3,1,9,33]{3,2,1,0:T(8,128)S(1)}, f32[3,1,9,33]{3,2,1,0:T(8,128)S(1)}, u32[]{:S(2)}, u32[]{:S(2)}) %collective-permute-start.21) | collective-permute-done | bytes 3596 | tf_op jit(solution)/shard_map/ppermute | solution.py:63
  234.0 7.8 %collective-permute-done.22 = f32[3,3,1,33]{3,2,1,0:T(1,128)S(1)} collective-permute-done((f32[3,3,1,33]{3,2,1,0:T(1,128)S(1)}, f32[3,3,1,33]{3,2,1,0:T(1,128)S(1)}, u32[]{:S(2)}, u32[]{:S(2)}) %collective-permute-start.22) | collective-permute-done | bytes 1220 | tf_op jit(solution)/shard_map/ppermute | solution.py:62
  249.5 4.3 %collective-permute-start.24 = (f32[3,3,9,1]{3,2,1,0:T(8,128)}, f32[3,3,9,1]{3,2,1,0:T(8,128)}, u32[]{:S(2)}, u32[]{:S(2)}) collective-permute-start(f32[3,3,9,1]{3,2,1,0:T(8,128)} %get-tuple-element.150), channel_id=1, source_target_pairs={{0,4},{4,8},{8,12},{1,5},{5,9},{9,13},{2,6},{6,10},{10,14},{3,7},{... | collective-permute-start | bytes 980 | tf_op jit(solution)/shard_map/ppermute | solution.py:62
  255.6 4.7 %collective-permute-done.25 = f32[3,3,9,1]{3,2,1,0:T(8,128)} collective-permute-done((f32[3,3,9,1]{3,2,1,0:T(8,128)}, f32[3,3,9,1]{3,2,1,0:T(8,128)}, u32[]{:S(2)}, u32[]{:S(2)}) %collective-permute-start.25) | collective-permute-done | bytes 356 | tf_op jit(solution)/shard_map/ppermute | solution.py:63
  272.3 4.2 %collective-permute-done.27 = f32[3,1,9,33]{3,2,1,0:T(8,128)S(1)} collective-permute-done((f32[3,1,9,33]{3,2,1,0:T(8,128)S(1)}, f32[3,1,9,33]{3,2,1,0:T(8,128)S(1)}, u32[]{:S(2)}, u32[]{:S(2)}) %collective-permute-start.27) | collective-permute-done | bytes 3596 | tf_op jit(solution)/shard_map/ppermute | solution.py:63
  278.5 7.8 %collective-permute-done.28 = f32[3,3,1,33]{3,2,1,0:T(1,128)S(1)} collective-permute-done((f32[3,3,1,33]{3,2,1,0:T(1,128)S(1)}, f32[3,3,1,33]{3,2,1,0:T(1,128)S(1)}, u32[]{:S(2)}, u32[]{:S(2)}) %collective-permute-start.28) | collective-permute-done | bytes 1220 | tf_op jit(solution)/shard_map/ppermute | solution.py:62
  293.2 4.3 %collective-permute-done.31 = f32[3,3,9,1]{3,2,1,0:T(8,128)S(1)} collective-permute-done((f32[3,3,9,1]{3,2,1,0:T(8,128)S(1)}, f32[3,3,9,1]{3,2,1,0:T(8,128)S(1)}, u32[]{:S(2)}, u32[]{:S(2)}) %collective-permute-start.31) | collective-permute-done | bytes 356 | tf_op jit(solution)/shard_map/ppermute | solution.py:63
  304.2 4.2 %collective-permute-done.33 = f32[3,1,9,33]{3,2,1,0:T(8,128)S(1)} collective-permute-done((f32[3,1,9,33]{3,2,1,0:T(8,128)S(1)}, f32[3,1,9,33]{3,2,1,0:T(8,128)S(1)}, u32[]{:S(2)}, u32[]{:S(2)}) %collective-permute-start.33) | collective-permute-done | bytes 3596 | tf_op jit(solution)/shard_map/ppermute | solution.py:63
  310.4 7.8 %collective-permute-done.34 = f32[3,3,1,33]{3,2,1,0:T(1,128)S(1)} collective-permute-done((f32[3,3,1,33]{3,2,1,0:T(1,128)S(1)}, f32[3,3,1,33]{3,2,1,0:T(1,128)S(1)}, u32[]{:S(2)}, u32[]{:S(2)}) %collective-permute-start.34) | collective-permute-done | bytes 1220 | tf_op jit(solution)/shard_map/ppermute | solution.py:62
  325.4 4.3 %collective-permute-done.37 = f32[3,3,9,1]{3,2,1,0:T(8,128)S(1)} collective-permute-done((f32[3,3,9,1]{3,2,1,0:T(8,128)S(1)}, f32[3,3,9,1]{3,2,1,0:T(8,128)S(1)}, u32[]{:S(2)}, u32[]{:S(2)}) %collective-permute-start.37) | collective-permute-done | bytes 356 | tf_op jit(solution)/shard_map/ppermute | solution.py:63
  336.5 4.2 %collective-permute-done.39 = f32[3,1,9,33]{3,2,1,0:T(8,128)S(1)} collective-permute-done((f32[3,1,9,33]{3,2,1,0:T(8,128)S(1)}, f32[3,1,9,33]{3,2,1,0:T(8,128)S(1)}, u32[]{:S(2)}, u32[]{:S(2)}) %collective-permute-start.39) | collective-permute-done | bytes 3596 | tf_op jit(solution)/shard_map/ppermute | solution.py:63
  342.7 7.8 %collective-permute-done.40 = f32[3,3,1,33]{3,2,1,0:T(1,128)S(1)} collective-permute-done((f32[3,3,1,33]{3,2,1,0:T(1,128)S(1)}, f32[3,3,1,33]{3,2,1,0:T(1,128)S(1)}, u32[]{:S(2)}, u32[]{:S(2)}) %collective-permute-start.40) | collective-permute-done | bytes 1220 | tf_op jit(solution)/shard_map/ppermute | solution.py:62
  357.8 4.3 %collective-permute-done.43 = f32[3,3,9,1]{3,2,1,0:T(8,128)S(1)} collective-permute-done((f32[3,3,9,1]{3,2,1,0:T(8,128)S(1)}, f32[3,3,9,1]{3,2,1,0:T(8,128)S(1)}, u32[]{:S(2)}, u32[]{:S(2)}) %collective-permute-start.43) | collective-permute-done | bytes 356 | tf_op jit(solution)/shard_map/ppermute | solution.py:63
  (264 shorter events, 128.9 us)
Async XLA Ops:
  67.4 6.4 %collective-permute-start = (f32[16,2,64,8]{2,3,1,0:T(8,128)S(1)}, f32[16,2,64,8]{2,3,1,0:T(8,128)S(1)}, u32[]{:S(2)}, u32[]{:S(2)}) collective-permute-start(f32[16,2,64,8]{2,3,1,0:T(8,128)S(1)} %copy.45), channel_id=1, source_target_pairs={{0,4},{4,8},{8,12},{1,5},{5,9},{9,13},{2,6},{6,10},{10,14},{3,7},{... | collective-permute-start | bytes 196616 | tf_op jit(solution)/shard_map/ppermute | solution.py:50
  71.3 7.0 %collective-permute-start.1 = (f32[16,2,64,8]{2,3,1,0:T(8,128)S(1)}, f32[16,2,64,8]{2,3,1,0:T(8,128)}, u32[]{:S(2)}, u32[]{:S(2)}) collective-permute-start(f32[16,2,64,8]{2,3,1,0:T(8,128)S(1)} %copy.46), channel_id=1, source_target_pairs={{4,0},{8,4},{12,8},{5,1},{9,5},{13,9},{6,2},{10,6},{14,10},{7,3},{... | collective-permute-start | bytes 196616 | tf_op jit(solution)/shard_map/ppermute | solution.py:51
  82.8 21.2 %collective-permute-start.2 = (f32[16,2,8,272]{3,2,1,0:T(8,128)}, f32[16,2,8,272]{3,2,1,0:T(8,128)S(1)}, u32[]{:S(2)}, u32[]{:S(2)}) collective-permute-start(f32[16,2,8,272]{3,2,1,0:T(8,128)} %get-tuple-element.48), channel_id=1, source_target_pairs={{0,16},{16,32},{32,48},{48,64},{64,80},{80,96},{96,112},{112,128},... | collective-permute-start | bytes 835592 | tf_op jit(solution)/shard_map/ppermute | solution.py:50
  84.7 20.8 %collective-permute-start.3 = (f32[16,2,8,272]{3,2,1,0:T(8,128)}, f32[16,2,8,272]{3,2,1,0:T(8,128)}, u32[]{:S(2)}, u32[]{:S(2)}) collective-permute-start(f32[16,2,8,272]{3,2,1,0:T(8,128)} %get-tuple-element.49), channel_id=1, source_target_pairs={{16,0},{32,16},{48,32},{64,48},{80,64},{96,80},{112,96},{128,112},... | collective-permute-start | bytes 835592 | tf_op jit(solution)/shard_map/ppermute | solution.py:51
  108.3 11.7 %collective-permute-start.5 = (f32[1,66,258]{2,1,0:T(8,128)S(1)}, f32[1,66,258]{2,1,0:T(8,128)S(1)}, u32[]{:S(2)}, u32[]{:S(2)}) collective-permute-start(f32[1,66,258]{2,1,0:T(8,128)S(1)} %get-tuple-element.59), channel_id=1, source_target_pairs={{0,1},{1,2},{2,3},{4,5},{5,6},{6,7},{8,9},{9,10},{10,11},{12,13},{... | collective-permute-start | bytes 204344 | tf_op jit(solution)/shard_map/ppermute | solution.py:50
  111.8 8.2 %collective-permute-start.4 = (f32[1,66,258]{2,1,0:T(8,128)S(1)}, f32[1,66,258]{2,1,0:T(8,128)S(1)}, u32[]{:S(2)}, u32[]{:S(2)}) collective-permute-start(f32[1,66,258]{2,1,0:T(8,128)S(1)} %get-tuple-element.60), channel_id=1, source_target_pairs={{1,0},{2,1},{3,2},{5,4},{6,5},{7,6},{9,8},{10,9},{11,10},{13,12},{... | collective-permute-start | bytes 204344 | tf_op jit(solution)/shard_map/ppermute | solution.py:51
  113.9 25.9 %collective-permute-start.6 = (f32[8,80,272]{2,1,0:T(8,128)S(1)}, f32[8,80,272]{2,1,0:T(8,128)S(1)}, u32[]{:S(2)}, u32[]{:S(2)}) collective-permute-start(f32[8,80,272]{2,1,0:T(8,128)S(1)} %get-tuple-element.50), channel_id=1, source_target_pairs={{0,1},{1,2},{2,3},{4,5},{5,6},{6,7},{8,9},{9,10},{10,11},{12,13},{... | collective-permute-start | bytes 2088968 | tf_op jit(solution)/shard_map/ppermute | solution.py:50
  118.5 26.0 %collective-permute-start.7 = (f32[8,80,272]{2,1,0:T(8,128)S(1)}, f32[8,80,272]{2,1,0:T(8,128)S(1)}, u32[]{:S(2)}, u32[]{:S(2)}) collective-permute-start(f32[8,80,272]{2,1,0:T(8,128)S(1)} %get-tuple-element.51), channel_id=1, source_target_pairs={{1,0},{2,1},{3,2},{5,4},{6,5},{7,6},{9,8},{10,9},{11,10},{13,12},{... | collective-permute-start | bytes 2088968 | tf_op jit(solution)/shard_map/ppermute | solution.py:51
  147.5 5.5 %collective-permute-start.8 = (f32[9,1,9,33]{3,2,1,0:T(8,128)S(1)}, f32[9,1,9,33]{3,2,1,0:T(8,128)S(1)}, u32[]{:S(2)}, u32[]{:S(2)}) collective-permute-start(f32[9,1,9,33]{3,2,1,0:T(8,128)S(1)} %fusion.60), channel_id=1, source_target_pairs={{0,1},{1,2},{2,3},{4,5},{5,6},{6,7},{8,9},{9,10},{10,11},{12,13},{... | collective-permute-start | bytes 32084 | tf_op jit(solution)/shard_map/ppermute | solution.py:62
  153.0 6.7 %collective-permute-start.9 = (f32[9,1,9,33]{3,2,1,0:T(8,128)S(1)}, f32[9,1,9,33]{3,2,1,0:T(8,128)S(1)}, u32[]{:S(2)}, u32[]{:S(2)}) collective-permute-start(f32[9,1,9,33]{3,2,1,0:T(8,128)S(1)} %get-tuple-element.42), channel_id=1, source_target_pairs={{1,0},{2,1},{3,2},{5,4},{6,5},{7,6},{9,8},{10,9},{11,10},{13,12},{... | collective-permute-start | bytes 32084 | tf_op jit(solution)/shard_map/ppermute | solution.py:63
  159.8 10.4 %collective-permute-start.10 = (f32[9,3,1,33]{3,2,1,0:T(1,128)S(1)}, f32[9,3,1,33]{3,2,1,0:T(1,128)S(1)}, u32[]{:S(2)}, u32[]{:S(2)}) collective-permute-start(f32[9,3,1,33]{3,2,1,0:T(1,128)S(1)} %get-tuple-element.118), channel_id=1, source_target_pairs={{0,16},{16,32},{32,48},{48,64},{64,80},{80,96},{96,112},{112,128},... | collective-permute-start | bytes 10700 | tf_op jit(solution)/shard_map/ppermute | solution.py:62
  161.7 9.9 %collective-permute-start.11 = (f32[9,3,1,33]{3,2,1,0:T(1,128)S(1)}, f32[9,3,1,33]{3,2,1,0:T(1,128)S(1)}, u32[]{:S(2)}, u32[]{:S(2)}) collective-permute-start(f32[9,3,1,33]{3,2,1,0:T(1,128)S(1)} %get-tuple-element.119), channel_id=1, source_target_pairs={{16,0},{32,16},{48,32},{64,48},{80,64},{96,80},{112,96},{128,112},... | collective-permute-start | bytes 10700 | tf_op jit(solution)/shard_map/ppermute | solution.py:63
  171.8 7.1 %collective-permute-start.12 = (f32[9,3,9,1]{3,2,1,0:T(8,128)S(1)}, f32[9,3,9,1]{3,2,1,0:T(8,128)S(1)}, u32[]{:S(2)}, u32[]{:S(2)}) collective-permute-start(f32[9,3,9,1]{3,2,1,0:T(8,128)S(1)} %get-tuple-element.114), channel_id=1, source_target_pairs={{0,4},{4,8},{8,12},{1,5},{5,9},{9,13},{2,6},{6,10},{10,14},{3,7},{... | collective-permute-start | bytes 2924 | tf_op jit(solution)/shard_map/ppermute | solution.py:62
  174.1 8.9 %collective-permute-start.13 = (f32[9,3,9,1]{3,2,1,0:T(8,128)S(1)}, f32[9,3,9,1]{3,2,1,0:T(8,128)S(1)}, u32[]{:S(2)}, u32[]{:S(2)}) collective-permute-start(f32[9,3,9,1]{3,2,1,0:T(8,128)S(1)} %get-tuple-element.115), channel_id=1, source_target_pairs={{4,0},{8,4},{12,8},{5,1},{9,5},{13,9},{6,2},{10,6},{14,10},{7,3},{... | collective-permute-start | bytes 2924 | tf_op jit(solution)/shard_map/ppermute | solution.py:63
  186.8 5.4 %collective-permute-start.14 = (f32[3,1,9,33]{3,2,1,0:T(8,128)S(1)}, f32[3,1,9,33]{3,2,1,0:T(8,128)S(1)}, u32[]{:S(2)}, u32[]{:S(2)}) collective-permute-start(f32[3,1,9,33]{3,2,1,0:T(8,128)S(1)} %get-tuple-element.164), channel_id=1, source_target_pairs={{0,1},{1,2},{2,3},{4,5},{5,6},{6,7},{8,9},{9,10},{10,11},{12,13},{... | collective-permute-start | bytes 10700 | tf_op jit(solution)/shard_map/ppermute | solution.py:62
  190.7 5.7 %collective-permute-start.15 = (f32[3,1,9,33]{3,2,1,0:T(8,128)S(1)}, f32[3,1,9,33]{3,2,1,0:T(8,128)S(1)}, u32[]{:S(2)}, u32[]{:S(2)}) collective-permute-start(f32[3,1,9,33]{3,2,1,0:T(8,128)S(1)} %get-tuple-element.165), channel_id=1, source_target_pairs={{1,0},{2,1},{3,2},{5,4},{6,5},{7,6},{9,8},{10,9},{11,10},{13,12},{... | collective-permute-start | bytes 10700 | tf_op jit(solution)/shard_map/ppermute | solution.py:63
  196.5 9.7 %collective-permute-start.16 = (f32[3,3,1,33]{3,2,1,0:T(1,128)S(1)}, f32[3,3,1,33]{3,2,1,0:T(1,128)S(1)}, u32[]{:S(2)}, u32[]{:S(2)}) collective-permute-start(f32[3,3,1,33]{3,2,1,0:T(1,128)S(1)} %pad_maximum_fusion.29), channel_id=1, source_target_pairs={{0,16},{16,32},{32,48},{48,64},{64,80},{80,96},{96,112},{112,128},... | collective-permute-start | bytes 3572 | tf_op jit(solution)/shard_map/ppermute | solution.py:62
  212.6 6.2 %collective-permute-start.19 = (f32[3,3,9,1]{3,2,1,0:T(8,128)S(1)}, f32[3,3,9,1]{3,2,1,0:T(8,128)S(1)}, u32[]{:S(2)}, u32[]{:S(2)}) collective-permute-start(f32[3,3,9,1]{3,2,1,0:T(8,128)S(1)} %get-tuple-element.160), channel_id=1, source_target_pairs={{4,0},{8,4},{12,8},{5,1},{9,5},{13,9},{6,2},{10,6},{14,10},{7,3},{... | collective-permute-start | bytes 980 | tf_op jit(solution)/shard_map/ppermute | solution.py:63
  226.3 5.7 %collective-permute-start.21 = (f32[3,1,9,33]{3,2,1,0:T(8,128)S(1)}, f32[3,1,9,33]{3,2,1,0:T(8,128)S(1)}, u32[]{:S(2)}, u32[]{:S(2)}) collective-permute-start(f32[3,1,9,33]{3,2,1,0:T(8,128)S(1)} %get-tuple-element.156), channel_id=1, source_target_pairs={{1,0},{2,1},{3,2},{5,4},{6,5},{7,6},{9,8},{10,9},{11,10},{13,12},{... | collective-permute-start | bytes 10700 | tf_op jit(solution)/shard_map/ppermute | solution.py:63
  232.1 9.7 %collective-permute-start.22 = (f32[3,3,1,33]{3,2,1,0:T(1,128)S(1)}, f32[3,3,1,33]{3,2,1,0:T(1,128)S(1)}, u32[]{:S(2)}, u32[]{:S(2)}) collective-permute-start(f32[3,3,1,33]{3,2,1,0:T(1,128)S(1)} %pad_maximum_fusion.27), channel_id=1, source_target_pairs={{0,16},{16,32},{32,48},{48,64},{64,80},{80,96},{96,112},{112,128},... | collective-permute-start | bytes 3572 | tf_op jit(solution)/shard_map/ppermute | solution.py:62
  241.9 6.1 %collective-permute-start.23 = (f32[3,3,1,33]{3,2,1,0:T(1,128)S(1)}, f32[3,3,1,33]{3,2,1,0:T(1,128)S(1)}, u32[]{:S(2)}, u32[]{:S(2)}) collective-permute-start(f32[3,3,1,33]{3,2,1,0:T(1,128)S(1)} %get-tuple-element.29), channel_id=1, source_target_pairs={{16,0},{32,16},{48,32},{64,48},{80,64},{96,80},{112,96},{128,112},... | collective-permute-start | bytes 3572 | tf_op jit(solution)/shard_map/ppermute | solution.py:63
  249.5 6.1 %collective-permute-start.24 = (f32[3,3,9,1]{3,2,1,0:T(8,128)}, f32[3,3,9,1]{3,2,1,0:T(8,128)}, u32[]{:S(2)}, u32[]{:S(2)}) collective-permute-start(f32[3,3,9,1]{3,2,1,0:T(8,128)} %get-tuple-element.150), channel_id=1, source_target_pairs={{0,4},{4,8},{8,12},{1,5},{5,9},{9,13},{2,6},{6,10},{10,14},{3,7},{... | collective-permute-start | bytes 980 | tf_op jit(solution)/shard_map/ppermute | solution.py:62
  253.8 6.6 %collective-permute-start.25 = (f32[3,3,9,1]{3,2,1,0:T(8,128)}, f32[3,3,9,1]{3,2,1,0:T(8,128)}, u32[]{:S(2)}, u32[]{:S(2)}) collective-permute-start(f32[3,3,9,1]{3,2,1,0:T(8,128)} %get-tuple-element.151), channel_id=1, source_target_pairs={{4,0},{8,4},{12,8},{5,1},{9,5},{13,9},{6,2},{10,6},{14,10},{7,3},{... | collective-permute-start | bytes 980 | tf_op jit(solution)/shard_map/ppermute | solution.py:63
  270.8 5.7 %collective-permute-start.27 = (f32[3,1,9,33]{3,2,1,0:T(8,128)S(1)}, f32[3,1,9,33]{3,2,1,0:T(8,128)S(1)}, u32[]{:S(2)}, u32[]{:S(2)}) collective-permute-start(f32[3,1,9,33]{3,2,1,0:T(8,128)S(1)} %get-tuple-element.147), channel_id=1, source_target_pairs={{1,0},{2,1},{3,2},{5,4},{6,5},{7,6},{9,8},{10,9},{11,10},{13,12},{... | collective-permute-start | bytes 10700 | tf_op jit(solution)/shard_map/ppermute | solution.py:63
  276.5 9.7 %collective-permute-start.28 = (f32[3,3,1,33]{3,2,1,0:T(1,128)S(1)}, f32[3,3,1,33]{3,2,1,0:T(1,128)S(1)}, u32[]{:S(2)}, u32[]{:S(2)}) collective-permute-start(f32[3,3,1,33]{3,2,1,0:T(1,128)S(1)} %pad_maximum_fusion.25), channel_id=1, source_target_pairs={{0,16},{16,32},{32,48},{48,64},{64,80},{80,96},{96,112},{112,128},... | collective-permute-start | bytes 3572 | tf_op jit(solution)/shard_map/ppermute | solution.py:62
  291.2 6.2 %collective-permute-start.31 = (f32[3,3,9,1]{3,2,1,0:T(8,128)S(1)}, f32[3,3,9,1]{3,2,1,0:T(8,128)S(1)}, u32[]{:S(2)}, u32[]{:S(2)}) collective-permute-start(f32[3,3,9,1]{3,2,1,0:T(8,128)S(1)} %get-tuple-element.142), channel_id=1, source_target_pairs={{4,0},{8,4},{12,8},{5,1},{9,5},{13,9},{6,2},{10,6},{14,10},{7,3},{... | collective-permute-start | bytes 980 | tf_op jit(solution)/shard_map/ppermute | solution.py:63
  302.7 5.7 %collective-permute-start.33 = (f32[3,1,9,33]{3,2,1,0:T(8,128)S(1)}, f32[3,1,9,33]{3,2,1,0:T(8,128)S(1)}, u32[]{:S(2)}, u32[]{:S(2)}) collective-permute-start(f32[3,1,9,33]{3,2,1,0:T(8,128)S(1)} %get-tuple-element.138), channel_id=1, source_target_pairs={{1,0},{2,1},{3,2},{5,4},{6,5},{7,6},{9,8},{10,9},{11,10},{13,12},{... | collective-permute-start | bytes 10700 | tf_op jit(solution)/shard_map/ppermute | solution.py:63
  308.4 9.7 %collective-permute-start.34 = (f32[3,3,1,33]{3,2,1,0:T(1,128)S(1)}, f32[3,3,1,33]{3,2,1,0:T(1,128)S(1)}, u32[]{:S(2)}, u32[]{:S(2)}) collective-permute-start(f32[3,3,1,33]{3,2,1,0:T(1,128)S(1)} %pad_maximum_fusion.23), channel_id=1, source_target_pairs={{0,16},{16,32},{32,48},{48,64},{64,80},{80,96},{96,112},{112,128},... | collective-permute-start | bytes 3572 | tf_op jit(solution)/shard_map/ppermute | solution.py:62
  323.5 6.2 %collective-permute-start.37 = (f32[3,3,9,1]{3,2,1,0:T(8,128)S(1)}, f32[3,3,9,1]{3,2,1,0:T(8,128)S(1)}, u32[]{:S(2)}, u32[]{:S(2)}) collective-permute-start(f32[3,3,9,1]{3,2,1,0:T(8,128)S(1)} %get-tuple-element.133), channel_id=1, source_target_pairs={{4,0},{8,4},{12,8},{5,1},{9,5},{13,9},{6,2},{10,6},{14,10},{7,3},{... | collective-permute-start | bytes 980 | tf_op jit(solution)/shard_map/ppermute | solution.py:63
  335.0 5.7 %collective-permute-start.39 = (f32[3,1,9,33]{3,2,1,0:T(8,128)S(1)}, f32[3,1,9,33]{3,2,1,0:T(8,128)S(1)}, u32[]{:S(2)}, u32[]{:S(2)}) collective-permute-start(f32[3,1,9,33]{3,2,1,0:T(8,128)S(1)} %get-tuple-element.129), channel_id=1, source_target_pairs={{1,0},{2,1},{3,2},{5,4},{6,5},{7,6},{9,8},{10,9},{11,10},{13,12},{... | collective-permute-start | bytes 10700 | tf_op jit(solution)/shard_map/ppermute | solution.py:63
  340.8 9.7 %collective-permute-start.40 = (f32[3,3,1,33]{3,2,1,0:T(1,128)S(1)}, f32[3,3,1,33]{3,2,1,0:T(1,128)S(1)}, u32[]{:S(2)}, u32[]{:S(2)}) collective-permute-start(f32[3,3,1,33]{3,2,1,0:T(1,128)S(1)} %pad_maximum_fusion.21), channel_id=1, source_target_pairs={{0,16},{16,32},{32,48},{48,64},{64,80},{80,96},{96,112},{112,128},... | collective-permute-start | bytes 3572 | tf_op jit(solution)/shard_map/ppermute | solution.py:62
  355.8 6.2 %collective-permute-start.43 = (f32[3,3,9,1]{3,2,1,0:T(8,128)S(1)}, f32[3,3,9,1]{3,2,1,0:T(8,128)S(1)}, u32[]{:S(2)}, u32[]{:S(2)}) collective-permute-start(f32[3,3,9,1]{3,2,1,0:T(8,128)S(1)} %get-tuple-element.124), channel_id=1, source_target_pairs={{4,0},{8,4},{12,8},{5,1},{9,5},{13,9},{6,2},{10,6},{14,10},{7,3},{... | collective-permute-start | bytes 980 | tf_op jit(solution)/shard_map/ppermute | solution.py:63
  (32 other events, 241.2 us)

commit v7 on v2

--- a/solution.py
+++ b/solution.py
@@ -152,7 +152,6 @@
 
 def bricks_of(image_slab, deformed_slab):
     both = jnp.concatenate([image_slab, deformed_slab], axis=0)
-    both = halo(both, "gy", 2, DMAX)
     n_gx = lax.axis_size("gx")
     fields, nx, ny = both.shape
     bx = nx // n_gx
@@ -163,6 +162,8 @@
     windows = jnp.concatenate([low, main, high], axis=2)
     windows = jnp.moveaxis(windows, 1, 0)
     brick = lax.all_to_all(windows, "gx", split_axis=0, concat_axis=0, tiled=True)
+    brick = halo(brick, "gy", 3, DMAX)
+    ny = brick.shape[3]
     forward, backward = neighbours("gz")
     bz = brick.shape[0]
     image = brick[:, 0]

time: 390 us -> 367 us (0.941)
  blocking collectives: 101 us -> 73.2 us
    all_to_all x1, blocking collectives: 101 us -> 73.2 us  [bricks_of(): lax.all_to_all(windows, 'gx', split_axis=0, concat_axis=0, tiled=True)]
  transfers between devices with their start and end apart: 40 -> 40, of which waited for: 38 -> 37; matrix products, arithmetic and copies ran while one was open for 1% -> 2% of each run, Pallas kernels for 0% -> 0%
where the time goes in v7:
time: 367 us; the launch traced here: 362 us
  waiting for transfers between devices  126 us (34%)
  starting transfers between devices  87.6 us (24%)
  blocking collectives  73.2 us (20%)
  other arithmetic  31.5 us (9%)
  local copies, waits for them, and re-layouts  21.7 us (6%)
  matrix products  11.5 us (3%)
  between operations  10.2 us (3%)
    all_to_all x1, blocking collectives, bricks_of(): lax.all_to_all(windows, 'gx', split_axis=0, concat_axis=0, tiled=True)  73.2 us
    ppermute x18, waiting for transfers between devices, share(): from_high = lax.ppermute(first, axis, backward)  59 us
    ppermute x18, waiting for transfers between devices, share(): from_low = lax.ppermute(last, axis, forward)  48.1 us
    ppermute x18, starting transfers between devices, share(): from_low = lax.ppermute(last, axis, forward)  42.5 us
    ppermute x18, starting transfers between devices, share(): from_high = lax.ppermute(first, axis, backward)  34 us
    ppermute x1, waiting for transfers between devices, bricks_of(): from_high = lax.ppermute(to_low, 'gz', backward)  12.4 us
  transfers between devices with their start and end apart: 40, of which 37 were waited for; matrix products, arithmetic and copies ran while one was open for 2% of the time, Pallas kernels for 0%

profile of v7, /device:TPU:4, one launch (start us, length us, event | category | flops | bytes accessed | tf_op | source)
XLA Modules:
  0.0 362.0 jit_solution(15256986685344556729)
XLA Ops:
  2.9 73.2 %all_to_all.5 = f32[16,2,80,256]{3,2,1,0:T(8,128)S(1)} all-to-all(f32[16,2,80,256]{3,2,1,0:T(8,128)S(1)} %copy.40), channel_id=1, replica_groups=mesh['gx'=16,'gy'=4,'gz'=4] {'gx'}, dimensions={0} | all-to-all | bytes 5242880 | tf_op jit(solution)/shard_map/all_to_all | solution.py:164
  79.7 3.6 %collective-permute-start = (f32[16,2,80,8]{2,3,1,0:T(8,128)S(1)}, f32[16,2,80,8]{2,3,1,0:T(8,128)S(1)}, u32[]{:S(2)}, u32[]{:S(2)}) collective-permute-start(f32[16,2,80,8]{2,3,1,0:T(8,128)S(1)} %copy.41), channel_id=1, source_target_pairs={{0,4},{4,8},{8,12},{1,5},{5,9},{9,13},{2,6},{6,10},{10,14},{3,7},{... | collective-permute-start | bytes 245768 | tf_op jit(solution)/shard_map/ppermute | solution.py:50
  87.8 4.1 %collective-permute-done.1 = f32[16,2,80,8]{2,3,1,0:T(8,128)S(1)} collective-permute-done((f32[16,2,80,8]{2,3,1,0:T(8,128)S(1)}, f32[16,2,80,8]{2,3,1,0:T(8,128)S(1)}, u32[]{:S(2)}, u32[]{:S(2)}) %collective-permute-start.1) | collective-permute-done | bytes 81952 | tf_op jit(solution)/shard_map/ppermute | solution.py:51
  93.4 3.1 pad_maximum_fusion
  102.4 4.8 %collective-permute-start.3 = (f32[9,80,272]{2,1,0:T(8,128)}, f32[9,80,272]{2,1,0:T(8,128)S(1)}, u32[]{:S(2)}, u32[]{:S(2)}) collective-permute-start(f32[9,80,272]{2,1,0:T(8,128)} %pad_maximum_fusion.8), channel_id=1, source_target_pairs={{0,1},{1,2},{2,3},{4,5},{5,6},{6,7},{8,9},{9,10},{10,11},{12,13},{... | collective-permute-start | bytes 2350088 | tf_op jit(solution)/shard_map/ppermute | solution.py:173
  114.5 12.4 %collective-permute-done.2 = f32[9,80,272]{2,1,0:T(8,128)S(1)} collective-permute-done((f32[9,80,272]{2,1,0:T(8,128)S(1)}, f32[9,80,272]{2,1,0:T(8,128)S(1)}, u32[]{:S(2)}, u32[]{:S(2)}) %collective-permute-start.2) | collective-permute-done | bytes 783392 | tf_op jit(solution)/shard_map/ppermute | solution.py:174
  126.9 2.6 collective-permute-done.3
  143.4 4.3 %collective-permute-start.4 = (f32[9,1,9,33]{3,2,1,0:T(8,128)S(1)}, f32[9,1,9,33]{3,2,1,0:T(8,128)S(1)}, u32[]{:S(2)}, u32[]{:S(2)}) collective-permute-start(f32[9,1,9,33]{3,2,1,0:T(8,128)S(1)} %fusion.61), channel_id=1, source_target_pairs={{0,1},{1,2},{2,3},{4,5},{5,6},{6,7},{8,9},{9,10},{10,11},{12,13},{... | collective-permute-start | bytes 32084 | tf_op jit(solution)/shard_map/ppermute | solution.py:62
  151.0 5.3 %collective-permute-done.5 = f32[9,1,9,33]{3,2,1,0:T(8,128)S(1)} collective-permute-done((f32[9,1,9,33]{3,2,1,0:T(8,128)S(1)}, f32[9,1,9,33]{3,2,1,0:T(8,128)S(1)}, u32[]{:S(2)}, u32[]{:S(2)}) %collective-permute-start.5) | collective-permute-done | bytes 10724 | tf_op jit(solution)/shard_map/ppermute | solution.py:63
  158.3 8.4 %collective-permute-start.7 = (f32[9,3,1,33]{3,2,1,0:T(1,128)S(1)}, f32[9,3,1,33]{3,2,1,0:T(1,128)S(1)}, u32[]{:S(2)}, u32[]{:S(2)}) collective-permute-start(f32[9,3,1,33]{3,2,1,0:T(1,128)S(1)} %get-tuple-element.119), channel_id=1, source_target_pairs={{16,0},{32,16},{48,32},{64,48},{80,64},{96,80},{112,96},{128,112},... | collective-permute-start | bytes 10700 | tf_op jit(solution)/shard_map/ppermute | solution.py:63
  168.3 2.8 collective-permute-start.8
  172.8 3.5 collective-permute-done.8
  176.3 4.1 %collective-permute-done.9 = f32[9,3,9,1]{3,2,1,0:T(8,128)S(1)} collective-permute-done((f32[9,3,9,1]{3,2,1,0:T(8,128)S(1)}, f32[9,3,9,1]{3,2,1,0:T(8,128)S(1)}, u32[]{:S(2)}, u32[]{:S(2)}) %collective-permute-start.9) | collective-permute-done | bytes 1004 | tf_op jit(solution)/shard_map/ppermute | solution.py:63
  184.2 3.9 %collective-permute-start.10 = (f32[3,1,9,33]{3,2,1,0:T(8,128)S(1)}, f32[3,1,9,33]{3,2,1,0:T(8,128)S(1)}, u32[]{:S(2)}, u32[]{:S(2)}) collective-permute-start(f32[3,1,9,33]{3,2,1,0:T(8,128)S(1)} %get-tuple-element.164), channel_id=1, source_target_pairs={{0,1},{1,2},{2,3},{4,5},{5,6},{6,7},{8,9},{9,10},{10,11},{12,13},{... | collective-permute-start | bytes 10700 | tf_op jit(solution)/shard_map/ppermute | solution.py:62
  189.6 4.2 %collective-permute-done.11 = f32[3,1,9,33]{3,2,1,0:T(8,128)S(1)} collective-permute-done((f32[3,1,9,33]{3,2,1,0:T(8,128)S(1)}, f32[3,1,9,33]{3,2,1,0:T(8,128)S(1)}, u32[]{:S(2)}, u32[]{:S(2)}) %collective-permute-start.11) | collective-permute-done | bytes 3596 | tf_op jit(solution)/shard_map/ppermute | solution.py:63
  195.8 7.8 %collective-permute-done.12 = f32[3,3,1,33]{3,2,1,0:T(1,128)S(1)} collective-permute-done((f32[3,3,1,33]{3,2,1,0:T(1,128)S(1)}, f32[3,3,1,33]{3,2,1,0:T(1,128)S(1)}, u32[]{:S(2)}, u32[]{:S(2)}) %collective-permute-start.12) | collective-permute-done | bytes 1220 | tf_op jit(solution)/shard_map/ppermute | solution.py:62
  207.0 2.5 collective-permute-start.14
  211.4 4.3 %collective-permute-done.15 = f32[3,3,9,1]{3,2,1,0:T(8,128)S(1)} collective-permute-done((f32[3,3,9,1]{3,2,1,0:T(8,128)S(1)}, f32[3,3,9,1]{3,2,1,0:T(8,128)S(1)}, u32[]{:S(2)}, u32[]{:S(2)}) %collective-permute-start.15) | collective-permute-done | bytes 356 | tf_op jit(solution)/shard_map/ppermute | solution.py:63
  219.7 3.5 collective-permute-start.16
  224.7 4.2 %collective-permute-done.17 = f32[3,1,9,33]{3,2,1,0:T(8,128)S(1)} collective-permute-done((f32[3,1,9,33]{3,2,1,0:T(8,128)S(1)}, f32[3,1,9,33]{3,2,1,0:T(8,128)S(1)}, u32[]{:S(2)}, u32[]{:S(2)}) %collective-permute-start.17) | collective-permute-done | bytes 3596 | tf_op jit(solution)/shard_map/ppermute | solution.py:63
  230.9 7.8 %collective-permute-done.18 = f32[3,3,1,33]{3,2,1,0:T(1,128)S(1)} collective-permute-done((f32[3,3,1,33]{3,2,1,0:T(1,128)S(1)}, f32[3,3,1,33]{3,2,1,0:T(1,128)S(1)}, u32[]{:S(2)}, u32[]{:S(2)}) %collective-permute-start.18) | collective-permute-done | bytes 1220 | tf_op jit(solution)/shard_map/ppermute | solution.py:62
  246.0 2.8 collective-permute-start.20
  250.7 4.7 %collective-permute-done.21 = f32[3,3,9,1]{3,2,1,0:T(8,128)} collective-permute-done((f32[3,3,9,1]{3,2,1,0:T(8,128)}, f32[3,3,9,1]{3,2,1,0:T(8,128)}, u32[]{:S(2)}, u32[]{:S(2)}) %collective-permute-start.21) | collective-permute-done | bytes 356 | tf_op jit(solution)/shard_map/ppermute | solution.py:63
  267.4 4.2 %collective-permute-done.23 = f32[3,1,9,33]{3,2,1,0:T(8,128)S(1)} collective-permute-done((f32[3,1,9,33]{3,2,1,0:T(8,128)S(1)}, f32[3,1,9,33]{3,2,1,0:T(8,128)S(1)}, u32[]{:S(2)}, u32[]{:S(2)}) %collective-permute-start.23) | collective-permute-done | bytes 3596 | tf_op jit(solution)/shard_map/ppermute | solution.py:63
  273.5 7.8 %collective-permute-done.24 = f32[3,3,1,33]{3,2,1,0:T(1,128)S(1)} collective-permute-done((f32[3,3,1,33]{3,2,1,0:T(1,128)S(1)}, f32[3,3,1,33]{3,2,1,0:T(1,128)S(1)}, u32[]{:S(2)}, u32[]{:S(2)}) %collective-permute-start.24) | collective-permute-done | bytes 1220 | tf_op jit(solution)/shard_map/ppermute | solution.py:62
  288.2 4.3 %collective-permute-done.27 = f32[3,3,9,1]{3,2,1,0:T(8,128)S(1)} collective-permute-done((f32[3,3,9,1]{3,2,1,0:T(8,128)S(1)}, f32[3,3,9,1]{3,2,1,0:T(8,128)S(1)}, u32[]{:S(2)}, u32[]{:S(2)}) %collective-permute-start.27) | collective-permute-done | bytes 356 | tf_op jit(solution)/shard_map/ppermute | solution.py:63
  299.3 4.2 %collective-permute-done.29 = f32[3,1,9,33]{3,2,1,0:T(8,128)S(1)} collective-permute-done((f32[3,1,9,33]{3,2,1,0:T(8,128)S(1)}, f32[3,1,9,33]{3,2,1,0:T(8,128)S(1)}, u32[]{:S(2)}, u32[]{:S(2)}) %collective-permute-start.29) | collective-permute-done | bytes 3596 | tf_op jit(solution)/shard_map/ppermute | solution.py:63
  305.5 7.8 %collective-permute-done.30 = f32[3,3,1,33]{3,2,1,0:T(1,128)S(1)} collective-permute-done((f32[3,3,1,33]{3,2,1,0:T(1,128)S(1)}, f32[3,3,1,33]{3,2,1,0:T(1,128)S(1)}, u32[]{:S(2)}, u32[]{:S(2)}) %collective-permute-start.30) | collective-permute-done | bytes 1220 | tf_op jit(solution)/shard_map/ppermute | solution.py:62
  320.5 4.3 %collective-permute-done.33 = f32[3,3,9,1]{3,2,1,0:T(8,128)S(1)} collective-permute-done((f32[3,3,9,1]{3,2,1,0:T(8,128)S(1)}, f32[3,3,9,1]{3,2,1,0:T(8,128)S(1)}, u32[]{:S(2)}, u32[]{:S(2)}) %collective-permute-start.33) | collective-permute-done | bytes 356 | tf_op jit(solution)/shard_map/ppermute | solution.py:63
  331.6 4.2 %collective-permute-done.35 = f32[3,1,9,33]{3,2,1,0:T(8,128)S(1)} collective-permute-done((f32[3,1,9,33]{3,2,1,0:T(8,128)S(1)}, f32[3,1,9,33]{3,2,1,0:T(8,128)S(1)}, u32[]{:S(2)}, u32[]{:S(2)}) %collective-permute-start.35) | collective-permute-done | bytes 3596 | tf_op jit(solution)/shard_map/ppermute | solution.py:63
  337.8 7.8 %collective-permute-done.36 = f32[3,3,1,33]{3,2,1,0:T(1,128)S(1)} collective-permute-done((f32[3,3,1,33]{3,2,1,0:T(1,128)S(1)}, f32[3,3,1,33]{3,2,1,0:T(1,128)S(1)}, u32[]{:S(2)}, u32[]{:S(2)}) %collective-permute-start.36) | collective-permute-done | bytes 1220 | tf_op jit(solution)/shard_map/ppermute | solution.py:62
  352.9 4.3 %collective-permute-done.39 = f32[3,3,9,1]{3,2,1,0:T(8,128)S(1)} collective-permute-done((f32[3,3,9,1]{3,2,1,0:T(8,128)S(1)}, f32[3,3,9,1]{3,2,1,0:T(8,128)S(1)}, u32[]{:S(2)}, u32[]{:S(2)}) %collective-permute-start.39) | collective-permute-done | bytes 356 | tf_op jit(solution)/shard_map/ppermute | solution.py:63
  (274 shorter events, 124.7 us)
Async XLA Ops:
  79.7 6.6 %collective-permute-start = (f32[16,2,80,8]{2,3,1,0:T(8,128)S(1)}, f32[16,2,80,8]{2,3,1,0:T(8,128)S(1)}, u32[]{:S(2)}, u32[]{:S(2)}) collective-permute-start(f32[16,2,80,8]{2,3,1,0:T(8,128)S(1)} %copy.41), channel_id=1, source_target_pairs={{0,4},{4,8},{8,12},{1,5},{5,9},{9,13},{2,6},{6,10},{10,14},{3,7},{... | collective-permute-start | bytes 245768 | tf_op jit(solution)/shard_map/ppermute | solution.py:50
  85.0 6.9 %collective-permute-start.1 = (f32[16,2,80,8]{2,3,1,0:T(8,128)S(1)}, f32[16,2,80,8]{2,3,1,0:T(8,128)S(1)}, u32[]{:S(2)}, u32[]{:S(2)}) collective-permute-start(f32[16,2,80,8]{2,3,1,0:T(8,128)S(1)} %copy.42), channel_id=1, source_target_pairs={{4,0},{8,4},{12,8},{5,1},{9,5},{13,9},{6,2},{10,6},{14,10},{7,3},{... | collective-permute-start | bytes 245768 | tf_op jit(solution)/shard_map/ppermute | solution.py:51
  100.0 26.9 %collective-permute-start.2 = (f32[9,80,272]{2,1,0:T(8,128)S(1)}, f32[9,80,272]{2,1,0:T(8,128)S(1)}, u32[]{:S(2)}, u32[]{:S(2)}) collective-permute-start(f32[9,80,272]{2,1,0:T(8,128)S(1)} %pad_maximum_fusion.7), channel_id=1, source_target_pairs={{1,0},{2,1},{3,2},{5,4},{6,5},{7,6},{9,8},{10,9},{11,10},{13,12},{... | collective-permute-start | bytes 2350088 | tf_op jit(solution)/shard_map/ppermute | solution.py:174
  102.4 27.1 %collective-permute-start.3 = (f32[9,80,272]{2,1,0:T(8,128)}, f32[9,80,272]{2,1,0:T(8,128)S(1)}, u32[]{:S(2)}, u32[]{:S(2)}) collective-permute-start(f32[9,80,272]{2,1,0:T(8,128)} %pad_maximum_fusion.8), channel_id=1, source_target_pairs={{0,1},{1,2},{2,3},{4,5},{5,6},{6,7},{8,9},{9,10},{10,11},{12,13},{... | collective-permute-start | bytes 2350088 | tf_op jit(solution)/shard_map/ppermute | solution.py:173
  143.4 6.2 %collective-permute-start.4 = (f32[9,1,9,33]{3,2,1,0:T(8,128)S(1)}, f32[9,1,9,33]{3,2,1,0:T(8,128)S(1)}, u32[]{:S(2)}, u32[]{:S(2)}) collective-permute-start(f32[9,1,9,33]{3,2,1,0:T(8,128)S(1)} %fusion.61), channel_id=1, source_target_pairs={{0,1},{1,2},{2,3},{4,5},{5,6},{6,7},{8,9},{9,10},{10,11},{12,13},{... | collective-permute-start | bytes 32084 | tf_op jit(solution)/shard_map/ppermute | solution.py:62
  149.7 6.6 %collective-permute-start.5 = (f32[9,1,9,33]{3,2,1,0:T(8,128)S(1)}, f32[9,1,9,33]{3,2,1,0:T(8,128)S(1)}, u32[]{:S(2)}, u32[]{:S(2)}) collective-permute-start(f32[9,1,9,33]{3,2,1,0:T(8,128)S(1)} %get-tuple-element.42), channel_id=1, source_target_pairs={{1,0},{2,1},{3,2},{5,4},{6,5},{7,6},{9,8},{10,9},{11,10},{13,12},{... | collective-permute-start | bytes 32084 | tf_op jit(solution)/shard_map/ppermute | solution.py:63
  156.3 10.4 %collective-permute-start.6 = (f32[9,3,1,33]{3,2,1,0:T(1,128)S(1)}, f32[9,3,1,33]{3,2,1,0:T(1,128)S(1)}, u32[]{:S(2)}, u32[]{:S(2)}) collective-permute-start(f32[9,3,1,33]{3,2,1,0:T(1,128)S(1)} %get-tuple-element.118), channel_id=1, source_target_pairs={{0,16},{16,32},{32,48},{48,64},{64,80},{80,96},{96,112},{112,128},... | collective-permute-start | bytes 10700 | tf_op jit(solution)/shard_map/ppermute | solution.py:62
  158.3 9.9 %collective-permute-start.7 = (f32[9,3,1,33]{3,2,1,0:T(1,128)S(1)}, f32[9,3,1,33]{3,2,1,0:T(1,128)S(1)}, u32[]{:S(2)}, u32[]{:S(2)}) collective-permute-start(f32[9,3,1,33]{3,2,1,0:T(1,128)S(1)} %get-tuple-element.119), channel_id=1, source_target_pairs={{16,0},{32,16},{48,32},{64,48},{80,64},{96,80},{112,96},{128,112},... | collective-permute-start | bytes 10700 | tf_op jit(solution)/shard_map/ppermute | solution.py:63
  168.3 8.0 %collective-permute-start.8 = (f32[9,3,9,1]{3,2,1,0:T(8,128)S(1)}, f32[9,3,9,1]{3,2,1,0:T(8,128)S(1)}, u32[]{:S(2)}, u32[]{:S(2)}) collective-permute-start(f32[9,3,9,1]{3,2,1,0:T(8,128)S(1)} %get-tuple-element.114), channel_id=1, source_target_pairs={{0,4},{4,8},{8,12},{1,5},{5,9},{9,13},{2,6},{6,10},{10,14},{3,7},{... | collective-permute-start | bytes 2924 | tf_op jit(solution)/shard_map/ppermute | solution.py:62
  171.2 9.3 %collective-permute-start.9 = (f32[9,3,9,1]{3,2,1,0:T(8,128)S(1)}, f32[9,3,9,1]{3,2,1,0:T(8,128)S(1)}, u32[]{:S(2)}, u32[]{:S(2)}) collective-permute-start(f32[9,3,9,1]{3,2,1,0:T(8,128)S(1)} %get-tuple-element.115), channel_id=1, source_target_pairs={{4,0},{8,4},{12,8},{5,1},{9,5},{13,9},{6,2},{10,6},{14,10},{7,3},{... | collective-permute-start | bytes 2924 | tf_op jit(solution)/shard_map/ppermute | solution.py:63
  184.2 5.4 %collective-permute-start.10 = (f32[3,1,9,33]{3,2,1,0:T(8,128)S(1)}, f32[3,1,9,33]{3,2,1,0:T(8,128)S(1)}, u32[]{:S(2)}, u32[]{:S(2)}) collective-permute-start(f32[3,1,9,33]{3,2,1,0:T(8,128)S(1)} %get-tuple-element.164), channel_id=1, source_target_pairs={{0,1},{1,2},{2,3},{4,5},{5,6},{6,7},{8,9},{9,10},{10,11},{12,13},{... | collective-permute-start | bytes 10700 | tf_op jit(solution)/shard_map/ppermute | solution.py:62
  188.1 5.7 %collective-permute-start.11 = (f32[3,1,9,33]{3,2,1,0:T(8,128)S(1)}, f32[3,1,9,33]{3,2,1,0:T(8,128)S(1)}, u32[]{:S(2)}, u32[]{:S(2)}) collective-permute-start(f32[3,1,9,33]{3,2,1,0:T(8,128)S(1)} %get-tuple-element.165), channel_id=1, source_target_pairs={{1,0},{2,1},{3,2},{5,4},{6,5},{7,6},{9,8},{10,9},{11,10},{13,12},{... | collective-permute-start | bytes 10700 | tf_op jit(solution)/shard_map/ppermute | solution.py:63
  193.9 9.7 %collective-permute-start.12 = (f32[3,3,1,33]{3,2,1,0:T(1,128)S(1)}, f32[3,3,1,33]{3,2,1,0:T(1,128)S(1)}, u32[]{:S(2)}, u32[]{:S(2)}) collective-permute-start(f32[3,3,1,33]{3,2,1,0:T(1,128)S(1)} %pad_maximum_fusion.28), channel_id=1, source_target_pairs={{0,16},{16,32},{32,48},{48,64},{64,80},{80,96},{96,112},{112,128},... | collective-permute-start | bytes 3572 | tf_op jit(solution)/shard_map/ppermute | solution.py:62
  207.0 4.4 %collective-permute-start.14 = (f32[3,3,9,1]{3,2,1,0:T(8,128)S(1)}, f32[3,3,9,1]{3,2,1,0:T(8,128)S(1)}, u32[]{:S(2)}, u32[]{:S(2)}) collective-permute-start(f32[3,3,9,1]{3,2,1,0:T(8,128)S(1)} %get-tuple-element.159), channel_id=1, source_target_pairs={{0,4},{4,8},{8,12},{1,5},{5,9},{9,13},{2,6},{6,10},{10,14},{3,7},{... | collective-permute-start | bytes 980 | tf_op jit(solution)/shard_map/ppermute | solution.py:62
  209.4 6.2 %collective-permute-start.15 = (f32[3,3,9,1]{3,2,1,0:T(8,128)S(1)}, f32[3,3,9,1]{3,2,1,0:T(8,128)S(1)}, u32[]{:S(2)}, u32[]{:S(2)}) collective-permute-start(f32[3,3,9,1]{3,2,1,0:T(8,128)S(1)} %get-tuple-element.160), channel_id=1, source_target_pairs={{4,0},{8,4},{12,8},{5,1},{9,5},{13,9},{6,2},{10,6},{14,10},{7,3},{... | collective-permute-start | bytes 980 | tf_op jit(solution)/shard_map/ppermute | solution.py:63
  219.7 5.0 %collective-permute-start.16 = (f32[3,1,9,33]{3,2,1,0:T(8,128)S(1)}, f32[3,1,9,33]{3,2,1,0:T(8,128)S(1)}, u32[]{:S(2)}, u32[]{:S(2)}) collective-permute-start(f32[3,1,9,33]{3,2,1,0:T(8,128)S(1)} %get-tuple-element.155), channel_id=1, source_target_pairs={{0,1},{1,2},{2,3},{4,5},{5,6},{6,7},{8,9},{9,10},{10,11},{12,13},{... | collective-permute-start | bytes 10700 | tf_op jit(solution)/shard_map/ppermute | solution.py:62
  223.2 5.7 %collective-permute-start.17 = (f32[3,1,9,33]{3,2,1,0:T(8,128)S(1)}, f32[3,1,9,33]{3,2,1,0:T(8,128)S(1)}, u32[]{:S(2)}, u32[]{:S(2)}) collective-permute-start(f32[3,1,9,33]{3,2,1,0:T(8,128)S(1)} %get-tuple-element.156), channel_id=1, source_target_pairs={{1,0},{2,1},{3,2},{5,4},{6,5},{7,6},{9,8},{10,9},{11,10},{13,12},{... | collective-permute-start | bytes 10700 | tf_op jit(solution)/shard_map/ppermute | solution.py:63
  229.0 9.7 %collective-permute-start.18 = (f32[3,3,1,33]{3,2,1,0:T(1,128)S(1)}, f32[3,3,1,33]{3,2,1,0:T(1,128)S(1)}, u32[]{:S(2)}, u32[]{:S(2)}) collective-permute-start(f32[3,3,1,33]{3,2,1,0:T(1,128)S(1)} %pad_maximum_fusion.26), channel_id=1, source_target_pairs={{0,16},{16,32},{32,48},{48,64},{64,80},{80,96},{96,112},{112,128},... | collective-permute-start | bytes 3572 | tf_op jit(solution)/shard_map/ppermute | solution.py:62
  238.7 5.7 %collective-permute-start.19 = (f32[3,3,1,33]{3,2,1,0:T(1,128)S(1)}, f32[3,3,1,33]{3,2,1,0:T(1,128)S(1)}, u32[]{:S(2)}, u32[]{:S(2)}) collective-permute-start(f32[3,3,1,33]{3,2,1,0:T(1,128)S(1)} %get-tuple-element.29), channel_id=1, source_target_pairs={{16,0},{32,16},{48,32},{64,48},{80,64},{96,80},{112,96},{128,112},... | collective-permute-start | bytes 3572 | tf_op jit(solution)/shard_map/ppermute | solution.py:63
  246.0 4.7 %collective-permute-start.20 = (f32[3,3,9,1]{3,2,1,0:T(8,128)}, f32[3,3,9,1]{3,2,1,0:T(8,128)}, u32[]{:S(2)}, u32[]{:S(2)}) collective-permute-start(f32[3,3,9,1]{3,2,1,0:T(8,128)} %get-tuple-element.150), channel_id=1, source_target_pairs={{0,4},{4,8},{8,12},{1,5},{5,9},{9,13},{2,6},{6,10},{10,14},{3,7},{... | collective-permute-start | bytes 980 | tf_op jit(solution)/shard_map/ppermute | solution.py:62
  248.8 6.6 %collective-permute-start.21 = (f32[3,3,9,1]{3,2,1,0:T(8,128)}, f32[3,3,9,1]{3,2,1,0:T(8,128)}, u32[]{:S(2)}, u32[]{:S(2)}) collective-permute-start(f32[3,3,9,1]{3,2,1,0:T(8,128)} %get-tuple-element.151), channel_id=1, source_target_pairs={{4,0},{8,4},{12,8},{5,1},{9,5},{13,9},{6,2},{10,6},{14,10},{7,3},{... | collective-permute-start | bytes 980 | tf_op jit(solution)/shard_map/ppermute | solution.py:63
  265.9 5.7 %collective-permute-start.23 = (f32[3,1,9,33]{3,2,1,0:T(8,128)S(1)}, f32[3,1,9,33]{3,2,1,0:T(8,128)S(1)}, u32[]{:S(2)}, u32[]{:S(2)}) collective-permute-start(f32[3,1,9,33]{3,2,1,0:T(8,128)S(1)} %get-tuple-element.147), channel_id=1, source_target_pairs={{1,0},{2,1},{3,2},{5,4},{6,5},{7,6},{9,8},{10,9},{11,10},{13,12},{... | collective-permute-start | bytes 10700 | tf_op jit(solution)/shard_map/ppermute | solution.py:63
  271.6 9.7 %collective-permute-start.24 = (f32[3,3,1,33]{3,2,1,0:T(1,128)S(1)}, f32[3,3,1,33]{3,2,1,0:T(1,128)S(1)}, u32[]{:S(2)}, u32[]{:S(2)}) collective-permute-start(f32[3,3,1,33]{3,2,1,0:T(1,128)S(1)} %pad_maximum_fusion.24), channel_id=1, source_target_pairs={{0,16},{16,32},{32,48},{48,64},{64,80},{80,96},{96,112},{112,128},... | collective-permute-start | bytes 3572 | tf_op jit(solution)/shard_map/ppermute | solution.py:62
  286.3 6.2 %collective-permute-start.27 = (f32[3,3,9,1]{3,2,1,0:T(8,128)S(1)}, f32[3,3,9,1]{3,2,1,0:T(8,128)S(1)}, u32[]{:S(2)}, u32[]{:S(2)}) collective-permute-start(f32[3,3,9,1]{3,2,1,0:T(8,128)S(1)} %get-tuple-element.142), channel_id=1, source_target_pairs={{4,0},{8,4},{12,8},{5,1},{9,5},{13,9},{6,2},{10,6},{14,10},{7,3},{... | collective-permute-start | bytes 980 | tf_op jit(solution)/shard_map/ppermute | solution.py:63
  297.8 5.7 %collective-permute-start.29 = (f32[3,1,9,33]{3,2,1,0:T(8,128)S(1)}, f32[3,1,9,33]{3,2,1,0:T(8,128)S(1)}, u32[]{:S(2)}, u32[]{:S(2)}) collective-permute-start(f32[3,1,9,33]{3,2,1,0:T(8,128)S(1)} %get-tuple-element.138), channel_id=1, source_target_pairs={{1,0},{2,1},{3,2},{5,4},{6,5},{7,6},{9,8},{10,9},{11,10},{13,12},{... | collective-permute-start | bytes 10700 | tf_op jit(solution)/shard_map/ppermute | solution.py:63
  303.5 9.7 %collective-permute-start.30 = (f32[3,3,1,33]{3,2,1,0:T(1,128)S(1)}, f32[3,3,1,33]{3,2,1,0:T(1,128)S(1)}, u32[]{:S(2)}, u32[]{:S(2)}) collective-permute-start(f32[3,3,1,33]{3,2,1,0:T(1,128)S(1)} %pad_maximum_fusion.22), channel_id=1, source_target_pairs={{0,16},{16,32},{32,48},{48,64},{64,80},{80,96},{96,112},{112,128},... | collective-permute-start | bytes 3572 | tf_op jit(solution)/shard_map/ppermute | solution.py:62
  316.6 3.9 %collective-permute-start.32 = (f32[3,3,9,1]{3,2,1,0:T(8,128)S(1)}, f32[3,3,9,1]{3,2,1,0:T(8,128)S(1)}, u32[]{:S(2)}, u32[]{:S(2)}) collective-permute-start(f32[3,3,9,1]{3,2,1,0:T(8,128)S(1)} %get-tuple-element.132), channel_id=1, source_target_pairs={{0,4},{4,8},{8,12},{1,5},{5,9},{9,13},{2,6},{6,10},{10,14},{3,7},{... | collective-permute-start | bytes 980 | tf_op jit(solution)/shard_map/ppermute | solution.py:62
  318.6 6.2 %collective-permute-start.33 = (f32[3,3,9,1]{3,2,1,0:T(8,128)S(1)}, f32[3,3,9,1]{3,2,1,0:T(8,128)S(1)}, u32[]{:S(2)}, u32[]{:S(2)}) collective-permute-start(f32[3,3,9,1]{3,2,1,0:T(8,128)S(1)} %get-tuple-element.133), channel_id=1, source_target_pairs={{4,0},{8,4},{12,8},{5,1},{9,5},{13,9},{6,2},{10,6},{14,10},{7,3},{... | collective-permute-start | bytes 980 | tf_op jit(solution)/shard_map/ppermute | solution.py:63
  330.1 5.7 %collective-permute-start.35 = (f32[3,1,9,33]{3,2,1,0:T(8,128)S(1)}, f32[3,1,9,33]{3,2,1,0:T(8,128)S(1)}, u32[]{:S(2)}, u32[]{:S(2)}) collective-permute-start(f32[3,1,9,33]{3,2,1,0:T(8,128)S(1)} %get-tuple-element.129), channel_id=1, source_target_pairs={{1,0},{2,1},{3,2},{5,4},{6,5},{7,6},{9,8},{10,9},{11,10},{13,12},{... | collective-permute-start | bytes 10700 | tf_op jit(solution)/shard_map/ppermute | solution.py:63
  335.9 9.7 %collective-permute-start.36 = (f32[3,3,1,33]{3,2,1,0:T(1,128)S(1)}, f32[3,3,1,33]{3,2,1,0:T(1,128)S(1)}, u32[]{:S(2)}, u32[]{:S(2)}) collective-permute-start(f32[3,3,1,33]{3,2,1,0:T(1,128)S(1)} %pad_maximum_fusion.20), channel_id=1, source_target_pairs={{0,16},{16,32},{32,48},{48,64},{64,80},{80,96},{96,112},{112,128},... | collective-permute-start | bytes 3572 | tf_op jit(solution)/shard_map/ppermute | solution.py:62
  349.0 3.9 %collective-permute-start.38 = (f32[3,3,9,1]{3,2,1,0:T(8,128)S(1)}, f32[3,3,9,1]{3,2,1,0:T(8,128)S(1)}, u32[]{:S(2)}, u32[]{:S(2)}) collective-permute-start(f32[3,3,9,1]{3,2,1,0:T(8,128)S(1)} %get-tuple-element.123), channel_id=1, source_target_pairs={{0,4},{4,8},{8,12},{1,5},{5,9},{9,13},{2,6},{6,10},{10,14},{3,7},{... | collective-permute-start | bytes 980 | tf_op jit(solution)/shard_map/ppermute | solution.py:62
  350.9 6.2 %collective-permute-start.39 = (f32[3,3,9,1]{3,2,1,0:T(8,128)S(1)}, f32[3,3,9,1]{3,2,1,0:T(8,128)S(1)}, u32[]{:S(2)}, u32[]{:S(2)}) collective-permute-start(f32[3,3,9,1]{3,2,1,0:T(8,128)S(1)} %get-tuple-element.124), channel_id=1, source_target_pairs={{4,0},{8,4},{12,8},{5,1},{9,5},{13,9},{6,2},{10,6},{14,10},{7,3},{... | collective-permute-start | bytes 980 | tf_op jit(solution)/shard_map/ppermute | solution.py:63
  (35 other events, 217.9 us)
